TPU v7x, 512 devices: a whole 4x4x16 slice. The times are simulated.
512 devices in a mesh: rep: 32 (over z_lo, x), seq: 16 (over z_hi, y, core).
Axes of the slice: x: 4, y: 4, z: 16 (z_hi: 2, z_lo: 8; z = z_hi * 8 + z_lo), core: 2. Of those that a mesh axis runs over, the one named last changes fastest.
Arguments:
- tokens: bfloat16 [32, 4096, 6144], P('rep', 'seq'), may hold values from -6 to 6
- queries: bfloat16 [32, 4096, 128], P('rep', 'seq'), may hold values from -4 to 4
- ctx_grad: bfloat16 [32, 4096, 128], P('rep', 'seq'), may hold values from -0.25 to 0.25
- kv_weight: bfloat16 [32, 6144, 256], P('rep', 'seq'), may hold values from -0.078125 to 0.078125
- rand_blocks: int32 [64, 3], replicated, may hold values from 0 to 63
- step_count: int32 [1], replicated, may hold values from 0 to 63
Outputs:
- mixed_update: float32 [32, 6144, 256], P('rep', 'seq')
- query_grad: bfloat16 [32, 4096, 128], P('rep', 'seq')
Inputs may be any that keep to these rules, and one draw needn't show every extreme that they name: `rand_blocks`: block indices of the same replica sequence.
All inputs are finite; a program needn't handle non-finite values.
Results may differ from a plain program's by a relative error of at most 0.02.
Values may be sent and summed in bfloat16 or wider, within the bound.
No kernel may reach another device: no remote copies, remote signals or barrier semaphores. Data moves between devices by JAX's collectives and lax.ppermute only.
A program may use at most 64 MiB of HBM per device.

v0:
```python
from functools import partial

import jax
import jax.numpy as jnp
from jax import lax
from jax.sharding import PartitionSpec as P

BLOCK = 64


def for_sending(value):

    def short(part):
        return part.astype(jnp.bfloat16) if part.dtype == jnp.float32 else part

    return jax.tree.map(short, value)


def shifted(value, axis, steps):
    count = lax.axis_size(axis)
    pairs = [(source, (source + steps) % count) for source in range(count)]
    return lax.ppermute(value, axis, pairs)


def fold_rows(tok_rows, row_piece):
    return jnp.dot(tok_rows, row_piece, preferred_element_type=jnp.float32)


def contract_rows(matrix_a, matrix_b):
    return lax.dot_general(
        matrix_a, matrix_b, (((0,), (0,)), ((), ())), preferred_element_type=jnp.float32
    )


def contract_cols(matrix_a, matrix_b):
    return lax.dot_general(
        matrix_a, matrix_b, (((1,), (1,)), ((), ())), preferred_element_type=jnp.float32
    )


def attend_mask(query_blocks, key_blocks, chosen_rows, blk_size):
    is_near = jnp.abs(query_blocks[:, None] - key_blocks[None, :]) <= 1
    picked = jnp.any(chosen_rows[:, :, None] == key_blocks[None, None, :], axis=1)
    allowed = is_near | (key_blocks[None, :] == 0) | picked
    return jnp.repeat(jnp.repeat(allowed, blk_size, axis=0), blk_size, axis=1)


def gossip(update, distance, rep_count):
    if distance == 0:
        return update
    from_low = jax.tree.map(
        lambda part, own: part.astype(own.dtype),
        shifted(for_sending(update), "rep", distance),
        update,
    )
    from_high = jax.tree.map(
        lambda part, own: part.astype(own.dtype),
        shifted(for_sending(update), "rep", rep_count - distance),
        update,
    )
    return (update + from_low + from_high) / 3.0


def per_device(tokens, queries, ctx_grad, kv_weight, rand_blocks, step_count):
    tokens_here = tokens[0]
    query_here = queries[0]
    grad_here = ctx_grad[0]
    weight_here = kv_weight[0]
    seq_count = lax.axis_size("seq")
    rep_count = lax.axis_size("rep")
    seq_index = lax.axis_index("seq")
    tok_count = tokens_here.shape[0]
    kv_width = weight_here.shape[1]
    head_size = kv_width // 2
    blk_size = BLOCK
    blocks_dev = tok_count // blk_size
    block_count = blocks_dev * seq_count
    inv_root = head_size ** (-0.5)
    kv_here = fold_rows(tokens_here, lax.all_gather(weight_here, "seq", axis=0, tiled=True)).astype(
        jnp.bfloat16
    )
    kv_all = lax.all_gather(kv_here, "seq", axis=0, tiled=True)
    keys_all = kv_all[:, :head_size]
    values_all = kv_all[:, head_size:]
    blocks_here = seq_index * blocks_dev + jnp.arange(blocks_dev, dtype=jnp.int32)
    every_block = jnp.arange(block_count, dtype=jnp.int32)
    chosen_here = lax.dynamic_slice_in_dim(rand_blocks, seq_index * blocks_dev, blocks_dev, 0)
    allowed = attend_mask(blocks_here, every_block, chosen_here, blk_size)
    scores = contract_cols(query_here, keys_all) * inv_root
    unnorm = jnp.where(allowed, jnp.exp(scores), jnp.float32(0.0))
    row_total = jnp.sum(unnorm, axis=1, keepdims=True)
    prob_rows = unnorm / row_total
    prob_low = prob_rows.astype(jnp.bfloat16)
    context = jnp.dot(prob_low, values_all, preferred_element_type=jnp.float32)
    row_delta = jnp.sum(grad_here.astype(jnp.float32) * context, axis=1, keepdims=True)
    prob_grad = contract_cols(grad_here, values_all)
    score_grad = (prob_rows * (prob_grad - row_delta) * inv_root).astype(jnp.bfloat16)
    query_grad = jnp.dot(score_grad, keys_all, preferred_element_type=jnp.float32).astype(
        jnp.bfloat16
    )
    key_terms = contract_rows(score_grad, query_here)
    value_terms = contract_rows(prob_low, grad_here)
    grad_terms = jnp.concatenate([key_terms, value_terms], axis=1).reshape(
        seq_count, tok_count, kv_width
    )
    received = lax.all_to_all(
        grad_terms.astype(jnp.bfloat16), "seq", split_axis=0, concat_axis=0, tiled=True
    ).astype(grad_terms.dtype)
    kv_grad = jnp.sum(received, axis=0).astype(jnp.bfloat16)
    grad_slice = lax.psum_scatter(
        contract_rows(tokens_here, kv_grad).astype(jnp.bfloat16),
        "seq",
        scatter_dimension=0,
        tiled=True,
    ).astype(jnp.float32)
    branches = [
        partial(gossip, distance=(1 << level_idx) % rep_count, rep_count=rep_count)
        for level_idx in range(4)
    ]
    mixed_update = lax.switch(step_count[0] % 4, branches, grad_slice)
    return (mixed_update[None], query_grad[None])


def solution(mesh):
    return jax.shard_map(
        per_device,
        mesh=mesh,
        in_specs=(
            P("rep", "seq", None),
            P("rep", "seq", None),
            P("rep", "seq", None),
            P("rep", "seq", None),
            P(),
            P(),
        ),
        out_specs=(P("rep", "seq", None), P("rep", "seq", None)),
        check_vma=False,
    )
```

profile of v0, /device:TPU:1, one launch (start us, length us, event | category | flops | bytes accessed | tf_op | source)
XLA Modules:
  0.0 497.8 jit_solution(13018875669005355405)
XLA Ops:
  7.2 0.0 copy-start
  7.2 0.0 all-gather.6.cloned.1.call-start
  7.2 0.7 all-gather.6.cloned.1.call-update
  7.9 0.0 copy-start.6
  7.9 0.0 copy-start.5
  7.9 0.0 copy-start.4
  7.9 0.0 all-gather.4.cloned.1.call-start
  8.0 115.5 %all-gather.6.cloned.1.call-done = bf16[1,6144,256]{2,1,0:T(8,128)(2,1)} async-done(((bf16[1,384,256]{2,1,0:T(8,128)(2,1)}), bf16[1,6144,256]{2,1,0:T(8,128)(2,1)}) %all-gather.6.cloned.1.call-update) | async-done | bytes 3145744 | tf_op jit(solution)/shard_map/all_gather | solution.py:79
  123.5 0.0 copy-done
  123.5 3.5 fusion.13
  127.1 0.0 all-gather.4.cloned.1.call-update
  127.1 0.0 reduce-scatter.4.cloned.1.call-start
  127.2 0.0 copy-done.6
  127.2 0.1 constant_dynamic-slice_fusion
  127.3 0.1 fusion.28
  127.3 0.1 fusion.30
  127.4 0.1 copy.22
  127.5 0.1 broadcast_in_dim.33
  127.7 0.1 reshape.24
  127.8 0.0 copy-done.5
  127.8 0.1 copy.23
  127.9 82.8 %all-gather.4.cloned.1.call-done = bf16[4096,256]{1,0:T(8,128)(2,1)} async-done(((bf16[256,256]{1,0:T(8,128)(2,1)}), bf16[4096,256]{1,0:T(8,128)(2,1)}) %all-gather.4.cloned.1.call-update) | async-done | bytes 2097168 | tf_op jit(solution)/shard_map/all_gather | solution.py:82
  210.8 0.3 broadcast_in_dim.34
  211.0 0.0 copy-done.4
  211.1 2.4 fusion.31
  213.5 0.3 fusion.12
  213.8 0.0 copy-start.2
  213.8 0.8 convolution_convert_fusion.1
  214.6 0.8 copy-done.2
  215.4 0.6 fusion.18
  216.0 0.8 fusion.7
  216.7 0.0 copy-start.1
  216.8 0.8 convolution_convert_fusion.2
  217.6 0.2 pad_maximum_fusion
  217.8 0.3 copy-done.1
  218.1 0.2 copy.35
  218.3 52.1 %all_to_all.5 = bf16[16,256,256]{1,2,0:T(8,128)(2,1)} all-to-all(bf16[16,256,256]{1,2,0:T(8,128)(2,1)S(1)} %bitcast.69), channel_id=1, replica_groups=mesh['rep'=32,'seq'=16] {'seq'}, dimensions={0} | all-to-all | bytes 4194304 | tf_op jit(solution)/shard_map/all_to_all | solution.py:106
  270.4 1.9 reduce_sum.32
  272.3 2.7 fusion
  275.0 4.6 copy.30
  279.6 0.0 reduce-scatter.4.cloned.1.call-update
  280.3 3.2 fusion.19
  283.6 180.4 %reduce-scatter.4.cloned.1.call-done = bf16[384,256]{1,0:T(8,128)(2,1)} async-done(((bf16[6144,256]{1,0:T(8,128)(2,1)}), bf16[384,256]{1,0:T(8,128)(2,1)}) %reduce-scatter.4.cloned.1.call-update) | async-done | bytes 196624
  463.9 1.7 copy.31
  465.7 1.0 convert_element_type.89
  466.6 23.9 %conditional.1 = (f32[1,384,256]{2,1,0:T(8,128)S(1)}) conditional(s32[]{:T(128)} %clamp.3, f32[384,256]{0,1:T(8,128)S(1)} %convert_element_type.89, f32[384,256]{0,1:T(8,128)S(1)} %convert_element_type.89, f32[384,256]{0,1:T(8,128)S(1)} %convert_element_type.89, f32[384,256]{0,1:T(8,128)S(1)} %convert_element_type.89), branch_computations={%region_5.6_spmd, %region_6.7_spmd, %region_7.8_spmd, %region_8.9_... | conditional | flops 589824 | bytes 4128856 | solution.py:120
  466.6 0.9 copy.27
  467.6 1.0 convert_element_type.64
  468.6 5.4 %collective-permute-start.3 = (bf16[384,256]{1,0:T(8,128)(2,1)S(1)}, bf16[384,256]{1,0:T(8,128)(2,1)S(1)}, u32[]{:S(2)}, u32[]{:S(2)}) collective-permute-start(bf16[384,256]{1,0:T(8,128)(2,1)S(1)} %convert_element_type.64), channel_id=1, source_target_pairs={{0,480},{16,496},{32,0},{48,16},{64,32},{80,48},{96,64},{112,80},{... | collective-permute-start | bytes 589832 | tf_op jit(solution)/shard_map/cond/branch_1_fun/ppermute | solution.py:22
  474.0 1.9 collective-permute-start.2
  475.9 0.7 collective-permute-done.3
  476.6 12.8 %collective-permute-done.2 = bf16[384,256]{1,0:T(8,128)(2,1)S(1)} collective-permute-done((bf16[384,256]{1,0:T(8,128)(2,1)S(1)}, bf16[384,256]{1,0:T(8,128)(2,1)S(1)}, u32[]{:S(2)}, u32[]{:S(2)}) %collective-permute-start.2) | collective-permute-done | bytes 196640 | tf_op jit(solution)/shard_map/cond/branch_1_fun/ppermute | solution.py:22
  489.4 1.1 multiply_bitcast_fusion.1
  490.5 0.0 copy-start.3
  490.5 0.7 copy-done.3
  (2 shorter events, 0.0 us)
Async XLA Ops:
  7.2 116.4 %copy-start = (bf16[1,256,6144]{2,1,0:T(8,128)(2,1)S(1)}, bf16[1,256,6144]{2,1,0:T(8,128)(2,1)}, u32[]{:S(2)}) copy-start(bf16[1,256,6144]{2,1,0:T(8,128)(2,1)} %param.10) | copy-start | bytes 9437188
  7.2 116.4 %all-gather.6.cloned.1.call-start = ((), (), s32[]{:S(2)}) async-start(), calls=%async_computation.3 | async-start | bytes 3342336 | tf_op jit(solution)/shard_map/all_gather | solution.py:79
  7.9 119.3 %copy-start.6 = (s32[64,3]{0,1:T(4,128)S(1)}, s32[64,3]{0,1:T(4,128)}, u32[]{:S(2)}) copy-start(s32[64,3]{0,1:T(4,128)} %param.14) | copy-start | bytes 2308
  7.9 119.9 %copy-start.5 = (bf16[1,256,128]{2,1,0:T(8,128)(2,1)S(1)}, bf16[1,256,128]{2,1,0:T(8,128)(2,1)}, u32[]{:S(2)}) copy-start(bf16[1,256,128]{2,1,0:T(8,128)(2,1)} %param.12) | copy-start | bytes 196612
  7.9 203.1 %copy-start.4 = (bf16[1,256,128]{2,1,0:T(8,128)(2,1)S(1)}, bf16[1,256,128]{2,1,0:T(8,128)(2,1)}, u32[]{:S(2)}) copy-start(bf16[1,256,128]{2,1,0:T(8,128)(2,1)} %param.11) | copy-start | bytes 196612
  7.9 202.8 %all-gather.4.cloned.1.call-start = ((), (), s32[]{:S(2)}) async-start(), calls=%async_computation.2 | async-start | bytes 2228224 | tf_op jit(solution)/shard_map/all_gather | solution.py:82
  127.1 336.8 %reduce-scatter.4.cloned.1.call-start = ((), (), s32[]{:S(2)}) async-start(), calls=%async_computation.4 | async-start | bytes 3342336
  213.8 1.6 copy-start.2
  216.7 1.4 copy-start.1
  468.6 8.0 %collective-permute-start.3 = (bf16[384,256]{1,0:T(8,128)(2,1)S(1)}, bf16[384,256]{1,0:T(8,128)(2,1)S(1)}, u32[]{:S(2)}, u32[]{:S(2)}) collective-permute-start(bf16[384,256]{1,0:T(8,128)(2,1)S(1)} %convert_element_type.64), channel_id=1, source_target_pairs={{0,480},{16,496},{32,0},{48,16},{64,32},{80,48},{96,64},{112,80},{... | collective-permute-start | bytes 589832 | tf_op jit(solution)/shard_map/cond/branch_1_fun/ppermute | solution.py:22
  474.0 15.4 %collective-permute-start.2 = (bf16[384,256]{1,0:T(8,128)(2,1)S(1)}, bf16[384,256]{1,0:T(8,128)(2,1)S(1)}, u32[]{:S(2)}, u32[]{:S(2)}) collective-permute-start(bf16[384,256]{1,0:T(8,128)(2,1)S(1)} %convert_element_type.64), channel_id=1, source_target_pairs={{0,32},{16,48},{32,64},{48,80},{64,96},{80,112},{96,128},{112,144}... | collective-permute-start | bytes 589832 | tf_op jit(solution)/shard_map/cond/branch_1_fun/ppermute | solution.py:22
  490.5 0.7 copy-start.3
Sparse Core Ops, SparseCore 0:
  11.3 112.1 all-gather.5
  127.4 83.3 all-gather.3
  279.8 184.1 reduce-scatter.3
where the time goes:
time: 499 us; the launch traced here: 498 us
  waiting for transfers between devices  393 us (79%)
  blocking collectives  52.1 us (10%)
  matrix products  14.8 us (3%)
  between operations  14.6 us (3%)
  local copies, waits for them, and re-layouts  10.2 us (2%)
  starting transfers between devices  7.44 us (1%)
  other arithmetic  5.65 us (1%)
    unnamed x4, waiting for transfers between devices  181 us
    all_gather x1, waiting for transfers between devices, per_device(): lax.all_gather(weight_here, 'seq', axis=0, tiled=True)  116 us
    all_gather x1, waiting for transfers between devices, per_device(): kv_all = lax.all_gather(kv_here, 'seq', axis=0, tiled=True)  82.8 us
    all_to_all x1, blocking collectives, per_device(): lax.all_to_all(grad_terms.astype(jnp.bfloat16), 'seq', split_axis=0, conc...  52.1 us
    ppermute x2, waiting for transfers between devices, shifted(): return lax.ppermute(value, axis, pairs)  13.5 us
  transfers between devices with their start and end apart: 5, of which 5 were waited for; matrix products, arithmetic and copies ran while one was open for 1% of the time, Pallas kernels for 0%

commit v1 on v0

--- a/solution.py
+++ b/solution.py
@@ -3,9 +3,11 @@
 import jax
 import jax.numpy as jnp
 from jax import lax
+from jax.sharding import Mesh
 from jax.sharding import PartitionSpec as P
 
 BLOCK = 64
+SEQ_AXES = ("zh", "y", "c")
 
 
 def for_sending(value):
@@ -20,6 +22,36 @@
     count = lax.axis_size(axis)
     pairs = [(source, (source + steps) % count) for source in range(count)]
     return lax.ppermute(value, axis, pairs)
+
+
+def seq_position():
+    return (lax.axis_index("zh") * lax.axis_size("y") + lax.axis_index("y")) * lax.axis_size(
+        "c"
+    ) + lax.axis_index("c")
+
+
+def gather_seq(piece):
+    step = lax.all_gather(piece, "zh", axis=0)
+    step = lax.all_gather(step, "y", axis=0)
+    step = lax.all_gather(step, "c", axis=0)
+    step = jnp.transpose(step, (2, 1, 0) + tuple(range(3, step.ndim)))
+    return step.reshape((-1,) + piece.shape[1:])
+
+
+def scatter_seq(whole, first_type, later_type):
+    zh_n, y_n, c_n = (lax.axis_size(name) for name in SEQ_AXES)
+    rows = whole.shape[0] // (zh_n * y_n * c_n)
+    parts = whole.reshape((zh_n, y_n, c_n, rows) + whole.shape[1:])
+    parts = jnp.moveaxis(parts, 2, 0).astype(first_type)
+    parts = lax.psum_scatter(parts, "c", scatter_dimension=0)
+    parts = jnp.moveaxis(parts, 1, 0).astype(later_type)
+    parts = lax.psum_scatter(parts, "y", scatter_dimension=0)
+    mine = lax.axis_index("zh")
+    other = 1 - mine
+    keep = lax.dynamic_index_in_dim(parts, mine, 0, keepdims=False).astype(jnp.float32)
+    send = lax.dynamic_index_in_dim(parts, other, 0, keepdims=False)
+    got = lax.ppermute(send, "zh", [(0, 1), (1, 0)])
+    return keep + got.astype(jnp.float32)
 
 
 def fold_rows(tok_rows, row_piece):
@@ -66,9 +98,9 @@
     query_here = queries[0]
     grad_here = ctx_grad[0]
     weight_here = kv_weight[0]
-    seq_count = lax.axis_size("seq")
+    seq_count = lax.axis_size(SEQ_AXES)
     rep_count = lax.axis_size("rep")
-    seq_index = lax.axis_index("seq")
+    seq_index = seq_position()
     tok_count = tokens_here.shape[0]
     kv_width = weight_here.shape[1]
     head_size = kv_width // 2
@@ -76,10 +108,8 @@
     blocks_dev = tok_count // blk_size
     block_count = blocks_dev * seq_count
     inv_root = head_size ** (-0.5)
-    kv_here = fold_rows(tokens_here, lax.all_gather(weight_here, "seq", axis=0, tiled=True)).astype(
-        jnp.bfloat16
-    )
-    kv_all = lax.all_gather(kv_here, "seq", axis=0, tiled=True)
+    kv_here = fold_rows(tokens_here, gather_seq(weight_here)).astype(jnp.bfloat16)
+    kv_all = gather_seq(kv_here)
     keys_all = kv_all[:, :head_size]
     values_all = kv_all[:, head_size:]
     blocks_here = seq_index * blocks_dev + jnp.arange(blocks_dev, dtype=jnp.int32)
@@ -100,19 +130,11 @@
     )
     key_terms = contract_rows(score_grad, query_here)
     value_terms = contract_rows(prob_low, grad_here)
-    grad_terms = jnp.concatenate([key_terms, value_terms], axis=1).reshape(
-        seq_count, tok_count, kv_width
+    grad_terms = jnp.concatenate([key_terms, value_terms], axis=1)
+    kv_grad = scatter_seq(grad_terms, jnp.float32, jnp.bfloat16).astype(jnp.bfloat16)
+    grad_slice = scatter_seq(
+        contract_rows(tokens_here, kv_grad).astype(jnp.bfloat16), jnp.float32, jnp.bfloat16
     )
-    received = lax.all_to_all(
-        grad_terms.astype(jnp.bfloat16), "seq", split_axis=0, concat_axis=0, tiled=True
-    ).astype(grad_terms.dtype)
-    kv_grad = jnp.sum(received, axis=0).astype(jnp.bfloat16)
-    grad_slice = lax.psum_scatter(
-        contract_rows(tokens_here, kv_grad).astype(jnp.bfloat16),
-        "seq",
-        scatter_dimension=0,
-        tiled=True,
-    ).astype(jnp.float32)
     branches = [
         partial(gossip, distance=(1 << level_idx) % rep_count, rep_count=rep_count)
         for level_idx in range(4)
@@ -122,17 +144,19 @@
 
 
 def solution(mesh):
+    rep_n, seq_n = mesh.devices.shape
+    sub_mesh = Mesh(mesh.devices.reshape(rep_n, 2, seq_n // 4, 2), ("rep",) + SEQ_AXES)
     return jax.shard_map(
         per_device,
-        mesh=mesh,
+        mesh=sub_mesh,
         in_specs=(
-            P("rep", "seq", None),
-            P("rep", "seq", None),
-            P("rep", "seq", None),
-            P("rep", "seq", None),
+            P("rep", SEQ_AXES, None),
+            P("rep", SEQ_AXES, None),
+            P("rep", SEQ_AXES, None),
+            P("rep", SEQ_AXES, None),
             P(),
             P(),
         ),
-        out_specs=(P("rep", "seq", None), P("rep", "seq", None)),
+        out_specs=(P("rep", SEQ_AXES, None), P("rep", SEQ_AXES, None)),
         check_vma=False,
     )

time: 499 us -> 472 us (0.946)
  waiting for transfers between devices: 393 us -> 297 us
  starting transfers between devices: 7.44 us -> 50.2 us
  local copies, waits for them, and re-layouts: 10.2 us -> 43.7 us
  blocking collectives: 52.1 us -> 43.2 us
    unnamed x4 -> x9, waiting for transfers between devices: 181 us -> 59.1 us
    reduce_scatter x0 -> x3, waiting for transfers between devices: none -> 91.9 us  [the longest x2 58.6 us: scatter_seq(): parts = lax.psum_scatter(parts, 'c', scatter_dimension=0)]
    all_gather x2 -> x4, waiting for transfers between devices: 198 us -> 129 us  [the longest x2 77 us: gather_seq(): step = lax.all_gather(step, 'y', axis=0)]
    all_to_all x1 -> x0, blocking collectives: 52.1 us -> none  [per_device(): lax.all_to_all(grad_terms.astype(jnp.bfloat16), 'seq', split_axis=0, conc...]
    all_gather x0 -> x2, blocking collectives: none -> 43.2 us  [gather_seq(): step = lax.all_gather(piece, 'zh', axis=0)]
    ppermute x0 -> x2, starting transfers between devices: none -> 25.1 us  [scatter_seq(): got = lax.ppermute(send, 'zh', [(0, 1), (1, 0)])]
    convert_element_type x2, local copies, waits for them, and re-layouts: 1.12 us -> 19.2 us  [scatter_seq(): parts = jnp.moveaxis(parts, 2, 0).astype(first_type)]
    ppermute x2, starting transfers between devices: 7.33 us -> 24.8 us  [shifted(): return lax.ppermute(value, axis, pairs)]
  transfers between devices with their start and end apart: 5 -> 12, of which waited for: 5 -> 12; matrix products, arithmetic and copies ran while one was open for 1% -> 1% of each run, Pallas kernels for 0% -> 0%
where the time goes in v1:
time: 472 us; the launch traced here: 471 us
  waiting for transfers between devices  297 us (63%)
  starting transfers between devices  50.2 us (11%)
  local copies, waits for them, and re-layouts  43.7 us (9%)
  blocking collectives  43.2 us (9%)
  between operations  15 us (3%)
  matrix products  11.9 us (3%)
  other arithmetic  9.68 us (2%)
    all_gather x2, waiting for transfers between devices, gather_seq(): step = lax.all_gather(step, 'y', axis=0)  77 us
    unnamed x9, waiting for transfers between devices  59.1 us
    reduce_scatter x2, waiting for transfers between devices, scatter_seq(): parts = lax.psum_scatter(parts, 'c', scatter_dimension=0)  58.6 us
    all_gather x2, waiting for transfers between devices, gather_seq(): step = lax.all_gather(step, 'c', axis=0)  52.4 us
    all_gather x2, blocking collectives, gather_seq(): step = lax.all_gather(piece, 'zh', axis=0)  43.2 us
    reduce_scatter x1, waiting for transfers between devices, scatter_seq(): parts = lax.psum_scatter(parts, 'y', scatter_dimension=0)  33.3 us
    ppermute x2, starting transfers between devices, scatter_seq(): got = lax.ppermute(send, 'zh', [(0, 1), (1, 0)])  25.1 us
    ppermute x2, starting transfers between devices, shifted(): return lax.ppermute(value, axis, pairs)  24.8 us
  transfers between devices with their start and end apart: 12, of which 12 were waited for; matrix products, arithmetic and copies ran while one was open for 1% of the time, Pallas kernels for 0%

profile of v1, /device:TPU:1, one launch (start us, length us, event | category | flops | bytes accessed | tf_op | source)
XLA Modules:
  0.0 471.2 jit_solution(1470566637891238517)
XLA Ops:
  7.2 0.0 all-gather.10.cloned.1.call-start
  7.2 28.8 %all_gather.33 = bf16[2,384,256]{2,1,0:T(8,128)(2,1)} all-gather(bf16[1,384,256]{2,1,0:T(8,128)(2,1)} %param.13), channel_id=1, replica_groups=mesh['rep'=32,'zh'=2,'y'=4,'c'=2] {'zh'}, dimensions={0}, use_global_device_ids=true | all-gather | bytes 589824 | tf_op jit(solution)/shard_map/all_gather | solution.py:34
  36.1 0.0 all-gather.10.cloned.1.call-update
  36.1 0.0 all-gather.12.cloned.1.call-start
  36.1 38.4 %all-gather.10.cloned.1.call-done = bf16[8,384,256]{2,1,0:T(8,128)(2,1)} async-done(((bf16[2,384,256]{2,1,0:T(8,128)(2,1)}), bf16[8,384,256]{2,1,0:T(8,128)(2,1)}) %all-gather.10.cloned.1.call-update) | async-done | bytes 1572880 | tf_op jit(solution)/shard_map/all_gather | solution.py:35
  74.5 0.0 all-gather.14.cloned.1.call-start
  74.6 26.3 %all-gather.12.cloned.1.call-done = bf16[8,2,384,256]{3,2,1,0:T(8,128)(2,1)} async-done(((bf16[4,2,384,256]{3,2,1,0:T(8,128)(2,1)}), bf16[8,2,384,256]{3,2,1,0:T(8,128)(2,1)}) %all-gather.12.cloned.1.call-update) | async-done | bytes 3145744 | tf_op jit(solution)/shard_map/all_gather | solution.py:36
  100.9 2.2 copy.30
  103.1 1.0 fusion.17
  104.0 14.3 %all-gather.2 = bf16[512,256]{1,0:T(8,128)(2,1)} all-gather(bf16[256,256]{1,0:T(8,128)(2,1)S(1)} %fusion.17), channel_id=4, replica_groups=mesh['rep'=32,'zh'=2,'y'=4,'c'=2] {'zh'}, dimensions={0}, use_global_device_ids=true | all-gather | bytes 393216 | tf_op jit(solution)/shard_map/all_gather | solution.py:34
  118.4 0.0 all-gather.14.cloned.1.call-update
  118.4 0.0 all-gather.16.cloned.1.call-start
  118.4 38.7 %all-gather.14.cloned.1.call-done = bf16[8,256,256]{2,1,0:T(8,128)(2,1)} async-done(((bf16[2,256,256]{2,1,0:T(8,128)(2,1)}), bf16[8,256,256]{2,1,0:T(8,128)(2,1)}) %all-gather.14.cloned.1.call-update) | async-done | bytes 1048592 | tf_op jit(solution)/shard_map/all_gather | solution.py:35
  157.1 0.0 all-gather.16.cloned.1.call-update
  157.1 0.0 reduce-scatter.7.cloned.1.call-start
  157.2 0.1 constant_dynamic-slice_fusion
  157.3 0.1 fusion.36
  157.4 0.1 fusion.38
  157.5 0.1 copy.29
  157.6 0.1 broadcast_in_dim.33
  157.7 0.1 reshape.54
  157.8 0.1 copy.32
  158.0 26.1 %all-gather.16.cloned.1.call-done = bf16[8,2,256,256]{3,2,1,0:T(8,128)(2,1)} async-done(((bf16[4,2,256,256]{3,2,1,0:T(8,128)(2,1)}), bf16[8,2,256,256]{3,2,1,0:T(8,128)(2,1)}) %all-gather.16.cloned.1.call-update) | async-done | bytes 2097168 | tf_op jit(solution)/shard_map/all_gather | solution.py:36
  184.0 1.7 copy.31
  185.8 0.3 broadcast_in_dim.34
  186.1 1.2 fusion.40
  187.2 0.3 fusion.16
  187.6 0.8 fusion.30
  188.4 0.6 fusion.20
  189.0 0.8 fusion.12
  189.8 1.3 copy-done.3
  191.1 0.8 fusion.33
  191.9 2.3 pad_maximum_fusion
  194.2 6.6 %reshape.58 = f32[2,4,2,256,256]{3,2,1,0,4:T(2,128)} reshape(f32[4096,256]{0,1:T(8,128)} %pad_maximum_fusion) | data formatting | bytes 8388608 | tf_op jit(solution)/shard_map/reshape | solution.py:44
  200.7 7.3 %copy.33 = f32[2,4,2,256,256]{4,3,1,0,2:T(8,128)} copy(f32[2,4,2,256,256]{3,2,1,0,4:T(2,128)} %reshape.58) | data formatting | bytes 8388608 | tf_op jit(solution)/shard_map/reshape | solution.py:44
  208.1 0.0 all-reduce.3.cloned.1.call-start
  208.1 23.5 %reduce-scatter.7.cloned.1.call-done = f32[1,2,4,256,256]{4,3,2,1,0:T(8,128)} async-done(((f32[2,2,4,256,256]{4,3,2,1,0:T(8,128)}), f32[1,2,4,256,256]{4,3,2,1,0:T(8,128)}) %reduce-scatter.7.cloned.1.call-update) | async-done | bytes 2097168 | tf_op jit(solution)/shard_map/reduce_scatter | solution.py:46
  231.6 2.7 convert_bitcast_fusion.1
  234.3 0.0 all-reduce.3.cloned.1.call-update
  234.3 0.0 reduce-scatter.9.cloned.1.call-start
  234.3 1.3 dynamic-slice.12
  235.6 59.0 %all-reduce.3.cloned.1.call-done = bf16[4,2,256,256]{3,2,0,1:T(8,128)(2,1)} async-done(((bf16[4,2,256,256]{3,2,0,1:T(8,128)(2,1)}), bf16[4,2,256,256]{3,2,0,1:T(8,128)(2,1)}) %all-reduce.3.cloned.1.call-update) | async-done | bytes 1048592
  294.6 1.6 dynamic-slice_bitcast_fusion
  296.2 0.7 dynamic-slice_bitcast_fusion.2
  296.9 12.5 %collective-permute-start.8 = (bf16[256,256]{1,0:T(8,128)(2,1)}, bf16[256,256]{1,0:T(8,128)(2,1)S(1)}, u32[]{:S(2)}, u32[]{:S(2)}) collective-permute-start(bf16[256,256]{1,0:T(8,128)(2,1)} %dynamic-slice_bitcast_fusion.2), channel_id=1, source_target_pairs={{0,8},{8,0},{1,9},{9,1},{2,10},{10,2},{3,11},{11,3},{4,12},{12,4},... | collective-permute-start | bytes 393224 | tf_op jit(solution)/shard_map/ppermute | solution.py:53
  309.4 2.9 collective-permute-done.8
  312.3 3.6 fusion.5
  315.9 9.0 %reshape.64 = f32[2,4,2,384,256]{3,2,1,0,4:T(2,128)} reshape(f32[6144,256]{0,1:T(8,128)} %fusion.5) | data formatting | bytes 12582912 | tf_op jit(solution)/shard_map/convert_element_type | solution.py:45
  324.9 10.2 %copy.36 = f32[2,4,2,384,256]{4,3,0,1,2:T(8,128)} copy(f32[2,4,2,384,256]{3,2,1,0,4:T(2,128)} %reshape.64) | data formatting | bytes 12582912 | tf_op jit(solution)/shard_map/convert_element_type | solution.py:45
  335.2 0.0 reduce-scatter.11.cloned.1.call-start
  335.2 35.1 %reduce-scatter.9.cloned.1.call-done = f32[1,2,4,384,256]{4,3,1,2,0:T(8,128)} async-done(((f32[2,2,4,384,256]{4,3,1,2,0:T(8,128)}), f32[1,2,4,384,256]{4,3,1,2,0:T(8,128)}) %reduce-scatter.9.cloned.1.call-update) | async-done | bytes 3145744 | tf_op jit(solution)/shard_map/reduce_scatter | solution.py:46
  370.3 3.2 convert_bitcast_fusion
  374.3 33.3 %reduce-scatter.11.cloned.1.call-done = bf16[1,2,384,256]{3,2,1,0:T(8,128)(2,1)} async-done(((bf16[4,2,384,256]{3,2,1,0:T(8,128)(2,1)}), bf16[1,2,384,256]{3,2,1,0:T(8,128)(2,1)}) %reduce-scatter.11.cloned.1.call-update) | async-done | bytes 393232 | tf_op jit(solution)/shard_map/reduce_scatter | solution.py:48
  407.6 1.0 dynamic-slice_bitcast_fusion.1
  408.6 12.5 %collective-permute-start.9 = (bf16[384,256]{1,0:T(8,128)(2,1)S(1)}, bf16[384,256]{1,0:T(8,128)(2,1)S(1)}, u32[]{:S(2)}, u32[]{:S(2)}) collective-permute-start(bf16[384,256]{1,0:T(8,128)(2,1)S(1)} %dynamic-slice_bitcast_fusion.1), channel_id=1, source_target_pairs={{0,8},{8,0},{1,9},{9,1},{2,10},{10,2},{3,11},{11,3},{4,12},{12,4},... | collective-permute-start | bytes 589832 | tf_op jit(solution)/shard_map/ppermute | solution.py:53
  421.2 3.2 fusion.21
  424.4 0.4 collective-permute-done.9
  424.8 39.5 %conditional.1 = (f32[1,384,256]{2,1,0:T(8,128)}) conditional(s32[]{:T(128)} %clamp.3, (bf16[1,2,384,256]{3,2,1,0:T(8,128)(2,1)S(1)}, s32[]{:T(128)}, f32[384,256]{1,0:T(8,128)S(1)}) %tuple.51, (bf16[1,2,384,256]{3,2,1,0:T(8,128)(2,1)S(1)}, s32[]{:T(128)}, f32[384,256]{1,0:T(8,128)S(1)}) %tuple.52, ...), branch_computations={%region_7.8_spmd, %region_8.9_spmd, %region_9.10_spmd, %region_10.... | conditional | flops 983040 | bytes 3735648 | solution.py:142
  424.9 0.1 fusion.3
  424.9 22.9 %collective-permute-start.7 = (bf16[384,256]{1,0:T(8,128)(2,1)S(1)}, bf16[384,256]{1,0:T(8,128)(2,1)S(1)}, u32[]{:S(2)}, u32[]{:S(2)}) collective-permute-start(bf16[384,256]{1,0:T(8,128)(2,1)S(1)} %fusion.3), channel_id=1, source_target_pairs={{0,384},{16,400},{32,416},{48,432},{64,448},{80,464},{96,480},{112... | collective-permute-start | bytes 589832 | tf_op jit(solution)/shard_map/cond/branch_3_fun/ppermute | solution.py:24
  447.8 1.9 collective-permute-start.6
  449.7 1.8 collective-permute-done.7
  451.6 12.0 %collective-permute-done.6 = bf16[384,256]{1,0:T(8,128)(2,1)S(1)} collective-permute-done((bf16[384,256]{1,0:T(8,128)(2,1)S(1)}, bf16[384,256]{1,0:T(8,128)(2,1)S(1)}, u32[]{:S(2)}, u32[]{:S(2)}) %collective-permute-start.6) | collective-permute-done | bytes 196640 | tf_op jit(solution)/shard_map/cond/branch_3_fun/ppermute | solution.py:24
  463.5 0.8 multiply_bitcast_fusion.3
  (20 shorter events, 0.1 us)
Async XLA Ops:
  7.2 95.9 %copy-start = (bf16[1,256,6144]{2,1,0:T(8,128)(2,1)S(1)}, bf16[1,256,6144]{2,1,0:T(8,128)(2,1)}, u32[]{:S(2)}) copy-start(bf16[1,256,6144]{2,1,0:T(8,128)(2,1)} %param.10) | copy-start | bytes 9437188
  7.2 67.3 %all-gather.10.cloned.1.call-start = ((), (), s32[]{:S(2)}) async-start(), calls=%async_computation.6 | async-start | bytes 1966080 | tf_op jit(solution)/shard_map/all_gather | solution.py:35
  36.1 64.8 %all-gather.12.cloned.1.call-start = ((), (), s32[]{:S(2)}) async-start(), calls=%async_computation.7 | async-start | bytes 4718592 | tf_op jit(solution)/shard_map/all_gather | solution.py:36
  74.5 82.6 %all-gather.14.cloned.1.call-start = ((), (), s32[]{:S(2)}) async-start(), calls=%async_computation.8 | async-start | bytes 1310720 | tf_op jit(solution)/shard_map/all_gather | solution.py:35
  103.0 54.2 %copy-start.6 = (s32[64,3]{0,1:T(4,128)S(1)}, s32[64,3]{0,1:T(4,128)}, u32[]{:S(2)}) copy-start(s32[64,3]{0,1:T(4,128)} %param.14) | copy-start | bytes 2308
  103.0 54.8 %copy-start.5 = (bf16[1,256,128]{2,1,0:T(8,128)(2,1)S(1)}, bf16[1,256,128]{2,1,0:T(8,128)(2,1)}, u32[]{:S(2)}) copy-start(bf16[1,256,128]{2,1,0:T(8,128)(2,1)} %param.12) | copy-start | bytes 196612
  118.4 65.7 %all-gather.16.cloned.1.call-start = ((), (), s32[]{:S(2)}) async-start(), calls=%async_computation.9 | async-start | bytes 3145728 | tf_op jit(solution)/shard_map/all_gather | solution.py:36
  157.1 29.0 %copy-start.4 = (bf16[1,256,128]{2,1,0:T(8,128)(2,1)S(1)}, bf16[1,256,128]{2,1,0:T(8,128)(2,1)}, u32[]{:S(2)}) copy-start(bf16[1,256,128]{2,1,0:T(8,128)(2,1)} %param.11) | copy-start | bytes 196612
  157.1 74.5 %reduce-scatter.7.cloned.1.call-start = ((), (), s32[]{:S(2)}) async-start(), calls=%async_computation.3 | async-start | bytes 6291456 | tf_op jit(solution)/shard_map/reduce_scatter | solution.py:46
  185.8 3.2 copy-start.2
  189.8 1.3 copy-start.3
  208.1 86.6 %all-reduce.3.cloned.1.call-start = ((), (), s32[]{:S(2)}) async-start(), calls=%async_computation.10 | async-start | bytes 2097152
  234.3 136.1 %reduce-scatter.9.cloned.1.call-start = ((), (), s32[]{:S(2)}) async-start(), calls=%async_computation.4 | async-start | bytes 9437184 | tf_op jit(solution)/shard_map/reduce_scatter | solution.py:46
  296.9 15.4 %collective-permute-start.8 = (bf16[256,256]{1,0:T(8,128)(2,1)}, bf16[256,256]{1,0:T(8,128)(2,1)S(1)}, u32[]{:S(2)}, u32[]{:S(2)}) collective-permute-start(bf16[256,256]{1,0:T(8,128)(2,1)} %dynamic-slice_bitcast_fusion.2), channel_id=1, source_target_pairs={{0,8},{8,0},{1,9},{9,1},{2,10},{10,2},{3,11},{11,3},{4,12},{12,4},... | collective-permute-start | bytes 393224 | tf_op jit(solution)/shard_map/ppermute | solution.py:53
  335.2 72.4 %reduce-scatter.11.cloned.1.call-start = ((), (), s32[]{:S(2)}) async-start(), calls=%async_computation.5 | async-start | bytes 1966080 | tf_op jit(solution)/shard_map/reduce_scatter | solution.py:48
  407.6 17.2 %copy-start.1 = (bf16[1,2,384,256]{3,2,1,0:T(8,128)(2,1)S(1)}, bf16[1,2,384,256]{3,2,1,0:T(8,128)(2,1)}, u32[]{:S(2)}) copy-start(bf16[1,2,384,256]{3,2,1,0:T(8,128)(2,1)} %reduce-scatter.11.cloned.1.call-done) | copy-start | bytes 1179652
  408.6 16.2 %collective-permute-start.9 = (bf16[384,256]{1,0:T(8,128)(2,1)S(1)}, bf16[384,256]{1,0:T(8,128)(2,1)S(1)}, u32[]{:S(2)}, u32[]{:S(2)}) collective-permute-start(bf16[384,256]{1,0:T(8,128)(2,1)S(1)} %dynamic-slice_bitcast_fusion.1), channel_id=1, source_target_pairs={{0,8},{8,0},{1,9},{9,1},{2,10},{10,2},{3,11},{11,3},{4,12},{12,4},... | collective-permute-start | bytes 589832 | tf_op jit(solution)/shard_map/ppermute | solution.py:53
  424.9 26.6 %collective-permute-start.7 = (bf16[384,256]{1,0:T(8,128)(2,1)S(1)}, bf16[384,256]{1,0:T(8,128)(2,1)S(1)}, u32[]{:S(2)}, u32[]{:S(2)}) collective-permute-start(bf16[384,256]{1,0:T(8,128)(2,1)S(1)} %fusion.3), channel_id=1, source_target_pairs={{0,384},{16,400},{32,416},{48,432},{64,448},{80,464},{96,480},{112... | collective-permute-start | bytes 589832 | tf_op jit(solution)/shard_map/cond/branch_3_fun/ppermute | solution.py:24
  447.8 15.7 %collective-permute-start.6 = (bf16[384,256]{1,0:T(8,128)(2,1)S(1)}, bf16[384,256]{1,0:T(8,128)(2,1)S(1)}, u32[]{:S(2)}, u32[]{:S(2)}) collective-permute-start(bf16[384,256]{1,0:T(8,128)(2,1)S(1)} %fusion.3), channel_id=1, source_target_pairs={{0,128},{16,144},{32,160},{48,176},{64,192},{80,208},{96,224},{112... | collective-permute-start | bytes 589832 | tf_op jit(solution)/shard_map/cond/branch_3_fun/ppermute | solution.py:24
Sparse Core Ops, SparseCore 0:
  36.2 38.2 all-gather.9
  76.6 24.2 all-gather.11
  118.5 38.5 all-gather.13
  159.0 24.9 all-gather.15
  208.2 23.3 reduce-scatter.6
  234.4 60.1 all-reduce.2
  335.3 35.0 reduce-scatter.8
  373.7 33.8 reduce-scatter.10

commit v2 on v1

--- a/solution.py
+++ b/solution.py
@@ -30,28 +30,45 @@
     ) + lax.axis_index("c")
 
 
-def gather_seq(piece):
-    step = lax.all_gather(piece, "zh", axis=0)
-    step = lax.all_gather(step, "y", axis=0)
-    step = lax.all_gather(step, "c", axis=0)
-    step = jnp.transpose(step, (2, 1, 0) + tuple(range(3, step.ndim)))
-    return step.reshape((-1,) + piece.shape[1:])
+def swap_zh(value):
+    return lax.ppermute(value, "zh", [(0, 1), (1, 0)])
 
 
-def scatter_seq(whole, first_type, later_type):
+def spread_half(piece):
+    count = lax.axis_size("y") * lax.axis_size("c")
+    copies = jnp.broadcast_to(piece[None], (count,) + piece.shape)
+    return lax.all_to_all(copies, ("y", "c"), 0, 0, tiled=False)
+
+
+def gather_seq(piece):
+    from_other = swap_zh(piece)
+    own_half = spread_half(piece)
+    other_half = spread_half(from_other)
+    first_own = lax.axis_index("zh") == 0
+    low = jnp.where(first_own, own_half, other_half)
+    high = jnp.where(first_own, other_half, own_half)
+    return jnp.concatenate([low, high]).reshape((-1,) + piece.shape[1:])
+
+
+def reduce_half(part):
+    core = lax.axis_index("c")
+    keep = lax.dynamic_index_in_dim(part, core, 1, keepdims=False)
+    send = lax.dynamic_index_in_dim(part, 1 - core, 1, keepdims=False)
+    got = lax.ppermute(send, "c", [(0, 1), (1, 0)])
+    summed = (keep.astype(jnp.float32) + got.astype(jnp.float32)).astype(jnp.bfloat16)
+    spread = lax.all_to_all(summed, "y", 0, 0, tiled=False)
+    return jnp.sum(spread.astype(jnp.float32), axis=0)
+
+
+def scatter_seq(whole):
     zh_n, y_n, c_n = (lax.axis_size(name) for name in SEQ_AXES)
     rows = whole.shape[0] // (zh_n * y_n * c_n)
     parts = whole.reshape((zh_n, y_n, c_n, rows) + whole.shape[1:])
-    parts = jnp.moveaxis(parts, 2, 0).astype(first_type)
-    parts = lax.psum_scatter(parts, "c", scatter_dimension=0)
-    parts = jnp.moveaxis(parts, 1, 0).astype(later_type)
-    parts = lax.psum_scatter(parts, "y", scatter_dimension=0)
     mine = lax.axis_index("zh")
-    other = 1 - mine
-    keep = lax.dynamic_index_in_dim(parts, mine, 0, keepdims=False).astype(jnp.float32)
-    send = lax.dynamic_index_in_dim(parts, other, 0, keepdims=False)
-    got = lax.ppermute(send, "zh", [(0, 1), (1, 0)])
-    return keep + got.astype(jnp.float32)
+    for_other = reduce_half(lax.dynamic_index_in_dim(parts, 1 - mine, 0, keepdims=False))
+    got = swap_zh(for_other.astype(jnp.bfloat16))
+    for_me = reduce_half(lax.dynamic_index_in_dim(parts, mine, 0, keepdims=False))
+    return for_me + got.astype(jnp.float32)
 
 
 def fold_rows(tok_rows, row_piece):
@@ -131,10 +148,8 @@
     key_terms = contract_rows(score_grad, query_here)
     value_terms = contract_rows(prob_low, grad_here)
     grad_terms = jnp.concatenate([key_terms, value_terms], axis=1)
-    kv_grad = scatter_seq(grad_terms, jnp.float32, jnp.bfloat16).astype(jnp.bfloat16)
-    grad_slice = scatter_seq(
-        contract_rows(tokens_here, kv_grad).astype(jnp.bfloat16), jnp.float32, jnp.bfloat16
-    )
+    kv_grad = scatter_seq(grad_terms.astype(jnp.bfloat16)).astype(jnp.bfloat16)
+    grad_slice = scatter_seq(contract_rows(tokens_here, kv_grad).astype(jnp.bfloat16))
     branches = [
         partial(gossip, distance=(1 << level_idx) % rep_count, rep_count=rep_count)
         for level_idx in range(4)

time: 472 us -> 290 us (0.61)
  waiting for transfers between devices: 297 us -> 67.5 us
  starting transfers between devices: 50.2 us -> 126 us
  blocking collectives: 43.2 us -> 12.3 us
  other arithmetic: 9.68 us -> 23.7 us
  between operations: 15 us -> 1.66 us
    all_gather x4 -> x0, waiting for transfers between devices: 129 us -> none  [the longest x2 77 us: gather_seq(): step = lax.all_gather(step, 'y', axis=0)]
    reduce_scatter x3 -> x0, waiting for transfers between devices: 91.9 us -> none  [the longest x2 58.6 us: scatter_seq(): parts = lax.psum_scatter(parts, 'c', scatter_dimension=0)]
    unnamed x9 -> x0, waiting for transfers between devices: 59.1 us -> none
    all_to_all x0 -> x7, waiting for transfers between devices: none -> 43.5 us  [the longest x4 38.8 us: spread_half(): return lax.all_to_all(copies, ('y', 'c'), 0, 0, tiled=False)]
    all_gather x2 -> x0, blocking collectives: 43.2 us -> none  [gather_seq(): step = lax.all_gather(piece, 'zh', axis=0)]
    all_to_all x0 -> x7, starting transfers between devices: none -> 39.5 us  [the longest x4 26.7 us: spread_half(): return lax.all_to_all(copies, ('y', 'c'), 0, 0, tiled=False)]
    ppermute x2 -> x8, starting transfers between devices: 25.1 us -> 53 us  [the longest x4 42 us: swap_zh(): return lax.ppermute(value, 'zh', [(0, 1), (1, 0)])]
    convert_element_type x2 -> x1, local copies, waits for them, and re-layouts: 19.2 us -> 0.1 us  [per_device(): fold_rows(tokens_here, gather_seq(weight_here)).astype(jnp.bfloat16)]
  transfers between devices with their start and end apart: 12 -> 17, of which waited for: 12 -> 9; matrix products, arithmetic and copies ran while one was open for 1% -> 10% of each run, Pallas kernels for 0% -> 0%
where the time goes in v2:
time: 290 us; the launch traced here: 287 us
  starting transfers between devices  126 us (43%)
  waiting for transfers between devices  67.5 us (23%)
  local copies, waits for them, and re-layouts  45 us (16%)
  other arithmetic  23.7 us (8%)
  blocking collectives  12.3 us (4%)
  matrix products  11.1 us (4%)
    ppermute x4, starting transfers between devices, swap_zh(): return lax.ppermute(value, 'zh', [(0, 1), (1, 0)])  42 us
    all_to_all x4, waiting for transfers between devices, spread_half(): return lax.all_to_all(copies, ('y', 'c'), 0, 0, tiled=False)  38.8 us
    ppermute x2, starting transfers between devices, shifted(): return lax.ppermute(value, axis, pairs)  33.6 us
    all_to_all x4, starting transfers between devices, spread_half(): return lax.all_to_all(copies, ('y', 'c'), 0, 0, tiled=False)  26.7 us
    unnamed x24, local copies, waits for them, and re-layouts  15.3 us
    ppermute x4, waiting for transfers between devices, swap_zh(): return lax.ppermute(value, 'zh', [(0, 1), (1, 0)])  14.4 us
    all_to_all x3, starting transfers between devices, reduce_half(): spread = lax.all_to_all(summed, 'y', 0, 0, tiled=False)  12.8 us
    all_to_all x1, blocking collectives, reduce_half(): spread = lax.all_to_all(summed, 'y', 0, 0, tiled=False)  12.3 us
  transfers between devices with their start and end apart: 17, of which 9 were waited for; matrix products, arithmetic and copies ran while one was open for 10% of the time, Pallas kernels for 0%

profile of v2, /device:TPU:1, one launch (start us, length us, event | category | flops | bytes accessed | tf_op | source)
XLA Modules:
  0.0 287.4 jit_solution(5294476079614480111)
XLA Ops:
  0.7 2.3 broadcast_in_dim.61
  3.0 11.0 %all-to-all-start = ((bf16[8,384,256]{2,1,0:T(8,128)(2,1)}), bf16[8,384,256]{2,1,0:T(8,128)(2,1)}, u32[]{:S(2)}, u32[]{:S(2)}) async-start(bf16[8,384,256]{2,1,0:T(8,128)(2,1)} %broadcast_in_dim.61), calls=%async_computation | async-start | bytes 3145728 | tf_op jit(solution)/shard_map/all_to_all | solution.py:40
  14.0 10.4 %collective-permute-start.8 = (bf16[384,256]{1,0:T(8,128)(2,1)S(1)}, bf16[384,256]{1,0:T(8,128)(2,1)S(1)}, u32[]{:S(2)}, u32[]{:S(2)}) collective-permute-start(bf16[384,256]{1,0:T(8,128)(2,1)S(1)} %bitcast.112), channel_id=1, source_target_pairs={{0,8},{8,0},{1,9},{9,1},{2,10},{10,2},{3,11},{11,3},{4,12},{12,4},... | collective-permute-start | bytes 589832 | tf_op jit(solution)/shard_map/ppermute | solution.py:34
  24.4 6.5 %collective-permute-done.8 = bf16[384,256]{1,0:T(8,128)(2,1)S(1)} collective-permute-done((bf16[384,256]{1,0:T(8,128)(2,1)S(1)}, bf16[384,256]{1,0:T(8,128)(2,1)S(1)}, u32[]{:S(2)}, u32[]{:S(2)}) %collective-permute-start.8) | collective-permute-done | bytes 196640 | tf_op jit(solution)/shard_map/ppermute | solution.py:34
  30.9 3.8 %all-to-all-done = bf16[8,384,256]{2,1,0:T(8,128)(2,1)} async-done(((bf16[8,384,256]{2,1,0:T(8,128)(2,1)}), bf16[8,384,256]{2,1,0:T(8,128)(2,1)}, u32[]{:S(2)}, u32[]{:S(2)}) %all-to-all-start) | async-done | bytes 1572896 | tf_op jit(solution)/shard_map/all_to_all | solution.py:40
  34.7 1.3 broadcast_in_dim.62
  36.0 5.1 %all-to-all-start.1 = ((bf16[8,384,256]{2,1,0:T(8,128)(2,1)}), bf16[8,384,256]{2,1,0:T(8,128)(2,1)}, u32[]{:S(2)}, u32[]{:S(2)}) async-start(bf16[8,384,256]{2,1,0:T(8,128)(2,1)} %broadcast_in_dim.62), calls=%async_computation.1 | async-start | bytes 3145728 | tf_op jit(solution)/shard_map/all_to_all | solution.py:40
  41.1 20.7 %all-to-all-done.1 = bf16[8,384,256]{2,1,0:T(8,128)(2,1)} async-done(((bf16[8,384,256]{2,1,0:T(8,128)(2,1)}), bf16[8,384,256]{2,1,0:T(8,128)(2,1)}, u32[]{:S(2)}, u32[]{:S(2)}) %all-to-all-start.1) | async-done | bytes 1572896 | tf_op jit(solution)/shard_map/all_to_all | solution.py:40
  61.8 2.1 broadcast_select_fusion.1
  64.2 1.1 fusion.17
  65.4 1.0 broadcast_in_dim.63
  66.4 5.1 %all-to-all-start.2 = ((bf16[8,256,256]{2,1,0:T(8,128)(2,1)}), bf16[8,256,256]{2,1,0:T(8,128)(2,1)}, u32[]{:S(2)}, u32[]{:S(2)}) async-start(bf16[8,256,256]{2,1,0:T(8,128)(2,1)} %broadcast_in_dim.63), calls=%async_computation.2 | async-start | bytes 2097152 | tf_op jit(solution)/shard_map/all_to_all | solution.py:40
  71.5 10.5 %collective-permute-start.9 = (bf16[256,256]{0,1:T(8,128)(2,1)S(1)}, bf16[256,256]{0,1:T(8,128)(2,1)}, u32[]{:S(2)}, u32[]{:S(2)}) collective-permute-start(bf16[256,256]{0,1:T(8,128)(2,1)S(1)} %fusion.17), channel_id=1, source_target_pairs={{0,8},{8,0},{1,9},{9,1},{2,10},{10,2},{3,11},{11,3},{4,12},{12,4},... | collective-permute-start | bytes 393224 | tf_op jit(solution)/shard_map/ppermute | solution.py:34
  82.0 5.2 %collective-permute-done.9 = bf16[256,256]{0,1:T(8,128)(2,1)} collective-permute-done((bf16[256,256]{0,1:T(8,128)(2,1)S(1)}, bf16[256,256]{0,1:T(8,128)(2,1)}, u32[]{:S(2)}, u32[]{:S(2)}) %collective-permute-start.9) | collective-permute-done | bytes 131104 | tf_op jit(solution)/shard_map/ppermute | solution.py:34
  87.2 1.0 copy.35
  88.2 1.1 broadcast_in_dim.64
  89.3 5.5 %all-to-all-start.3 = ((bf16[8,256,256]{2,1,0:T(8,128)(2,1)}), bf16[8,256,256]{2,1,0:T(8,128)(2,1)}, u32[]{:S(2)}, u32[]{:S(2)}) async-start(bf16[8,256,256]{2,1,0:T(8,128)(2,1)} %broadcast_in_dim.64), calls=%async_computation.3 | async-start | bytes 2097152 | tf_op jit(solution)/shard_map/all_to_all | solution.py:40
  95.5 14.3 %all-to-all-done.3 = bf16[8,256,256]{2,1,0:T(8,128)(2,1)} async-done(((bf16[8,256,256]{2,1,0:T(8,128)(2,1)}), bf16[8,256,256]{2,1,0:T(8,128)(2,1)}, u32[]{:S(2)}, u32[]{:S(2)}) %all-to-all-start.3) | async-done | bytes 1048608 | tf_op jit(solution)/shard_map/all_to_all | solution.py:40
  109.8 1.7 broadcast_select_fusion.3
  111.7 0.3 broadcast_in_dim.59
  112.0 0.3 copy-done.6
  112.4 1.2 fusion.47
  113.5 0.3 fusion.11
  113.9 0.6 fusion.20
  114.4 0.8 fusion.7
  115.2 0.8 convolution_convert_fusion.2
  116.1 0.8 convolution_convert_fusion.1
  116.9 1.2 fusion.29
  118.2 2.9 %collective-permute-start.11 = (bf16[4,256,256]{1,2,0:T(8,128)(2,1)}, bf16[4,256,256]{1,2,0:T(8,128)(2,1)}, u32[]{:S(2)}, u32[]{:S(2)}) collective-permute-start(bf16[4,256,256]{1,2,0:T(8,128)(2,1)} %get-tuple-element.60), channel_id=1, source_target_pairs={{0,1},{1,0},{2,3},{3,2},{4,5},{5,4},{6,7},{7,6},{8,9},{9,8},{10,11... | collective-permute-start | bytes 1572872 | tf_op jit(solution)/shard_map/ppermute | solution.py:57
  121.1 1.9 collective-permute-start.10
  123.1 2.2 collective-permute-done.10
  125.3 2.6 fusion.22
  127.8 12.3 %all_to_all.40 = bf16[4,256,256]{1,2,0:T(8,128)(2,1)} all-to-all(bf16[4,256,256]{1,2,0:T(8,128)(2,1)S(1)} %get-tuple-element.58), channel_id=1, replica_groups=mesh['rep'=32,'zh'=2,'y'=4,'c'=2] {'y'}, dimensions={0} | all-to-all | bytes 1048576 | tf_op jit(solution)/shard_map/all_to_all | solution.py:59
  140.1 4.1 %all-to-all-start.4 = ((bf16[4,256,256]{1,2,0:T(8,128)(2,1)}), bf16[4,256,256]{1,2,0:T(8,128)(2,1)}, u32[]{:S(2)}, u32[]{:S(2)}) async-start(bf16[4,256,256]{1,2,0:T(8,128)(2,1)} %get-tuple-element.59), calls=%async_computation.4 | async-start | bytes 1048576 | tf_op jit(solution)/shard_map/all_to_all | solution.py:59
  144.3 1.1 reduce_sum.82
  145.4 10.6 %collective-permute-start.12 = (bf16[256,256]{0,1:T(8,128)(2,1)S(1)}, bf16[256,256]{0,1:T(8,128)(2,1)S(1)}, u32[]{:S(2)}, u32[]{:S(2)}) collective-permute-start(bf16[256,256]{0,1:T(8,128)(2,1)S(1)} %reduce_sum.82), channel_id=1, source_target_pairs={{0,8},{8,0},{1,9},{9,1},{2,10},{10,2},{3,11},{11,3},{4,12},{12,4},... | collective-permute-start | bytes 393224 | tf_op jit(solution)/shard_map/ppermute | solution.py:34
  156.1 1.1 convert_reduce_fusion
  157.2 2.6 collective-permute-done.12
  159.8 2.7 fusion
  162.5 8.1 %reshape.67 = bf16[2,4,2,384,256]{3,2,1,0,4:T(2,128)(2,1)} reshape(bf16[6144,256]{0,1:T(8,128)(2,1)} %fusion) | data formatting | bytes 6291456 | tf_op jit(solution)/shard_map/reshape | solution.py:66
  170.5 9.4 %constant_dynamic-slice_fusion.1 = (bf16[1,4,1,384,256]{3,2,1,0,4:T(2,128)(2,1)}, bf16[1,4,1,384,256]{3,2,1,0,4:T(2,128)(2,1)}, bf16[1,4,1,384,256]{3,2,1,0,4:T(2,128)(2,1)}, bf16[1,4,1,384,256]{3,2,1,0,4:T(2,128)(2,1)}) fusion(bf16[2,4,2,384,256]{3,2,1,0,4:T(2,128)(2,1)} %reshape.67, s32[]{:T(128)S(6)} %select_n.86, s32[]{:T(128)S(6)} %select_n.82, ...), kind=kLoop, calls=%fused_computation.71 | loop fusion | bytes 6291472 | tf_op jit(solution)/shard_map/jit(dynamic_index_in_dim)/dynamic_slice | solution.py:55
  180.0 4.7 %copy.47 = bf16[1,4,1,384,256]{4,3,1,2,0:T(8,128)(2,1)} copy(bf16[1,4,1,384,256]{3,2,1,0,4:T(2,128)(2,1)} %get-tuple-element.55) | data formatting | bytes 1572864
  184.6 4.3 %collective-permute-start.14 = (bf16[4,384,256]{2,1,0:T(8,128)(2,1)}, bf16[4,384,256]{2,1,0:T(8,128)(2,1)}, u32[]{:S(2)}, u32[]{:S(2)}) collective-permute-start(bf16[4,384,256]{2,1,0:T(8,128)(2,1)} %bitcast.110), channel_id=1, source_target_pairs={{0,1},{1,0},{2,3},{3,2},{4,5},{5,4},{6,7},{7,6},{8,9},{9,8},{10,11... | collective-permute-start | bytes 2359304 | tf_op jit(solution)/shard_map/ppermute | solution.py:57
  188.9 4.7 %copy.39 = bf16[1,4,1,384,256]{4,3,1,2,0:T(8,128)(2,1)} copy(bf16[1,4,1,384,256]{3,2,1,0,4:T(2,128)(2,1)} %get-tuple-element.54) | data formatting | bytes 1572864 | tf_op jit(solution)/shard_map/jit(dynamic_index_in_dim)/dynamic_slice | solution.py:56
  193.5 1.9 collective-permute-start.13
  195.5 4.6 %copy.46 = bf16[1,4,1,384,256]{4,3,1,2,0:T(8,128)(2,1)} copy(bf16[1,4,1,384,256]{3,2,1,0,4:T(2,128)(2,1)} %get-tuple-element.52) | data formatting | bytes 1572864
  200.1 2.4 fusion.12
  202.5 4.5 %all-to-all-start.7 = ((bf16[4,384,256]{2,1,0:T(8,128)(2,1)}), bf16[4,384,256]{2,1,0:T(8,128)(2,1)}, u32[]{:S(2)}, u32[]{:S(2)}) async-start(bf16[4,384,256]{2,1,0:T(8,128)(2,1)} %fusion.12), calls=%async_computation.7 | async-start | bytes 1572864 | tf_op jit(solution)/shard_map/all_to_all | solution.py:59
  207.0 4.6 %copy.45 = bf16[1,4,1,384,256]{4,3,1,2,0:T(8,128)(2,1)} copy(bf16[1,4,1,384,256]{3,2,1,0,4:T(2,128)(2,1)} %get-tuple-element.53) | data formatting | bytes 1572864
  211.7 2.5 fusion.13
  214.1 4.6 %all-to-all-done.7 = bf16[4,384,256]{2,1,0:T(8,128)(2,1)} async-done(((bf16[4,384,256]{2,1,0:T(8,128)(2,1)}), bf16[4,384,256]{2,1,0:T(8,128)(2,1)}, u32[]{:S(2)}, u32[]{:S(2)}) %all-to-all-start.7) | async-done | bytes 786464 | tf_op jit(solution)/shard_map/all_to_all | solution.py:59
  218.8 4.2 %all-to-all-start.6 = ((bf16[4,384,256]{2,1,0:T(8,128)(2,1)}), bf16[4,384,256]{2,1,0:T(8,128)(2,1)}, u32[]{:S(2)}, u32[]{:S(2)}) async-start(bf16[4,384,256]{2,1,0:T(8,128)(2,1)} %fusion.13), calls=%async_computation.6 | async-start | bytes 1572864 | tf_op jit(solution)/shard_map/all_to_all | solution.py:59
  223.6 1.3 reduce_sum.83
  224.9 10.5 %collective-permute-start.15 = (bf16[384,256]{1,0:T(8,128)(2,1)S(1)}, bf16[384,256]{1,0:T(8,128)(2,1)}, u32[]{:S(2)}, u32[]{:S(2)}) collective-permute-start(bf16[384,256]{1,0:T(8,128)(2,1)S(1)} %reduce_sum.83), channel_id=1, source_target_pairs={{0,8},{8,0},{1,9},{9,1},{2,10},{10,2},{3,11},{11,3},{4,12},{12,4},... | collective-permute-start | bytes 589832 | tf_op jit(solution)/shard_map/ppermute | solution.py:34
  235.4 3.2 %fusion.21 = bf16[1,256,128]{2,1,0:T(8,128)(2,1)} fusion(bf16[256,4096]{0,1:T(8,128)(2,1)} %copy-done.4, bf16[4096,256]{1,0:T(8,128)(2,1)} %bitcast.105), kind=kOutput, calls=%fused_computation.43 | convolution fusion | flops 268468224 | bytes 3211264 | tf_op jit(solution)/shard_map/dot_general | solution.py:145
  238.7 2.4 convert_element_type.155
  241.1 1.0 convert_element_type.160
  242.1 44.6 %conditional.1 = (f32[1,384,256]{2,1,0:T(8,128)S(1)}) conditional(s32[]{:T(128)} %clamp.83, (f32[4,384,256]{2,1,0:T(8,128)}, f32[384,256]{1,0:T(8,128)S(1)}) %tuple.28, (f32[4,384,256]{2,1,0:T(8,128)}, f32[384,256]{1,0:T(8,128)S(1)}) %tuple.28, (f32[4,384,256]{2,1,0:T(8,128)}, f32[384,256]{1,0:T(8,128)S(1)}) %tuple.28, ...), branch_computations={%region_6.8_spmd, %region_8.10_spmd, %region_10.12_spmd, %region_1... | conditional | flops 983040 | bytes 6094940 | solution.py:157
  242.1 2.3 reduce_sum.72
  244.4 1.0 fusion.45
  245.4 21.9 %collective-permute-start.5 = (bf16[384,256]{1,0:T(8,128)(2,1)S(1)}, bf16[384,256]{1,0:T(8,128)(2,1)S(1)}, u32[]{:S(2)}, u32[]{:S(2)}) collective-permute-start(bf16[384,256]{1,0:T(8,128)(2,1)S(1)} %get-tuple-element.48), channel_id=1, source_target_pairs={{0,448},{16,464},{32,480},{48,496},{64,0},{80,16},{96,32},{112,48}... | collective-permute-start | bytes 589832 | tf_op jit(solution)/shard_map/cond/branch_2_fun/ppermute | solution.py:24
  267.3 11.7 %collective-permute-start.4 = (bf16[384,256]{1,0:T(8,128)(2,1)S(1)}, bf16[384,256]{1,0:T(8,128)(2,1)S(1)}, u32[]{:S(2)}, u32[]{:S(2)}) collective-permute-start(bf16[384,256]{1,0:T(8,128)(2,1)S(1)} %get-tuple-element.48), channel_id=1, source_target_pairs={{0,64},{16,80},{32,96},{48,112},{64,128},{80,144},{96,160},{112,17... | collective-permute-start | bytes 589832 | tf_op jit(solution)/shard_map/cond/branch_2_fun/ppermute | solution.py:24
  279.1 7.5 %collective-permute-done.5 = bf16[384,256]{1,0:T(8,128)(2,1)S(1)} collective-permute-done((bf16[384,256]{1,0:T(8,128)(2,1)S(1)}, bf16[384,256]{1,0:T(8,128)(2,1)S(1)}, u32[]{:S(2)}, u32[]{:S(2)}) %collective-permute-start.5) | collective-permute-done | bytes 196640 | tf_op jit(solution)/shard_map/cond/branch_2_fun/ppermute | solution.py:24
  286.6 0.7 copy-done.5
  (39 shorter events, 1.6 us)
Async XLA Ops:
  0.6 63.6 %copy-start = (bf16[1,256,6144]{2,1,0:T(8,128)(2,1)S(1)}, bf16[1,256,6144]{2,1,0:T(8,128)(2,1)}, u32[]{:S(2)}) copy-start(bf16[1,256,6144]{2,1,0:T(8,128)(2,1)} %param.10) | copy-start | bytes 9437188
  0.6 13.4 %copy-start.8 = (bf16[1,384,256]{2,1,0:T(8,128)(2,1)S(1)}, bf16[1,384,256]{2,1,0:T(8,128)(2,1)}, u32[]{:S(2)}) copy-start(bf16[1,384,256]{2,1,0:T(8,128)(2,1)} %param.13) | copy-start | bytes 589828
  3.0 31.7 %all-to-all-start = ((bf16[8,384,256]{2,1,0:T(8,128)(2,1)}), bf16[8,384,256]{2,1,0:T(8,128)(2,1)}, u32[]{:S(2)}, u32[]{:S(2)}) async-start(bf16[8,384,256]{2,1,0:T(8,128)(2,1)} %broadcast_in_dim.61), calls=%async_computation | async-start | bytes 3145728 | tf_op jit(solution)/shard_map/all_to_all | solution.py:40
  14.0 16.9 %collective-permute-start.8 = (bf16[384,256]{1,0:T(8,128)(2,1)S(1)}, bf16[384,256]{1,0:T(8,128)(2,1)S(1)}, u32[]{:S(2)}, u32[]{:S(2)}) collective-permute-start(bf16[384,256]{1,0:T(8,128)(2,1)S(1)} %bitcast.112), channel_id=1, source_target_pairs={{0,8},{8,0},{1,9},{9,1},{2,10},{10,2},{3,11},{11,3},{4,12},{12,4},... | collective-permute-start | bytes 589832 | tf_op jit(solution)/shard_map/ppermute | solution.py:34
  36.0 25.8 %all-to-all-start.1 = ((bf16[8,384,256]{2,1,0:T(8,128)(2,1)}), bf16[8,384,256]{2,1,0:T(8,128)(2,1)}, u32[]{:S(2)}, u32[]{:S(2)}) async-start(bf16[8,384,256]{2,1,0:T(8,128)(2,1)} %broadcast_in_dim.62), calls=%async_computation.1 | async-start | bytes 3145728 | tf_op jit(solution)/shard_map/all_to_all | solution.py:40
  66.4 21.8 %all-to-all-start.2 = ((bf16[8,256,256]{2,1,0:T(8,128)(2,1)}), bf16[8,256,256]{2,1,0:T(8,128)(2,1)}, u32[]{:S(2)}, u32[]{:S(2)}) async-start(bf16[8,256,256]{2,1,0:T(8,128)(2,1)} %broadcast_in_dim.63), calls=%async_computation.2 | async-start | bytes 2097152 | tf_op jit(solution)/shard_map/all_to_all | solution.py:40
  71.5 23.3 %copy-start.9 = (s32[64,3]{0,1:T(4,128)S(1)}, s32[64,3]{0,1:T(4,128)}, u32[]{:S(2)}) copy-start(s32[64,3]{0,1:T(4,128)} %param.14) | copy-start | bytes 2308
  71.5 23.9 %copy-start.7 = (bf16[1,256,128]{2,1,0:T(8,128)(2,1)S(1)}, bf16[1,256,128]{2,1,0:T(8,128)(2,1)}, u32[]{:S(2)}) copy-start(bf16[1,256,128]{2,1,0:T(8,128)(2,1)} %param.12) | copy-start | bytes 196612
  71.5 15.7 %collective-permute-start.9 = (bf16[256,256]{0,1:T(8,128)(2,1)S(1)}, bf16[256,256]{0,1:T(8,128)(2,1)}, u32[]{:S(2)}, u32[]{:S(2)}) collective-permute-start(bf16[256,256]{0,1:T(8,128)(2,1)S(1)} %fusion.17), channel_id=1, source_target_pairs={{0,8},{8,0},{1,9},{9,1},{2,10},{10,2},{3,11},{11,3},{4,12},{12,4},... | collective-permute-start | bytes 393224 | tf_op jit(solution)/shard_map/ppermute | solution.py:34
  89.3 20.5 %all-to-all-start.3 = ((bf16[8,256,256]{2,1,0:T(8,128)(2,1)}), bf16[8,256,256]{2,1,0:T(8,128)(2,1)}, u32[]{:S(2)}, u32[]{:S(2)}) async-start(bf16[8,256,256]{2,1,0:T(8,128)(2,1)} %broadcast_in_dim.64), calls=%async_computation.3 | async-start | bytes 2097152 | tf_op jit(solution)/shard_map/all_to_all | solution.py:40
  111.5 0.8 copy-start.6
  111.7 2.7 copy-start.3
  115.2 1.7 copy-start.4
  116.1 2.0 copy-start.1
  116.9 1.3 copy-start.2
  118.2 4.8 %collective-permute-start.11 = (bf16[4,256,256]{1,2,0:T(8,128)(2,1)}, bf16[4,256,256]{1,2,0:T(8,128)(2,1)}, u32[]{:S(2)}, u32[]{:S(2)}) collective-permute-start(bf16[4,256,256]{1,2,0:T(8,128)(2,1)} %get-tuple-element.60), channel_id=1, source_target_pairs={{0,1},{1,0},{2,3},{3,2},{4,5},{5,4},{6,7},{7,6},{8,9},{9,8},{10,11... | collective-permute-start | bytes 1572872 | tf_op jit(solution)/shard_map/ppermute | solution.py:57
  121.1 4.1 %collective-permute-start.10 = (bf16[4,256,256]{1,2,0:T(8,128)(2,1)}, bf16[4,256,256]{1,2,0:T(8,128)(2,1)}, u32[]{:S(2)}, u32[]{:S(2)}) collective-permute-start(bf16[4,256,256]{1,2,0:T(8,128)(2,1)} %get-tuple-element.61), channel_id=1, source_target_pairs={{0,1},{1,0},{2,3},{3,2},{4,5},{5,4},{6,7},{7,6},{8,9},{9,8},{10,11... | collective-permute-start | bytes 1572872 | tf_op jit(solution)/shard_map/ppermute | solution.py:57
  140.1 15.9 %all-to-all-start.4 = ((bf16[4,256,256]{1,2,0:T(8,128)(2,1)}), bf16[4,256,256]{1,2,0:T(8,128)(2,1)}, u32[]{:S(2)}, u32[]{:S(2)}) async-start(bf16[4,256,256]{1,2,0:T(8,128)(2,1)} %get-tuple-element.59), calls=%async_computation.4 | async-start | bytes 1048576 | tf_op jit(solution)/shard_map/all_to_all | solution.py:59
  145.4 14.4 %collective-permute-start.12 = (bf16[256,256]{0,1:T(8,128)(2,1)S(1)}, bf16[256,256]{0,1:T(8,128)(2,1)S(1)}, u32[]{:S(2)}, u32[]{:S(2)}) collective-permute-start(bf16[256,256]{0,1:T(8,128)(2,1)S(1)} %reduce_sum.82), channel_id=1, source_target_pairs={{0,8},{8,0},{1,9},{9,1},{2,10},{10,2},{3,11},{11,3},{4,12},{12,4},... | collective-permute-start | bytes 393224 | tf_op jit(solution)/shard_map/ppermute | solution.py:34
  184.6 15.5 %collective-permute-start.14 = (bf16[4,384,256]{2,1,0:T(8,128)(2,1)}, bf16[4,384,256]{2,1,0:T(8,128)(2,1)}, u32[]{:S(2)}, u32[]{:S(2)}) collective-permute-start(bf16[4,384,256]{2,1,0:T(8,128)(2,1)} %bitcast.110), channel_id=1, source_target_pairs={{0,1},{1,0},{2,3},{3,2},{4,5},{5,4},{6,7},{7,6},{8,9},{9,8},{10,11... | collective-permute-start | bytes 2359304 | tf_op jit(solution)/shard_map/ppermute | solution.py:57
  193.5 18.1 %collective-permute-start.13 = (bf16[4,384,256]{2,1,0:T(8,128)(2,1)}, bf16[4,384,256]{2,1,0:T(8,128)(2,1)}, u32[]{:S(2)}, u32[]{:S(2)}) collective-permute-start(bf16[4,384,256]{2,1,0:T(8,128)(2,1)} %bitcast.109), channel_id=1, source_target_pairs={{0,1},{1,0},{2,3},{3,2},{4,5},{5,4},{6,7},{7,6},{8,9},{9,8},{10,11... | collective-permute-start | bytes 2359304 | tf_op jit(solution)/shard_map/ppermute | solution.py:57
  202.5 16.2 %all-to-all-start.7 = ((bf16[4,384,256]{2,1,0:T(8,128)(2,1)}), bf16[4,384,256]{2,1,0:T(8,128)(2,1)}, u32[]{:S(2)}, u32[]{:S(2)}) async-start(bf16[4,384,256]{2,1,0:T(8,128)(2,1)} %fusion.12), calls=%async_computation.7 | async-start | bytes 1572864 | tf_op jit(solution)/shard_map/all_to_all | solution.py:59
  218.8 19.9 %all-to-all-start.6 = ((bf16[4,384,256]{2,1,0:T(8,128)(2,1)}), bf16[4,384,256]{2,1,0:T(8,128)(2,1)}, u32[]{:S(2)}, u32[]{:S(2)}) async-start(bf16[4,384,256]{2,1,0:T(8,128)(2,1)} %fusion.13), calls=%async_computation.6 | async-start | bytes 1572864 | tf_op jit(solution)/shard_map/all_to_all | solution.py:59
  224.9 16.2 %collective-permute-start.15 = (bf16[384,256]{1,0:T(8,128)(2,1)S(1)}, bf16[384,256]{1,0:T(8,128)(2,1)}, u32[]{:S(2)}, u32[]{:S(2)}) collective-permute-start(bf16[384,256]{1,0:T(8,128)(2,1)S(1)} %reduce_sum.83), channel_id=1, source_target_pairs={{0,8},{8,0},{1,9},{9,1},{2,10},{10,2},{3,11},{11,3},{4,12},{12,4},... | collective-permute-start | bytes 589832 | tf_op jit(solution)/shard_map/ppermute | solution.py:34
  245.4 41.1 %collective-permute-start.5 = (bf16[384,256]{1,0:T(8,128)(2,1)S(1)}, bf16[384,256]{1,0:T(8,128)(2,1)S(1)}, u32[]{:S(2)}, u32[]{:S(2)}) collective-permute-start(bf16[384,256]{1,0:T(8,128)(2,1)S(1)} %get-tuple-element.48), channel_id=1, source_target_pairs={{0,448},{16,464},{32,480},{48,496},{64,0},{80,16},{96,32},{112,48}... | collective-permute-start | bytes 589832 | tf_op jit(solution)/shard_map/cond/branch_2_fun/ppermute | solution.py:24
  267.3 19.2 %collective-permute-start.4 = (bf16[384,256]{1,0:T(8,128)(2,1)S(1)}, bf16[384,256]{1,0:T(8,128)(2,1)S(1)}, u32[]{:S(2)}, u32[]{:S(2)}) collective-permute-start(bf16[384,256]{1,0:T(8,128)(2,1)S(1)} %get-tuple-element.48), channel_id=1, source_target_pairs={{0,64},{16,80},{32,96},{48,112},{64,128},{80,144},{96,160},{112,17... | collective-permute-start | bytes 589832 | tf_op jit(solution)/shard_map/cond/branch_2_fun/ppermute | solution.py:24
  286.6 0.7 copy-start.5

commit v3 on v2

--- a/solution.py
+++ b/solution.py
@@ -50,25 +50,25 @@
     return jnp.concatenate([low, high]).reshape((-1,) + piece.shape[1:])
 
 
+def gather_other_first(piece):
+    from_other = swap_zh(piece)
+    own_half = spread_half(piece)
+    other_half = spread_half(from_other)
+    return jnp.concatenate([other_half, own_half]).reshape((-1,) + piece.shape[1:])
+
+
 def reduce_half(part):
-    core = lax.axis_index("c")
-    keep = lax.dynamic_index_in_dim(part, core, 1, keepdims=False)
-    send = lax.dynamic_index_in_dim(part, 1 - core, 1, keepdims=False)
-    got = lax.ppermute(send, "c", [(0, 1), (1, 0)])
-    summed = (keep.astype(jnp.float32) + got.astype(jnp.float32)).astype(jnp.bfloat16)
+    paired = lax.all_to_all(part, "c", 1, 1, tiled=False)
+    summed = jnp.sum(paired.astype(jnp.float32), axis=1).astype(jnp.bfloat16)
     spread = lax.all_to_all(summed, "y", 0, 0, tiled=False)
     return jnp.sum(spread.astype(jnp.float32), axis=0)
 
 
-def scatter_seq(whole):
-    zh_n, y_n, c_n = (lax.axis_size(name) for name in SEQ_AXES)
-    rows = whole.shape[0] // (zh_n * y_n * c_n)
-    parts = whole.reshape((zh_n, y_n, c_n, rows) + whole.shape[1:])
-    mine = lax.axis_index("zh")
-    for_other = reduce_half(lax.dynamic_index_in_dim(parts, 1 - mine, 0, keepdims=False))
-    got = swap_zh(for_other.astype(jnp.bfloat16))
-    for_me = reduce_half(lax.dynamic_index_in_dim(parts, mine, 0, keepdims=False))
-    return for_me + got.astype(jnp.float32)
+def scatter_halves(for_other, for_me):
+    y_n, c_n = lax.axis_size("y"), lax.axis_size("c")
+    shape = (y_n, c_n, for_other.shape[0] // (y_n * c_n)) + for_other.shape[1:]
+    got = swap_zh(reduce_half(for_other.reshape(shape)).astype(jnp.bfloat16))
+    return reduce_half(for_me.reshape(shape)) + got.astype(jnp.float32)
 
 
 def fold_rows(tok_rows, row_piece):
@@ -123,14 +123,16 @@
     head_size = kv_width // 2
     blk_size = BLOCK
     blocks_dev = tok_count // blk_size
-    block_count = blocks_dev * seq_count
     inv_root = head_size ** (-0.5)
     kv_here = fold_rows(tokens_here, gather_seq(weight_here)).astype(jnp.bfloat16)
-    kv_all = gather_seq(kv_here)
+    kv_all = gather_other_first(kv_here)
     keys_all = kv_all[:, :head_size]
     values_all = kv_all[:, head_size:]
+    half_n = seq_count // 2
+    my_half = lax.axis_index("zh")
+    order = jnp.concatenate([(1 - my_half) * half_n + jnp.arange(half_n), my_half * half_n + jnp.arange(half_n)])
+    every_block = (order[:, None] * blocks_dev + jnp.arange(blocks_dev)[None, :]).reshape(-1).astype(jnp.int32)
     blocks_here = seq_index * blocks_dev + jnp.arange(blocks_dev, dtype=jnp.int32)
-    every_block = jnp.arange(block_count, dtype=jnp.int32)
     chosen_here = lax.dynamic_slice_in_dim(rand_blocks, seq_index * blocks_dev, blocks_dev, 0)
     allowed = attend_mask(blocks_here, every_block, chosen_here, blk_size)
     scores = contract_cols(query_here, keys_all) * inv_root
@@ -147,9 +149,16 @@
     )
     key_terms = contract_rows(score_grad, query_here)
     value_terms = contract_rows(prob_low, grad_here)
-    grad_terms = jnp.concatenate([key_terms, value_terms], axis=1)
-    kv_grad = scatter_seq(grad_terms.astype(jnp.bfloat16)).astype(jnp.bfloat16)
-    grad_slice = scatter_seq(contract_rows(tokens_here, kv_grad).astype(jnp.bfloat16))
+    grad_terms = jnp.concatenate([key_terms, value_terms], axis=1).astype(jnp.bfloat16)
+    half_rows = grad_terms.shape[0] // 2
+    kv_grad = scatter_halves(grad_terms[:half_rows], grad_terms[half_rows:]).astype(jnp.bfloat16)
+    tok_view = tokens_here.reshape(tok_count, 2, -1)
+    tok_other = lax.dynamic_index_in_dim(tok_view, 1 - my_half, 1, keepdims=False)
+    tok_mine = lax.dynamic_index_in_dim(tok_view, my_half, 1, keepdims=False)
+    grad_slice = scatter_halves(
+        contract_rows(tok_other, kv_grad).astype(jnp.bfloat16),
+        contract_rows(tok_mine, kv_grad).astype(jnp.bfloat16),
+    )
     branches = [
         partial(gossip, distance=(1 << level_idx) % rep_count, rep_count=rep_count)
         for level_idx in range(4)

time: 290 us -> 264 us (0.910)
  local copies, waits for them, and re-layouts: 45 us -> 19.4 us
  other arithmetic: 23.7 us -> 12.5 us
  waiting for transfers between devices: 67.5 us -> 75 us
  starting transfers between devices: 126 us -> 131 us
    dynamic_slice x2 -> x0, local copies, waits for them, and re-layouts: 14.1 us -> none  [the longest x1 9.42 us: reduce_half(): keep = lax.dynamic_index_in_dim(part, core, 1, keepdims=False)]
    all_to_all x3 -> x4, waiting for transfers between devices: 4.62 us -> 17.7 us  [reduce_half(): spread = lax.all_to_all(summed, 'y', 0, 0, tiled=False)]
    ppermute x4 -> x0, starting transfers between devices: 11 us -> none  [reduce_half(): got = lax.ppermute(send, 'c', [(0, 1), (1, 0)])]
    all_to_all x0 -> x2, starting transfers between devices: none -> 10.7 us  [reduce_half(): paired = lax.all_to_all(part, 'c', 1, 1, tiled=False)]
    unnamed x24, local copies, waits for them, and re-layouts: 15.3 us -> 6.13 us
    convert_element_type x4 -> x1, other arithmetic: 8.41 us -> 0.03 us  [scatter_halves(): return reduce_half(for_me.reshape(shape)) + got.astype(jnp.float32)]
    reduce_sum x0 -> x4, other arithmetic: none -> 6.39 us  [reduce_half(): summed = jnp.sum(paired.astype(jnp.float32), axis=1).astype(jnp.bfloat16)]
    all_to_all x3 -> x4, starting transfers between devices: 12.8 us -> 16.4 us  [reduce_half(): spread = lax.all_to_all(summed, 'y', 0, 0, tiled=False)]
  transfers between devices with their start and end apart: 17 -> 16, of which waited for: 9 -> 11; matrix products, arithmetic and copies ran while one was open for 10% -> 8% of each run, Pallas kernels for 0% -> 0%
where the time goes in v3:
time: 264 us; the launch traced here: 261 us
  starting transfers between devices  131 us (50%)
  waiting for transfers between devices  75 us (28%)
  local copies, waits for them, and re-layouts  19.4 us (7%)
  other arithmetic  12.5 us (5%)
  matrix products  11.1 us (4%)
  blocking collectives  9.75 us (4%)
    ppermute x4, starting transfers between devices, swap_zh(): return lax.ppermute(value, 'zh', [(0, 1), (1, 0)])  44.4 us
    all_to_all x4, waiting for transfers between devices, spread_half(): return lax.all_to_all(copies, ('y', 'c'), 0, 0, tiled=False)  38.3 us
    ppermute x2, starting transfers between devices, shifted(): return lax.ppermute(value, axis, pairs)  35.3 us
    all_to_all x4, starting transfers between devices, spread_half(): return lax.all_to_all(copies, ('y', 'c'), 0, 0, tiled=False)  24.6 us
    all_to_all x4, waiting for transfers between devices, reduce_half(): spread = lax.all_to_all(summed, 'y', 0, 0, tiled=False)  17.7 us
    all_to_all x4, starting transfers between devices, reduce_half(): spread = lax.all_to_all(summed, 'y', 0, 0, tiled=False)  16.4 us
    ppermute x4, waiting for transfers between devices, swap_zh(): return lax.ppermute(value, 'zh', [(0, 1), (1, 0)])  13.3 us
    all_to_all x2, starting transfers between devices, reduce_half(): paired = lax.all_to_all(part, 'c', 1, 1, tiled=False)  10.7 us
  transfers between devices with their start and end apart: 16, of which 11 were waited for; matrix products, arithmetic and copies ran while one was open for 8% of the time, Pallas kernels for 0%

profile of v3, /device:TPU:1, one launch (start us, length us, event | category | flops | bytes accessed | tf_op | source)
XLA Modules:
  0.0 261.1 jit_solution(2579036588017752001)
XLA Ops:
  0.7 2.2 broadcast_in_dim.60
  2.9 10.3 %all-to-all-start = ((bf16[8,384,256]{2,1,0:T(8,128)(2,1)}), bf16[8,384,256]{2,1,0:T(8,128)(2,1)S(1)}, u32[]{:S(2)}, u32[]{:S(2)}) async-start(bf16[8,384,256]{2,1,0:T(8,128)(2,1)} %broadcast_in_dim.60), calls=%async_computation | async-start | bytes 3145728 | tf_op jit(solution)/shard_map/all_to_all | solution.py:40
  13.2 11.1 %collective-permute-start.8 = (bf16[384,256]{1,0:T(8,128)(2,1)S(1)}, bf16[384,256]{1,0:T(8,128)(2,1)S(1)}, u32[]{:S(2)}, u32[]{:S(2)}) collective-permute-start(bf16[384,256]{1,0:T(8,128)(2,1)S(1)} %bitcast.87), channel_id=1, source_target_pairs={{0,8},{8,0},{1,9},{9,1},{2,10},{10,2},{3,11},{11,3},{4,12},{12,4},... | collective-permute-start | bytes 589832 | tf_op jit(solution)/shard_map/ppermute | solution.py:34
  24.3 5.9 %collective-permute-done.8 = bf16[384,256]{1,0:T(8,128)(2,1)S(1)} collective-permute-done((bf16[384,256]{1,0:T(8,128)(2,1)S(1)}, bf16[384,256]{1,0:T(8,128)(2,1)S(1)}, u32[]{:S(2)}, u32[]{:S(2)}) %collective-permute-start.8) | collective-permute-done | bytes 196640 | tf_op jit(solution)/shard_map/ppermute | solution.py:34
  30.2 3.7 %all-to-all-done = bf16[8,384,256]{2,1,0:T(8,128)(2,1)S(1)} async-done(((bf16[8,384,256]{2,1,0:T(8,128)(2,1)}), bf16[8,384,256]{2,1,0:T(8,128)(2,1)S(1)}, u32[]{:S(2)}, u32[]{:S(2)}) %all-to-all-start) | async-done | bytes 1572896 | tf_op jit(solution)/shard_map/all_to_all | solution.py:40
  33.8 1.3 broadcast_in_dim.61
  35.1 4.4 %all-to-all-start.1 = ((bf16[8,384,256]{2,1,0:T(8,128)(2,1)}), bf16[8,384,256]{2,1,0:T(8,128)(2,1)S(1)}, u32[]{:S(2)}, u32[]{:S(2)}) async-start(bf16[8,384,256]{2,1,0:T(8,128)(2,1)} %broadcast_in_dim.61), calls=%async_computation.1 | async-start | bytes 3145728 | tf_op jit(solution)/shard_map/all_to_all | solution.py:40
  39.5 20.6 %all-to-all-done.1 = bf16[8,384,256]{2,1,0:T(8,128)(2,1)S(1)} async-done(((bf16[8,384,256]{2,1,0:T(8,128)(2,1)}), bf16[8,384,256]{2,1,0:T(8,128)(2,1)S(1)}, u32[]{:S(2)}, u32[]{:S(2)}) %all-to-all-start.1) | async-done | bytes 1572896 | tf_op jit(solution)/shard_map/all_to_all | solution.py:40
  60.7 1.6 copy-done.4
  62.3 1.0 fusion.17
  63.4 1.0 broadcast_in_dim.63
  64.4 4.4 %all-to-all-start.3 = ((bf16[8,256,256]{2,1,0:T(8,128)(2,1)}), bf16[8,256,256]{2,1,0:T(8,128)(2,1)S(1)}, u32[]{:S(2)}, u32[]{:S(2)}) async-start(bf16[8,256,256]{2,1,0:T(8,128)(2,1)} %broadcast_in_dim.63), calls=%async_computation.3 | async-start | bytes 2097152 | tf_op jit(solution)/shard_map/all_to_all | solution.py:40
  68.9 11.2 %collective-permute-start.9 = (bf16[256,256]{0,1:T(8,128)(2,1)S(1)}, bf16[256,256]{0,1:T(8,128)(2,1)S(1)}, u32[]{:S(2)}, u32[]{:S(2)}) collective-permute-start(bf16[256,256]{0,1:T(8,128)(2,1)S(1)} %fusion.17), channel_id=1, source_target_pairs={{0,8},{8,0},{1,9},{9,1},{2,10},{10,2},{3,11},{11,3},{4,12},{12,4},... | collective-permute-start | bytes 393224 | tf_op jit(solution)/shard_map/ppermute | solution.py:34
  80.1 4.4 %collective-permute-done.9 = bf16[256,256]{0,1:T(8,128)(2,1)S(1)} collective-permute-done((bf16[256,256]{0,1:T(8,128)(2,1)S(1)}, bf16[256,256]{0,1:T(8,128)(2,1)S(1)}, u32[]{:S(2)}, u32[]{:S(2)}) %collective-permute-start.9) | collective-permute-done | bytes 131104 | tf_op jit(solution)/shard_map/ppermute | solution.py:34
  84.6 1.0 broadcast_in_dim.62
  85.7 5.4 %all-to-all-start.2 = ((bf16[8,256,256]{2,1,0:T(8,128)(2,1)}), bf16[8,256,256]{2,1,0:T(8,128)(2,1)S(1)}, u32[]{:S(2)}, u32[]{:S(2)}) async-start(bf16[8,256,256]{2,1,0:T(8,128)(2,1)} %broadcast_in_dim.62), calls=%async_computation.2 | async-start | bytes 2097152 | tf_op jit(solution)/shard_map/all_to_all | solution.py:40
  92.0 14.0 %all-to-all-done.2 = bf16[8,256,256]{2,1,0:T(8,128)(2,1)S(1)} async-done(((bf16[8,256,256]{2,1,0:T(8,128)(2,1)}), bf16[8,256,256]{2,1,0:T(8,128)(2,1)S(1)}, u32[]{:S(2)}, u32[]{:S(2)}) %all-to-all-start.2) | async-done | bytes 1048608 | tf_op jit(solution)/shard_map/all_to_all | solution.py:40
  106.3 0.3 broadcast_in_dim.58
  106.5 1.2 fusion.39
  107.7 0.3 fusion.9
  108.1 0.8 convolution_convert_fusion
  108.9 0.6 fusion.20
  109.5 0.8 fusion.6
  110.3 0.8 convolution_convert_fusion.1
  111.3 0.3 copy-done.5
  111.6 0.8 reshape.95
  112.4 0.4 copy.63
  112.8 5.2 %all_to_all.60 = bf16[4,2,256,256]{2,0,3,1:T(4,128)(2,1)S(1)} all-to-all(bf16[4,2,256,256]{2,0,3,1:T(4,128)(2,1)S(1)} %copy.63), channel_id=1, replica_groups=mesh['rep'=32,'zh'=2,'y'=4,'c'=2] {'c'}, dimensions={1} | all-to-all | bytes 2097152 | tf_op jit(solution)/shard_map/all_to_all | solution.py:61
  118.0 1.1 reduce_sum.131
  119.1 0.9 copy.65
  120.0 0.8 reshape.94
  120.7 0.4 copy.59
  121.2 4.6 %all_to_all.61 = bf16[4,2,256,256]{2,0,3,1:T(4,128)(2,1)S(1)} all-to-all(bf16[4,2,256,256]{2,0,3,1:T(4,128)(2,1)S(1)} %copy.59), channel_id=1, replica_groups=mesh['rep'=32,'zh'=2,'y'=4,'c'=2] {'c'}, dimensions={1} | all-to-all | bytes 2097152 | tf_op jit(solution)/shard_map/all_to_all | solution.py:61
  125.7 3.6 %all-to-all-start.7 = ((bf16[4,256,256]{1,2,0:T(8,128)(2,1)}), bf16[4,256,256]{1,2,0:T(8,128)(2,1)S(1)}, u32[]{:S(2)}, u32[]{:S(2)}) async-start(bf16[4,256,256]{1,2,0:T(8,128)(2,1)} %copy.65), calls=%async_computation.7 | async-start | bytes 1048576 | tf_op jit(solution)/shard_map/all_to_all | solution.py:63
  129.4 1.1 reduce_sum.129
  130.5 0.9 copy.61
  131.4 7.0 %all-to-all-done.7 = bf16[4,256,256]{1,2,0:T(8,128)(2,1)S(1)} async-done(((bf16[4,256,256]{1,2,0:T(8,128)(2,1)}), bf16[4,256,256]{1,2,0:T(8,128)(2,1)S(1)}, u32[]{:S(2)}, u32[]{:S(2)}) %all-to-all-start.7) | async-done | bytes 524320 | tf_op jit(solution)/shard_map/all_to_all | solution.py:63
  138.4 4.1 %all-to-all-start.5 = ((bf16[4,256,256]{1,2,0:T(8,128)(2,1)}), bf16[4,256,256]{1,2,0:T(8,128)(2,1)}, u32[]{:S(2)}, u32[]{:S(2)}) async-start(bf16[4,256,256]{1,2,0:T(8,128)(2,1)} %copy.61), calls=%async_computation.5 | async-start | bytes 1048576 | tf_op jit(solution)/shard_map/all_to_all | solution.py:63
  142.5 3.2 %copy.53 = bf16[1,256,6144]{1,2,0:T(8,128)(2,1)S(1)} copy(bf16[1,256,6144]{2,1,0:T(8,128)(2,1)} %param.10) | data formatting | bytes 6291456 | tf_op args[0]
  145.7 1.8 reduce_sum.132
  147.5 11.1 %collective-permute-start.10 = (bf16[256,256]{0,1:T(8,128)(2,1)}, bf16[256,256]{0,1:T(8,128)(2,1)}, u32[]{:S(2)}, u32[]{:S(2)}) collective-permute-start(bf16[256,256]{0,1:T(8,128)(2,1)} %reduce_sum.132), channel_id=1, source_target_pairs={{0,8},{8,0},{1,9},{9,1},{2,10},{10,2},{3,11},{11,3},{4,12},{12,4},... | collective-permute-start | bytes 393224 | tf_op jit(solution)/shard_map/ppermute | solution.py:34
  158.6 1.1 convert_reduce_fusion
  159.8 2.5 collective-permute-done.10
  162.3 1.5 convolution_convert_fusion.2
  163.8 1.4 copy.69
  165.1 7.0 %all-to-all-start.10 = ((bf16[4,2,384,256]{3,2,0,1:T(8,128)(2,1)}), bf16[4,2,384,256]{3,2,0,1:T(8,128)(2,1)}, u32[]{:S(2)}, u32[]{:S(2)}) async-start(bf16[4,2,384,256]{3,2,0,1:T(8,128)(2,1)} %copy.69), calls=%async_computation.10 | async-start | bytes 3145728 | tf_op jit(solution)/shard_map/all_to_all | solution.py:61
  172.1 1.5 convolution_convert_fusion.3
  173.6 1.3 copy.67
  174.9 3.7 %all-to-all-start.8 = ((bf16[4,2,384,256]{3,2,0,1:T(8,128)(2,1)}), bf16[4,2,384,256]{3,2,0,1:T(8,128)(2,1)S(1)}, u32[]{:S(2)}, u32[]{:S(2)}) async-start(bf16[4,2,384,256]{3,2,0,1:T(8,128)(2,1)} %copy.67), calls=%async_computation.8 | async-start | bytes 3145728 | tf_op jit(solution)/shard_map/all_to_all | solution.py:61
  178.6 2.8 %reduce_sum.134 = bf16[4,384,256]{2,1,0:T(8,128)(2,1)} reduce(bf16[4,2,384,256]{3,2,0,1:T(8,128)(2,1)} %all-to-all-done.10, bf16[]{:T(256)} %constant.72.clone.1), dimensions={1}, to_apply=%region_8.9 | reduce | flops 393216 | bytes 2359298 | tf_op jit(solution)/shard_map/reduce_sum | solution.py:62
  181.3 4.5 %all-to-all-start.11 = ((bf16[4,384,256]{2,1,0:T(8,128)(2,1)}), bf16[4,384,256]{2,1,0:T(8,128)(2,1)S(1)}, u32[]{:S(2)}, u32[]{:S(2)}) async-start(bf16[4,384,256]{2,1,0:T(8,128)(2,1)} %reduce_sum.134), calls=%async_computation.11 | async-start | bytes 1572864 | tf_op jit(solution)/shard_map/all_to_all | solution.py:63
  185.8 1.4 reduce_sum.133
  187.2 10.7 %all-to-all-done.11 = bf16[4,384,256]{2,1,0:T(8,128)(2,1)S(1)} async-done(((bf16[4,384,256]{2,1,0:T(8,128)(2,1)}), bf16[4,384,256]{2,1,0:T(8,128)(2,1)S(1)}, u32[]{:S(2)}, u32[]{:S(2)}) %all-to-all-start.11) | async-done | bytes 786464 | tf_op jit(solution)/shard_map/all_to_all | solution.py:63
  197.9 4.2 %all-to-all-start.9 = ((bf16[4,384,256]{2,1,0:T(8,128)(2,1)}), bf16[4,384,256]{2,1,0:T(8,128)(2,1)}, u32[]{:S(2)}, u32[]{:S(2)}) async-start(bf16[4,384,256]{2,1,0:T(8,128)(2,1)} %reduce_sum.133), calls=%async_computation.9 | async-start | bytes 1572864 | tf_op jit(solution)/shard_map/all_to_all | solution.py:63
  202.9 11.1 %collective-permute-start.11 = (bf16[384,256]{1,0:T(8,128)(2,1)S(1)}, bf16[384,256]{1,0:T(8,128)(2,1)S(1)}, u32[]{:S(2)}, u32[]{:S(2)}) collective-permute-start(bf16[384,256]{1,0:T(8,128)(2,1)S(1)} %reduce_sum.135), channel_id=1, source_target_pairs={{0,8},{8,0},{1,9},{9,1},{2,10},{10,2},{3,11},{11,3},{4,12},{12,4},... | collective-permute-start | bytes 589832 | tf_op jit(solution)/shard_map/ppermute | solution.py:34
  214.0 3.0 %fusion.21 = bf16[1,256,128]{2,1,0:T(8,128)(2,1)} fusion(bf16[256,4096]{0,1:T(8,128)(2,1)} %copy-done.5, bf16[4096,256]{1,0:T(8,128)(2,1)S(1)} %bitcast.83), kind=kOutput, calls=%fused_computation.36 | convolution fusion | flops 268468224 | bytes 3211264 | tf_op jit(solution)/shard_map/dot_general | solution.py:147
  217.0 1.3 convert_element_type.101
  218.3 0.6 collective-permute-done.11
  218.8 41.4 %conditional.1 = (f32[1,384,256]{2,1,0:T(8,128)S(1)}) conditional(s32[]{:T(128)} %clamp.3, (f32[4,384,256]{2,1,0:T(8,128)S(1)}, f32[384,256]{1,0:T(8,128)S(1)}) %tuple.28, (f32[4,384,256]{2,1,0:T(8,128)S(1)}, f32[384,256]{1,0:T(8,128)S(1)}) %tuple.28, (f32[4,384,256]{2,1,0:T(8,128)S(1)}, ...), branch_computations={%region_10.12_spmd, %region_12.14_spmd, %region_14.16_spmd, %regio... | conditional | flops 983040 | bytes 6094940 | solution.py:166
  219.1 33.4 %collective-permute-start.4 = (bf16[384,256]{1,0:T(8,128)(2,1)S(1)}, bf16[384,256]{1,0:T(8,128)(2,1)S(1)}, u32[]{:S(2)}, u32[]{:S(2)}) collective-permute-start(bf16[384,256]{1,0:T(8,128)(2,1)S(1)} %get-tuple-element.48), channel_id=1, source_target_pairs={{0,64},{16,80},{32,96},{48,112},{64,128},{80,144},{96,160},{112,17... | collective-permute-start | bytes 589832 | tf_op jit(solution)/shard_map/cond/branch_2_fun/ppermute | solution.py:24
  252.4 1.9 collective-permute-start.5
  254.4 1.5 collective-permute-done.4
  255.9 4.2 %collective-permute-done.5 = bf16[384,256]{1,0:T(8,128)(2,1)S(1)} collective-permute-done((bf16[384,256]{1,0:T(8,128)(2,1)S(1)}, bf16[384,256]{1,0:T(8,128)(2,1)S(1)}, u32[]{:S(2)}, u32[]{:S(2)}) %collective-permute-start.5) | collective-permute-done | bytes 196640 | tf_op jit(solution)/shard_map/cond/branch_2_fun/ppermute | solution.py:24
  260.2 0.7 copy-done.7
  (48 shorter events, 2.7 us)
Async XLA Ops:
  0.6 105.9 %copy-start = (bf16[1,256,128]{2,1,0:T(8,128)(2,1)S(1)}, bf16[1,256,128]{2,1,0:T(8,128)(2,1)}, u32[]{:S(2)}) copy-start(bf16[1,256,128]{2,1,0:T(8,128)(2,1)} %param.11) | copy-start | bytes 196612
  0.6 12.6 %copy-start.9 = (bf16[1,384,256]{2,1,0:T(8,128)(2,1)S(1)}, bf16[1,384,256]{2,1,0:T(8,128)(2,1)}, u32[]{:S(2)}) copy-start(bf16[1,384,256]{2,1,0:T(8,128)(2,1)} %param.13) | copy-start | bytes 589828
  2.9 30.9 %all-to-all-start = ((bf16[8,384,256]{2,1,0:T(8,128)(2,1)}), bf16[8,384,256]{2,1,0:T(8,128)(2,1)S(1)}, u32[]{:S(2)}, u32[]{:S(2)}) async-start(bf16[8,384,256]{2,1,0:T(8,128)(2,1)} %broadcast_in_dim.60), calls=%async_computation | async-start | bytes 3145728 | tf_op jit(solution)/shard_map/all_to_all | solution.py:40
  13.2 16.9 %collective-permute-start.8 = (bf16[384,256]{1,0:T(8,128)(2,1)S(1)}, bf16[384,256]{1,0:T(8,128)(2,1)S(1)}, u32[]{:S(2)}, u32[]{:S(2)}) collective-permute-start(bf16[384,256]{1,0:T(8,128)(2,1)S(1)} %bitcast.87), channel_id=1, source_target_pairs={{0,8},{8,0},{1,9},{9,1},{2,10},{10,2},{3,11},{11,3},{4,12},{12,4},... | collective-permute-start | bytes 589832 | tf_op jit(solution)/shard_map/ppermute | solution.py:34
  35.1 25.1 %all-to-all-start.1 = ((bf16[8,384,256]{2,1,0:T(8,128)(2,1)}), bf16[8,384,256]{2,1,0:T(8,128)(2,1)S(1)}, u32[]{:S(2)}, u32[]{:S(2)}) async-start(bf16[8,384,256]{2,1,0:T(8,128)(2,1)} %broadcast_in_dim.61), calls=%async_computation.1 | async-start | bytes 3145728 | tf_op jit(solution)/shard_map/all_to_all | solution.py:40
  60.4 1.9 copy-start.4
  64.4 20.2 %all-to-all-start.3 = ((bf16[8,256,256]{2,1,0:T(8,128)(2,1)}), bf16[8,256,256]{2,1,0:T(8,128)(2,1)S(1)}, u32[]{:S(2)}, u32[]{:S(2)}) async-start(bf16[8,256,256]{2,1,0:T(8,128)(2,1)} %broadcast_in_dim.63), calls=%async_computation.3 | async-start | bytes 2097152 | tf_op jit(solution)/shard_map/all_to_all | solution.py:40
  68.9 22.4 %copy-start.10 = (s32[64,3]{0,1:T(4,128)S(1)}, s32[64,3]{0,1:T(4,128)}, u32[]{:S(2)}) copy-start(s32[64,3]{0,1:T(4,128)} %param.14) | copy-start | bytes 2308
  68.9 23.0 %copy-start.8 = (bf16[1,256,128]{2,1,0:T(8,128)(2,1)S(1)}, bf16[1,256,128]{2,1,0:T(8,128)(2,1)}, u32[]{:S(2)}) copy-start(bf16[1,256,128]{2,1,0:T(8,128)(2,1)} %param.12) | copy-start | bytes 196612
  68.9 15.6 %collective-permute-start.9 = (bf16[256,256]{0,1:T(8,128)(2,1)S(1)}, bf16[256,256]{0,1:T(8,128)(2,1)S(1)}, u32[]{:S(2)}, u32[]{:S(2)}) collective-permute-start(bf16[256,256]{0,1:T(8,128)(2,1)S(1)} %fusion.17), channel_id=1, source_target_pairs={{0,8},{8,0},{1,9},{9,1},{2,10},{10,2},{3,11},{11,3},{4,12},{12,4},... | collective-permute-start | bytes 393224 | tf_op jit(solution)/shard_map/ppermute | solution.py:34
  85.7 20.4 %all-to-all-start.2 = ((bf16[8,256,256]{2,1,0:T(8,128)(2,1)}), bf16[8,256,256]{2,1,0:T(8,128)(2,1)S(1)}, u32[]{:S(2)}, u32[]{:S(2)}) async-start(bf16[8,256,256]{2,1,0:T(8,128)(2,1)} %broadcast_in_dim.62), calls=%async_computation.2 | async-start | bytes 2097152 | tf_op jit(solution)/shard_map/all_to_all | solution.py:40
  106.2 3.2 %copy-start.2 = (bf16[16,256,256]{2,1,0:T(8,128)(2,1)}, bf16[16,256,256]{2,1,0:T(8,128)(2,1)S(1)}, u32[]{:S(2)}) copy-start(bf16[16,256,256]{2,1,0:T(8,128)(2,1)S(1)} %pad_maximum_fusion.1) | copy-start | bytes 6291460
  110.3 1.3 copy-start.5
  125.7 12.6 %all-to-all-start.7 = ((bf16[4,256,256]{1,2,0:T(8,128)(2,1)}), bf16[4,256,256]{1,2,0:T(8,128)(2,1)S(1)}, u32[]{:S(2)}, u32[]{:S(2)}) async-start(bf16[4,256,256]{1,2,0:T(8,128)(2,1)} %copy.65), calls=%async_computation.7 | async-start | bytes 1048576 | tf_op jit(solution)/shard_map/all_to_all | solution.py:63
  138.4 4.2 %copy-start.6 = (bf16[4,256,256]{1,2,0:T(8,128)(2,1)}, bf16[4,256,256]{1,2,0:T(8,128)(2,1)S(1)}, u32[]{:S(2)}) copy-start(bf16[4,256,256]{1,2,0:T(8,128)(2,1)S(1)} %all-to-all-done.7) | copy-start | bytes 1572868
  138.4 20.2 %all-to-all-start.5 = ((bf16[4,256,256]{1,2,0:T(8,128)(2,1)}), bf16[4,256,256]{1,2,0:T(8,128)(2,1)}, u32[]{:S(2)}, u32[]{:S(2)}) async-start(bf16[4,256,256]{1,2,0:T(8,128)(2,1)} %copy.61), calls=%async_computation.5 | async-start | bytes 1048576 | tf_op jit(solution)/shard_map/all_to_all | solution.py:63
  147.5 14.7 %collective-permute-start.10 = (bf16[256,256]{0,1:T(8,128)(2,1)}, bf16[256,256]{0,1:T(8,128)(2,1)}, u32[]{:S(2)}, u32[]{:S(2)}) collective-permute-start(bf16[256,256]{0,1:T(8,128)(2,1)} %reduce_sum.132), channel_id=1, source_target_pairs={{0,8},{8,0},{1,9},{9,1},{2,10},{10,2},{3,11},{11,3},{4,12},{12,4},... | collective-permute-start | bytes 393224 | tf_op jit(solution)/shard_map/ppermute | solution.py:34
  165.1 9.8 %all-to-all-start.10 = ((bf16[4,2,384,256]{3,2,0,1:T(8,128)(2,1)}), bf16[4,2,384,256]{3,2,0,1:T(8,128)(2,1)}, u32[]{:S(2)}, u32[]{:S(2)}) async-start(bf16[4,2,384,256]{3,2,0,1:T(8,128)(2,1)} %copy.69), calls=%async_computation.10 | async-start | bytes 3145728 | tf_op jit(solution)/shard_map/all_to_all | solution.py:61
  174.9 6.5 %all-to-all-start.8 = ((bf16[4,2,384,256]{3,2,0,1:T(8,128)(2,1)}), bf16[4,2,384,256]{3,2,0,1:T(8,128)(2,1)S(1)}, u32[]{:S(2)}, u32[]{:S(2)}) async-start(bf16[4,2,384,256]{3,2,0,1:T(8,128)(2,1)} %copy.67), calls=%async_computation.8 | async-start | bytes 3145728 | tf_op jit(solution)/shard_map/all_to_all | solution.py:61
  181.3 16.5 %all-to-all-start.11 = ((bf16[4,384,256]{2,1,0:T(8,128)(2,1)}), bf16[4,384,256]{2,1,0:T(8,128)(2,1)S(1)}, u32[]{:S(2)}, u32[]{:S(2)}) async-start(bf16[4,384,256]{2,1,0:T(8,128)(2,1)} %reduce_sum.134), calls=%async_computation.11 | async-start | bytes 1572864 | tf_op jit(solution)/shard_map/all_to_all | solution.py:63
  187.2 26.8 %copy-start.3 = (bf16[16,256,256]{2,1,0:T(8,128)(2,1)S(1)}, bf16[16,256,256]{2,1,0:T(8,128)(2,1)}, u32[]{:S(2)}) copy-start(bf16[16,256,256]{2,1,0:T(8,128)(2,1)} %copy-done.2) | copy-start | bytes 6291460
  197.9 19.1 %all-to-all-start.9 = ((bf16[4,384,256]{2,1,0:T(8,128)(2,1)}), bf16[4,384,256]{2,1,0:T(8,128)(2,1)}, u32[]{:S(2)}, u32[]{:S(2)}) async-start(bf16[4,384,256]{2,1,0:T(8,128)(2,1)} %reduce_sum.133), calls=%async_computation.9 | async-start | bytes 1572864 | tf_op jit(solution)/shard_map/all_to_all | solution.py:63
  202.9 15.9 %collective-permute-start.11 = (bf16[384,256]{1,0:T(8,128)(2,1)S(1)}, bf16[384,256]{1,0:T(8,128)(2,1)S(1)}, u32[]{:S(2)}, u32[]{:S(2)}) collective-permute-start(bf16[384,256]{1,0:T(8,128)(2,1)S(1)} %reduce_sum.135), channel_id=1, source_target_pairs={{0,8},{8,0},{1,9},{9,1},{2,10},{10,2},{3,11},{11,3},{4,12},{12,4},... | collective-permute-start | bytes 589832 | tf_op jit(solution)/shard_map/ppermute | solution.py:34
  219.1 36.8 %collective-permute-start.4 = (bf16[384,256]{1,0:T(8,128)(2,1)S(1)}, bf16[384,256]{1,0:T(8,128)(2,1)S(1)}, u32[]{:S(2)}, u32[]{:S(2)}) collective-permute-start(bf16[384,256]{1,0:T(8,128)(2,1)S(1)} %get-tuple-element.48), channel_id=1, source_target_pairs={{0,64},{16,80},{32,96},{48,112},{64,128},{80,144},{96,160},{112,17... | collective-permute-start | bytes 589832 | tf_op jit(solution)/shard_map/cond/branch_2_fun/ppermute | solution.py:24
  252.4 7.7 %collective-permute-start.5 = (bf16[384,256]{1,0:T(8,128)(2,1)S(1)}, bf16[384,256]{1,0:T(8,128)(2,1)S(1)}, u32[]{:S(2)}, u32[]{:S(2)}) collective-permute-start(bf16[384,256]{1,0:T(8,128)(2,1)S(1)} %get-tuple-element.48), channel_id=1, source_target_pairs={{0,448},{16,464},{32,480},{48,496},{64,0},{80,16},{96,32},{112,48}... | collective-permute-start | bytes 589832 | tf_op jit(solution)/shard_map/cond/branch_2_fun/ppermute | solution.py:24
  260.2 0.7 copy-start.7
  260.2 0.9 copy-start.1

commit v4 on v3

--- a/solution.py
+++ b/solution.py
@@ -124,10 +124,12 @@
     blk_size = BLOCK
     blocks_dev = tok_count // blk_size
     inv_root = head_size ** (-0.5)
-    kv_here = fold_rows(tokens_here, gather_seq(weight_here)).astype(jnp.bfloat16)
-    kv_all = gather_other_first(kv_here)
-    keys_all = kv_all[:, :head_size]
-    values_all = kv_all[:, head_size:]
+    keys_here = fold_rows(tokens_here, gather_seq(weight_here[:, :head_size])).astype(jnp.bfloat16)
+    values_here = fold_rows(tokens_here, gather_seq(weight_here[:, head_size:])).astype(
+        jnp.bfloat16
+    )
+    keys_all = gather_other_first(keys_here)
+    values_all = gather_other_first(values_here)
     half_n = seq_count // 2
     my_half = lax.axis_index("zh")
     order = jnp.concatenate([(1 - my_half) * half_n + jnp.arange(half_n), my_half * half_n + jnp.arange(half_n)])
@@ -147,18 +149,23 @@
     query_grad = jnp.dot(score_grad, keys_all, preferred_element_type=jnp.float32).astype(
         jnp.bfloat16
     )
-    key_terms = contract_rows(score_grad, query_here)
-    value_terms = contract_rows(prob_low, grad_here)
-    grad_terms = jnp.concatenate([key_terms, value_terms], axis=1).astype(jnp.bfloat16)
-    half_rows = grad_terms.shape[0] // 2
-    kv_grad = scatter_halves(grad_terms[:half_rows], grad_terms[half_rows:]).astype(jnp.bfloat16)
+    value_terms = contract_rows(prob_low, grad_here).astype(jnp.bfloat16)
+    key_terms = contract_rows(score_grad, query_here).astype(jnp.bfloat16)
+    half_rows = key_terms.shape[0] // 2
+    value_grad = scatter_halves(value_terms[:half_rows], value_terms[half_rows:])
+    key_grad = scatter_halves(key_terms[:half_rows], key_terms[half_rows:])
     tok_view = tokens_here.reshape(tok_count, 2, -1)
     tok_other = lax.dynamic_index_in_dim(tok_view, 1 - my_half, 1, keepdims=False)
     tok_mine = lax.dynamic_index_in_dim(tok_view, my_half, 1, keepdims=False)
-    grad_slice = scatter_halves(
-        contract_rows(tok_other, kv_grad).astype(jnp.bfloat16),
-        contract_rows(tok_mine, kv_grad).astype(jnp.bfloat16),
-    )
+
+    def weight_part(column_grad):
+        column_grad = column_grad.astype(jnp.bfloat16)
+        return scatter_halves(
+            contract_rows(tok_other, column_grad).astype(jnp.bfloat16),
+            contract_rows(tok_mine, column_grad).astype(jnp.bfloat16),
+        )
+
+    grad_slice = jnp.concatenate([weight_part(key_grad), weight_part(value_grad)], axis=1)
     branches = [
         partial(gossip, distance=(1 << level_idx) % rep_count, rep_count=rep_count)
         for level_idx in range(4)

time: 264 us -> 388 us (1.47)
  the two profiles are of different devices: /device:TPU:1 before, /device:TPU:8 now
where the time goes in v4:
time: 388 us; the launch traced here: 385 us
  starting transfers between devices  195 us (50%)
  waiting for transfers between devices  66.4 us (17%)
  blocking collectives  42.4 us (11%)
  other arithmetic  32.9 us (8%)
  local copies, waits for them, and re-layouts  28.2 us (7%)
  matrix products  18.9 us (5%)
    ppermute x8, starting transfers between devices, swap_zh(): return lax.ppermute(value, 'zh', [(0, 1), (1, 0)])  77.9 us
    all_to_all x8, starting transfers between devices, reduce_half(): spread = lax.all_to_all(summed, 'y', 0, 0, tiled=False)  42.5 us
    all_to_all x7, starting transfers between devices, spread_half(): return lax.all_to_all(copies, ('y', 'c'), 0, 0, tiled=False)  35.2 us
    all_to_all x8, waiting for transfers between devices, reduce_half(): spread = lax.all_to_all(summed, 'y', 0, 0, tiled=False)  23.7 us
    ppermute x2, starting transfers between devices, shifted(): return lax.ppermute(value, axis, pairs)  22.5 us
    all_to_all x4, blocking collectives, reduce_half(): paired = lax.all_to_all(part, 'c', 1, 1, tiled=False)  22.4 us
    ppermute x8, waiting for transfers between devices, swap_zh(): return lax.ppermute(value, 'zh', [(0, 1), (1, 0)])  21.3 us
    all_to_all x1, blocking collectives, spread_half(): return lax.all_to_all(copies, ('y', 'c'), 0, 0, tiled=False)  20 us
  transfers between devices with their start and end apart: 29, of which 16 were waited for; matrix products, arithmetic and copies ran while one was open for 14% of the time, Pallas kernels for 0%

profile of v4, /device:TPU:8, one launch (start us, length us, event | category | flops | bytes accessed | tf_op | source)
XLA Modules:
  0.0 385.3 jit_solution(17373079888435024427)
XLA Ops:
  1.7 20.0 %all_to_all.120 = bf16[8,384,128]{2,1,0:T(8,128)(2,1)S(1)} all-to-all(bf16[8,384,128]{2,1,0:T(8,128)(2,1)S(1)} %broadcast_in_dim.40), channel_id=1, replica_groups=mesh['rep'=32,'zh'=2,'y'=4,'c'=2] {'y','c'}, dimensions={0} | all-to-all | bytes 1572864 | tf_op jit(solution)/shard_map/all_to_all | solution.py:40
  22.7 4.9 %all-to-all-start.4 = ((bf16[8,384,128]{2,1,0:T(8,128)(2,1)}), bf16[8,384,128]{2,1,0:T(8,128)(2,1)S(1)}, u32[]{:S(2)}, u32[]{:S(2)}) async-start(bf16[8,384,128]{2,1,0:T(8,128)(2,1)} %broadcast_in_dim.87), calls=%async_computation.4 | async-start | bytes 1572864 | tf_op jit(solution)/shard_map/all_to_all | solution.py:40
  27.6 12.2 %collective-permute-start.8 = (bf16[384,128]{1,0:T(8,128)(2,1)S(1)}, bf16[384,128]{1,0:T(8,128)(2,1)S(1)}, u32[]{:S(2)}, u32[]{:S(2)}) collective-permute-start(bf16[384,128]{1,0:T(8,128)(2,1)S(1)} %get-tuple-element.21), channel_id=1, source_target_pairs={{0,8},{8,0},{1,9},{9,1},{2,10},{10,2},{3,11},{11,3},{4,12},{12,4},... | collective-permute-start | bytes 294920 | tf_op jit(solution)/shard_map/ppermute | solution.py:34
  39.8 3.5 collective-permute-done.8
  44.3 4.9 %all-to-all-start.1 = ((bf16[8,384,128]{2,1,0:T(8,128)(2,1)}), bf16[8,384,128]{2,1,0:T(8,128)(2,1)S(1)}, u32[]{:S(2)}, u32[]{:S(2)}) async-start(bf16[8,384,128]{2,1,0:T(8,128)(2,1)} %broadcast_in_dim.41), calls=%async_computation.1 | async-start | bytes 1572864 | tf_op jit(solution)/shard_map/all_to_all | solution.py:40
  49.2 12.1 %collective-permute-start.10 = (bf16[384,128]{1,0:T(8,128)(2,1)S(1)}, bf16[384,128]{1,0:T(8,128)(2,1)S(1)}, u32[]{:S(2)}, u32[]{:S(2)}) collective-permute-start(bf16[384,128]{1,0:T(8,128)(2,1)S(1)} %get-tuple-element.20), channel_id=1, source_target_pairs={{0,8},{8,0},{1,9},{9,1},{2,10},{10,2},{3,11},{11,3},{4,12},{12,4},... | collective-permute-start | bytes 294920 | tf_op jit(solution)/shard_map/ppermute | solution.py:34
  61.4 3.3 collective-permute-done.10
  65.6 4.8 %all-to-all-start.5 = ((bf16[8,384,128]{2,1,0:T(8,128)(2,1)}), bf16[8,384,128]{2,1,0:T(8,128)(2,1)S(1)}, u32[]{:S(2)}, u32[]{:S(2)}) async-start(bf16[8,384,128]{2,1,0:T(8,128)(2,1)} %broadcast_in_dim.88), calls=%async_computation.5 | async-start | bytes 1572864 | tf_op jit(solution)/shard_map/all_to_all | solution.py:40
  70.9 11.2 %all-to-all-done.5 = bf16[8,384,128]{2,1,0:T(8,128)(2,1)S(1)} async-done(((bf16[8,384,128]{2,1,0:T(8,128)(2,1)}), bf16[8,384,128]{2,1,0:T(8,128)(2,1)S(1)}, u32[]{:S(2)}, u32[]{:S(2)}) %all-to-all-start.5) | async-done | bytes 786464 | tf_op jit(solution)/shard_map/all_to_all | solution.py:40
  87.5 5.5 %all-to-all-start.3 = ((bf16[8,256,128]{2,1,0:T(8,128)(2,1)}), bf16[8,256,128]{2,1,0:T(8,128)(2,1)}, u32[]{:S(2)}, u32[]{:S(2)}) async-start(bf16[8,256,128]{2,1,0:T(8,128)(2,1)} %broadcast_in_dim.43), calls=%async_computation.3 | async-start | bytes 1048576 | tf_op jit(solution)/shard_map/all_to_all | solution.py:40
  93.0 12.1 %collective-permute-start.9 = (bf16[256,128]{0,1:T(8,128)(2,1)S(1)}, bf16[256,128]{0,1:T(8,128)(2,1)S(1)}, u32[]{:S(2)}, u32[]{:S(2)}) collective-permute-start(bf16[256,128]{0,1:T(8,128)(2,1)S(1)} %fusion.30), channel_id=1, source_target_pairs={{0,8},{8,0},{1,9},{9,1},{2,10},{10,2},{3,11},{11,3},{4,12},{12,4},... | collective-permute-start | bytes 196616 | tf_op jit(solution)/shard_map/ppermute | solution.py:34
  105.2 2.7 pad_maximum_fusion.1
  108.9 4.8 %all-to-all-start.2 = ((bf16[8,256,128]{2,1,0:T(8,128)(2,1)}), bf16[8,256,128]{2,1,0:T(8,128)(2,1)}, u32[]{:S(2)}, u32[]{:S(2)}) async-start(bf16[8,256,128]{2,1,0:T(8,128)(2,1)} %broadcast_in_dim.42), calls=%async_computation.2 | async-start | bytes 1048576 | tf_op jit(solution)/shard_map/all_to_all | solution.py:40
  113.7 2.6 fusion.27
  116.3 12.1 %collective-permute-start.11 = (bf16[256,128]{0,1:T(8,128)(2,1)S(1)}, bf16[256,128]{0,1:T(8,128)(2,1)S(1)}, u32[]{:S(2)}, u32[]{:S(2)}) collective-permute-start(bf16[256,128]{0,1:T(8,128)(2,1)S(1)} %fusion.27), channel_id=1, source_target_pairs={{0,8},{8,0},{1,9},{9,1},{2,10},{10,2},{3,11},{11,3},{4,12},{12,4},... | collective-permute-start | bytes 196616 | tf_op jit(solution)/shard_map/ppermute | solution.py:34
  129.2 2.0 collective-permute-done.11
  132.2 4.8 %all-to-all-start.7 = ((bf16[8,256,128]{2,1,0:T(8,128)(2,1)}), bf16[8,256,128]{2,1,0:T(8,128)(2,1)}, u32[]{:S(2)}, u32[]{:S(2)}) async-start(bf16[8,256,128]{2,1,0:T(8,128)(2,1)} %broadcast_in_dim.90), calls=%async_computation.7 | async-start | bytes 1048576 | tf_op jit(solution)/shard_map/all_to_all | solution.py:40
  139.3 3.1 fusion.47
  142.4 3.6 all-to-all-done.7
  146.9 5.5 %all-to-all-start.6 = ((bf16[8,256,128]{2,1,0:T(8,128)(2,1)}), bf16[8,256,128]{2,1,0:T(8,128)(2,1)}, u32[]{:S(2)}, u32[]{:S(2)}) async-start(bf16[8,256,128]{2,1,0:T(8,128)(2,1)} %broadcast_in_dim.89), calls=%async_computation.6 | async-start | bytes 1048576 | tf_op jit(solution)/shard_map/all_to_all | solution.py:40
  152.3 2.5 fusion.11
  156.2 1.8 convolution_convert_fusion
  158.0 3.4 all-to-all-done.6
  163.8 3.0 fusion.6
  169.9 4.2 %all-to-all-start.10 = ((bf16[4,2,256,128]{3,2,0,1:T(8,128)(2,1)}), bf16[4,2,256,128]{3,2,0,1:T(8,128)(2,1)}, u32[]{:S(2)}, u32[]{:S(2)}) async-start(bf16[4,2,256,128]{3,2,0,1:T(8,128)(2,1)} %copy.55), calls=%async_computation.10 | async-start | bytes 1048576 | tf_op jit(solution)/shard_map/all_to_all | solution.py:61
  174.1 1.9 copy.54
  179.0 4.2 %all-to-all-start.8 = ((bf16[4,2,256,128]{3,2,0,1:T(8,128)(2,1)}), bf16[4,2,256,128]{3,2,0,1:T(8,128)(2,1)}, u32[]{:S(2)}, u32[]{:S(2)}) async-start(bf16[4,2,256,128]{3,2,0,1:T(8,128)(2,1)} %copy.54), calls=%async_computation.8 | async-start | bytes 1048576 | tf_op jit(solution)/shard_map/all_to_all | solution.py:61
  183.2 1.9 reduce_sum.202
  185.1 6.1 %all_to_all.121 = bf16[4,2,256,128]{3,2,0,1:T(8,128)(2,1)} all-to-all(bf16[4,2,256,128]{3,2,0,1:T(8,128)(2,1)} %copy.60), channel_id=1, replica_groups=mesh['rep'=32,'zh'=2,'y'=4,'c'=2] {'c'}, dimensions={1} | all-to-all | bytes 1048576 | tf_op jit(solution)/shard_map/all_to_all | solution.py:61
  191.2 6.1 %all_to_all.122 = bf16[4,2,256,128]{3,2,0,1:T(8,128)(2,1)} all-to-all(bf16[4,2,256,128]{3,2,0,1:T(8,128)(2,1)} %copy.59), channel_id=1, replica_groups=mesh['rep'=32,'zh'=2,'y'=4,'c'=2] {'c'}, dimensions={1} | all-to-all | bytes 1048576 | tf_op jit(solution)/shard_map/all_to_all | solution.py:61
  197.2 4.8 %all-to-all-start.11 = ((bf16[4,256,128]{2,1,0:T(8,128)(2,1)}), bf16[4,256,128]{2,1,0:T(8,128)(2,1)S(1)}, u32[]{:S(2)}, u32[]{:S(2)}) async-start(bf16[4,256,128]{2,1,0:T(8,128)(2,1)} %reduce_sum.202), calls=%async_computation.11 | async-start | bytes 524288 | tf_op jit(solution)/shard_map/all_to_all | solution.py:63
  202.0 1.9 reduce_sum.200
  203.9 3.9 %all-to-all-done.11 = bf16[4,256,128]{2,1,0:T(8,128)(2,1)S(1)} async-done(((bf16[4,256,128]{2,1,0:T(8,128)(2,1)}), bf16[4,256,128]{2,1,0:T(8,128)(2,1)S(1)}, u32[]{:S(2)}, u32[]{:S(2)}) %all-to-all-start.11) | async-done | bytes 262176 | tf_op jit(solution)/shard_map/all_to_all | solution.py:63
  207.8 5.5 %all-to-all-start.9 = ((bf16[4,256,128]{2,1,0:T(8,128)(2,1)}), bf16[4,256,128]{2,1,0:T(8,128)(2,1)}, u32[]{:S(2)}, u32[]{:S(2)}) async-start(bf16[4,256,128]{2,1,0:T(8,128)(2,1)} %reduce_sum.200), calls=%async_computation.9 | async-start | bytes 524288 | tf_op jit(solution)/shard_map/all_to_all | solution.py:63
  213.3 1.9 reduce_sum.210
  215.2 3.4 all-to-all-done.9
  218.6 5.5 %all-to-all-start.19 = ((bf16[4,256,128]{2,1,0:T(8,128)(2,1)}), bf16[4,256,128]{2,1,0:T(8,128)(2,1)}, u32[]{:S(2)}, u32[]{:S(2)}) async-start(bf16[4,256,128]{2,1,0:T(8,128)(2,1)} %reduce_sum.210), calls=%async_computation.19 | async-start | bytes 524288 | tf_op jit(solution)/shard_map/all_to_all | solution.py:63
  224.1 1.9 reduce_sum.208
  226.0 3.4 all-to-all-done.19
  229.4 5.5 %all-to-all-start.17 = ((bf16[4,256,128]{2,1,0:T(8,128)(2,1)}), bf16[4,256,128]{2,1,0:T(8,128)(2,1)}, u32[]{:S(2)}, u32[]{:S(2)}) async-start(bf16[4,256,128]{2,1,0:T(8,128)(2,1)} %reduce_sum.208), calls=%async_computation.17 | async-start | bytes 524288 | tf_op jit(solution)/shard_map/all_to_all | solution.py:63
  234.9 2.8 copy.46
  237.7 12.3 %collective-permute-start.12 = (bf16[256,128]{1,0:T(8,128)(2,1)S(1)}, bf16[256,128]{1,0:T(8,128)(2,1)S(1)}, u32[]{:S(2)}, u32[]{:S(2)}) collective-permute-start(bf16[256,128]{1,0:T(8,128)(2,1)S(1)} %reduce_sum.203), channel_id=1, source_target_pairs={{0,8},{8,0},{1,9},{9,1},{2,10},{10,2},{3,11},{11,3},{4,12},{12,4},... | collective-permute-start | bytes 196616 | tf_op jit(solution)/shard_map/ppermute | solution.py:34
  251.6 2.4 collective-permute-start.14
  256.7 2.0 convolution_convert_fusion.4
  259.7 4.5 %all-to-all-start.14 = ((bf16[4,2,384,128]{3,2,0,1:T(8,128)(2,1)}), bf16[4,2,384,128]{3,2,0,1:T(8,128)(2,1)}, u32[]{:S(2)}, u32[]{:S(2)}) async-start(bf16[4,2,384,128]{3,2,0,1:T(8,128)(2,1)} %copy.58), calls=%async_computation.14 | async-start | bytes 1572864 | tf_op jit(solution)/shard_map/all_to_all | solution.py:61
  269.0 3.7 all-to-all-start.12
  272.6 2.1 reduce_sum.206
  274.8 5.1 %all_to_all.123 = bf16[4,2,384,128]{3,2,0,1:T(8,128)(2,1)} all-to-all(bf16[4,2,384,128]{3,2,0,1:T(8,128)(2,1)S(1)} %copy-done.9), channel_id=1, replica_groups=mesh['rep'=32,'zh'=2,'y'=4,'c'=2] {'c'}, dimensions={1} | all-to-all | bytes 1572864 | tf_op jit(solution)/shard_map/all_to_all | solution.py:61
  279.9 5.1 %all_to_all.124 = bf16[4,2,384,128]{3,2,0,1:T(8,128)(2,1)} all-to-all(bf16[4,2,384,128]{3,2,0,1:T(8,128)(2,1)S(1)} %copy.61), channel_id=1, replica_groups=mesh['rep'=32,'zh'=2,'y'=4,'c'=2] {'c'}, dimensions={1} | all-to-all | bytes 1572864 | tf_op jit(solution)/shard_map/all_to_all | solution.py:61
  285.0 4.8 %all-to-all-start.15 = ((bf16[4,384,128]{2,1,0:T(8,128)(2,1)}), bf16[4,384,128]{2,1,0:T(8,128)(2,1)S(1)}, u32[]{:S(2)}, u32[]{:S(2)}) async-start(bf16[4,384,128]{2,1,0:T(8,128)(2,1)} %reduce_sum.206), calls=%async_computation.15 | async-start | bytes 786432 | tf_op jit(solution)/shard_map/all_to_all | solution.py:63
  290.8 5.9 %all-to-all-done.15 = bf16[4,384,128]{2,1,0:T(8,128)(2,1)S(1)} async-done(((bf16[4,384,128]{2,1,0:T(8,128)(2,1)}), bf16[4,384,128]{2,1,0:T(8,128)(2,1)S(1)}, u32[]{:S(2)}, u32[]{:S(2)}) %all-to-all-start.15) | async-done | bytes 393248 | tf_op jit(solution)/shard_map/all_to_all | solution.py:63
  297.5 5.5 %all-to-all-start.13 = ((bf16[4,384,128]{2,1,0:T(8,128)(2,1)}), bf16[4,384,128]{2,1,0:T(8,128)(2,1)}, u32[]{:S(2)}, u32[]{:S(2)}) async-start(bf16[4,384,128]{2,1,0:T(8,128)(2,1)} %reduce_sum.204), calls=%async_computation.13 | async-start | bytes 786432 | tf_op jit(solution)/shard_map/all_to_all | solution.py:63
  303.0 2.3 reduce_sum.214
  305.3 3.8 all-to-all-done.13
  309.0 5.5 %all-to-all-start.23 = ((bf16[4,384,128]{2,1,0:T(8,128)(2,1)}), bf16[4,384,128]{2,1,0:T(8,128)(2,1)}, u32[]{:S(2)}, u32[]{:S(2)}) async-start(bf16[4,384,128]{2,1,0:T(8,128)(2,1)} %reduce_sum.214), calls=%async_computation.23 | async-start | bytes 786432 | tf_op jit(solution)/shard_map/all_to_all | solution.py:63
  315.2 2.1 reduce_sum.212
  317.4 3.2 all-to-all-done.23
  320.6 5.5 %all-to-all-start.21 = ((bf16[4,384,128]{2,1,0:T(8,128)(2,1)}), bf16[4,384,128]{2,1,0:T(8,128)(2,1)}, u32[]{:S(2)}, u32[]{:S(2)}) async-start(bf16[4,384,128]{2,1,0:T(8,128)(2,1)} %reduce_sum.212), calls=%async_computation.21 | async-start | bytes 786432 | tf_op jit(solution)/shard_map/all_to_all | solution.py:63
  328.6 11.9 %collective-permute-start.13 = (bf16[384,128]{1,0:T(8,128)(2,1)S(1)}, bf16[384,128]{1,0:T(8,128)(2,1)S(1)}, u32[]{:S(2)}, u32[]{:S(2)}) collective-permute-start(bf16[384,128]{1,0:T(8,128)(2,1)S(1)} %reduce_sum.207), channel_id=1, source_target_pairs={{0,8},{8,0},{1,9},{9,1},{2,10},{10,2},{3,11},{11,3},{4,12},{12,4},... | collective-permute-start | bytes 294920 | tf_op jit(solution)/shard_map/ppermute | solution.py:34
  341.5 2.7 collective-permute-start.15
  346.4 12.3 %collective-permute-done.15 = bf16[384,128]{1,0:T(8,128)(2,1)S(1)} collective-permute-done((bf16[384,128]{1,0:T(8,128)(2,1)S(1)}, bf16[384,128]{1,0:T(8,128)(2,1)S(1)}, u32[]{:S(2)}, u32[]{:S(2)}) %collective-permute-start.15) | collective-permute-done | bytes 98336 | tf_op jit(solution)/shard_map/ppermute | solution.py:34
  358.7 25.8 %conditional.1 = (f32[1,384,256]{2,1,0:T(8,128)S(1)}) conditional(s32[]{:T(128)} %clamp.3, f32[384,256]{1,0:T(8,128)S(1)} %pad_maximum_fusion.4, f32[384,256]{1,0:T(8,128)S(1)} %pad_maximum_fusion.4, f32[384,256]{1,0:T(8,128)S(1)} %pad_maximum_fusion.4, f32[384,256]{1,0:T(8,128)S(1)} %pad_maximum_fusion.4), branch_computations={%region_19.20_spmd, %region_20.21_spmd, %region_21.22_spmd, %regio... | conditional | flops 589824 | bytes 3342424 | solution.py:173
  358.8 5.0 %collective-permute-start.2 = (bf16[384,256]{1,0:T(8,128)(2,1)S(1)}, bf16[384,256]{1,0:T(8,128)(2,1)S(1)}, u32[]{:S(2)}, u32[]{:S(2)}) collective-permute-start(bf16[384,256]{1,0:T(8,128)(2,1)S(1)} %convert_element_type.17), channel_id=1, source_target_pairs={{0,32},{16,48},{32,64},{48,80},{64,96},{80,112},{96,128},{112,144}... | collective-permute-start | bytes 589832 | tf_op jit(solution)/shard_map/cond/branch_1_fun/ppermute | solution.py:24
  363.8 17.5 %collective-permute-start.3 = (bf16[384,256]{1,0:T(8,128)(2,1)S(1)}, bf16[384,256]{1,0:T(8,128)(2,1)S(1)}, u32[]{:S(2)}, u32[]{:S(2)}) collective-permute-start(bf16[384,256]{1,0:T(8,128)(2,1)S(1)} %convert_element_type.17), channel_id=1, source_target_pairs={{0,480},{16,496},{32,0},{48,16},{64,32},{80,48},{96,64},{112,80},{... | collective-permute-start | bytes 589832 | tf_op jit(solution)/shard_map/cond/branch_1_fun/ppermute | solution.py:24
  (107 shorter events, 47.0 us)
Async XLA Ops:
  0.6 138.7 %copy-start = (bf16[1,256,128]{2,1,0:T(8,128)(2,1)S(1)}, bf16[1,256,128]{2,1,0:T(8,128)(2,1)}, u32[]{:S(2)}) copy-start(bf16[1,256,128]{2,1,0:T(8,128)(2,1)} %param.11) | copy-start | bytes 196612
  22.7 20.6 %all-to-all-start.4 = ((bf16[8,384,128]{2,1,0:T(8,128)(2,1)}), bf16[8,384,128]{2,1,0:T(8,128)(2,1)S(1)}, u32[]{:S(2)}, u32[]{:S(2)}) async-start(bf16[8,384,128]{2,1,0:T(8,128)(2,1)} %broadcast_in_dim.87), calls=%async_computation.4 | async-start | bytes 1572864 | tf_op jit(solution)/shard_map/all_to_all | solution.py:40
  27.6 15.7 %collective-permute-start.8 = (bf16[384,128]{1,0:T(8,128)(2,1)S(1)}, bf16[384,128]{1,0:T(8,128)(2,1)S(1)}, u32[]{:S(2)}, u32[]{:S(2)}) collective-permute-start(bf16[384,128]{1,0:T(8,128)(2,1)S(1)} %get-tuple-element.21), channel_id=1, source_target_pairs={{0,8},{8,0},{1,9},{9,1},{2,10},{10,2},{3,11},{11,3},{4,12},{12,4},... | collective-permute-start | bytes 294920 | tf_op jit(solution)/shard_map/ppermute | solution.py:34
  44.3 26.4 %copy-start.14 = (s32[64,3]{0,1:T(4,128)S(1)}, s32[64,3]{0,1:T(4,128)}, u32[]{:S(2)}) copy-start(s32[64,3]{0,1:T(4,128)} %param.14) | copy-start | bytes 2308
  44.3 20.4 %all-to-all-start.1 = ((bf16[8,384,128]{2,1,0:T(8,128)(2,1)}), bf16[8,384,128]{2,1,0:T(8,128)(2,1)S(1)}, u32[]{:S(2)}, u32[]{:S(2)}) async-start(bf16[8,384,128]{2,1,0:T(8,128)(2,1)} %broadcast_in_dim.41), calls=%async_computation.1 | async-start | bytes 1572864 | tf_op jit(solution)/shard_map/all_to_all | solution.py:40
  49.2 15.4 %collective-permute-start.10 = (bf16[384,128]{1,0:T(8,128)(2,1)S(1)}, bf16[384,128]{1,0:T(8,128)(2,1)S(1)}, u32[]{:S(2)}, u32[]{:S(2)}) collective-permute-start(bf16[384,128]{1,0:T(8,128)(2,1)S(1)} %get-tuple-element.20), channel_id=1, source_target_pairs={{0,8},{8,0},{1,9},{9,1},{2,10},{10,2},{3,11},{11,3},{4,12},{12,4},... | collective-permute-start | bytes 294920 | tf_op jit(solution)/shard_map/ppermute | solution.py:34
  65.6 16.5 %all-to-all-start.5 = ((bf16[8,384,128]{2,1,0:T(8,128)(2,1)}), bf16[8,384,128]{2,1,0:T(8,128)(2,1)S(1)}, u32[]{:S(2)}, u32[]{:S(2)}) async-start(bf16[8,384,128]{2,1,0:T(8,128)(2,1)} %broadcast_in_dim.88), calls=%async_computation.5 | async-start | bytes 1572864 | tf_op jit(solution)/shard_map/all_to_all | solution.py:40
  83.4 1.9 copy-start.1
  87.5 20.5 %all-to-all-start.3 = ((bf16[8,256,128]{2,1,0:T(8,128)(2,1)}), bf16[8,256,128]{2,1,0:T(8,128)(2,1)}, u32[]{:S(2)}, u32[]{:S(2)}) async-start(bf16[8,256,128]{2,1,0:T(8,128)(2,1)} %broadcast_in_dim.43), calls=%async_computation.3 | async-start | bytes 1048576 | tf_op jit(solution)/shard_map/all_to_all | solution.py:40
  93.0 14.9 %collective-permute-start.9 = (bf16[256,128]{0,1:T(8,128)(2,1)S(1)}, bf16[256,128]{0,1:T(8,128)(2,1)S(1)}, u32[]{:S(2)}, u32[]{:S(2)}) collective-permute-start(bf16[256,128]{0,1:T(8,128)(2,1)S(1)} %fusion.30), channel_id=1, source_target_pairs={{0,8},{8,0},{1,9},{9,1},{2,10},{10,2},{3,11},{11,3},{4,12},{12,4},... | collective-permute-start | bytes 196616 | tf_op jit(solution)/shard_map/ppermute | solution.py:34
  108.9 22.4 %all-to-all-start.2 = ((bf16[8,256,128]{2,1,0:T(8,128)(2,1)}), bf16[8,256,128]{2,1,0:T(8,128)(2,1)}, u32[]{:S(2)}, u32[]{:S(2)}) async-start(bf16[8,256,128]{2,1,0:T(8,128)(2,1)} %broadcast_in_dim.42), calls=%async_computation.2 | async-start | bytes 1048576 | tf_op jit(solution)/shard_map/all_to_all | solution.py:40
  113.7 15.2 %copy-start.12 = (bf16[1,256,128]{2,1,0:T(8,128)(2,1)S(1)}, bf16[1,256,128]{2,1,0:T(8,128)(2,1)}, u32[]{:S(2)}) copy-start(bf16[1,256,128]{2,1,0:T(8,128)(2,1)} %param.12) | copy-start | bytes 196612
  116.3 14.9 %collective-permute-start.11 = (bf16[256,128]{0,1:T(8,128)(2,1)S(1)}, bf16[256,128]{0,1:T(8,128)(2,1)S(1)}, u32[]{:S(2)}, u32[]{:S(2)}) collective-permute-start(bf16[256,128]{0,1:T(8,128)(2,1)S(1)} %fusion.27), channel_id=1, source_target_pairs={{0,8},{8,0},{1,9},{9,1},{2,10},{10,2},{3,11},{11,3},{4,12},{12,4},... | collective-permute-start | bytes 196616 | tf_op jit(solution)/shard_map/ppermute | solution.py:34
  132.2 13.8 %all-to-all-start.7 = ((bf16[8,256,128]{2,1,0:T(8,128)(2,1)}), bf16[8,256,128]{2,1,0:T(8,128)(2,1)}, u32[]{:S(2)}, u32[]{:S(2)}) async-start(bf16[8,256,128]{2,1,0:T(8,128)(2,1)} %broadcast_in_dim.90), calls=%async_computation.7 | async-start | bytes 1048576 | tf_op jit(solution)/shard_map/all_to_all | solution.py:40
  138.3 1.0 copy-start.7
  146.9 14.5 %all-to-all-start.6 = ((bf16[8,256,128]{2,1,0:T(8,128)(2,1)}), bf16[8,256,128]{2,1,0:T(8,128)(2,1)}, u32[]{:S(2)}, u32[]{:S(2)}) async-start(bf16[8,256,128]{2,1,0:T(8,128)(2,1)} %broadcast_in_dim.89), calls=%async_computation.6 | async-start | bytes 1048576 | tf_op jit(solution)/shard_map/all_to_all | solution.py:40
  154.9 1.4 copy-start.5
  161.3 1.9 copy-start.6
  166.8 1.4 copy-start.3
  169.9 9.1 %all-to-all-start.10 = ((bf16[4,2,256,128]{3,2,0,1:T(8,128)(2,1)}), bf16[4,2,256,128]{3,2,0,1:T(8,128)(2,1)}, u32[]{:S(2)}, u32[]{:S(2)}) async-start(bf16[4,2,256,128]{3,2,0,1:T(8,128)(2,1)} %copy.55), calls=%async_computation.10 | async-start | bytes 1048576 | tf_op jit(solution)/shard_map/all_to_all | solution.py:61
  179.0 6.1 %all-to-all-start.8 = ((bf16[4,2,256,128]{3,2,0,1:T(8,128)(2,1)}), bf16[4,2,256,128]{3,2,0,1:T(8,128)(2,1)}, u32[]{:S(2)}, u32[]{:S(2)}) async-start(bf16[4,2,256,128]{3,2,0,1:T(8,128)(2,1)} %copy.54), calls=%async_computation.8 | async-start | bytes 1048576 | tf_op jit(solution)/shard_map/all_to_all | solution.py:61
  197.2 10.6 %all-to-all-start.11 = ((bf16[4,256,128]{2,1,0:T(8,128)(2,1)}), bf16[4,256,128]{2,1,0:T(8,128)(2,1)S(1)}, u32[]{:S(2)}, u32[]{:S(2)}) async-start(bf16[4,256,128]{2,1,0:T(8,128)(2,1)} %reduce_sum.202), calls=%async_computation.11 | async-start | bytes 524288 | tf_op jit(solution)/shard_map/all_to_all | solution.py:63
  207.8 10.8 %all-to-all-start.9 = ((bf16[4,256,128]{2,1,0:T(8,128)(2,1)}), bf16[4,256,128]{2,1,0:T(8,128)(2,1)}, u32[]{:S(2)}, u32[]{:S(2)}) async-start(bf16[4,256,128]{2,1,0:T(8,128)(2,1)} %reduce_sum.200), calls=%async_computation.9 | async-start | bytes 524288 | tf_op jit(solution)/shard_map/all_to_all | solution.py:63
  218.6 10.8 %all-to-all-start.19 = ((bf16[4,256,128]{2,1,0:T(8,128)(2,1)}), bf16[4,256,128]{2,1,0:T(8,128)(2,1)}, u32[]{:S(2)}, u32[]{:S(2)}) async-start(bf16[4,256,128]{2,1,0:T(8,128)(2,1)} %reduce_sum.210), calls=%async_computation.19 | async-start | bytes 524288 | tf_op jit(solution)/shard_map/all_to_all | solution.py:63
  229.4 25.7 %all-to-all-start.17 = ((bf16[4,256,128]{2,1,0:T(8,128)(2,1)}), bf16[4,256,128]{2,1,0:T(8,128)(2,1)}, u32[]{:S(2)}, u32[]{:S(2)}) async-start(bf16[4,256,128]{2,1,0:T(8,128)(2,1)} %reduce_sum.208), calls=%async_computation.17 | async-start | bytes 524288 | tf_op jit(solution)/shard_map/all_to_all | solution.py:63
  237.7 18.4 %collective-permute-start.12 = (bf16[256,128]{1,0:T(8,128)(2,1)S(1)}, bf16[256,128]{1,0:T(8,128)(2,1)S(1)}, u32[]{:S(2)}, u32[]{:S(2)}) collective-permute-start(bf16[256,128]{1,0:T(8,128)(2,1)S(1)} %reduce_sum.203), channel_id=1, source_target_pairs={{0,8},{8,0},{1,9},{9,1},{2,10},{10,2},{3,11},{11,3},{4,12},{12,4},... | collective-permute-start | bytes 196616 | tf_op jit(solution)/shard_map/ppermute | solution.py:34
  251.6 15.1 %collective-permute-start.14 = (bf16[256,128]{1,0:T(8,128)(2,1)}, bf16[256,128]{1,0:T(8,128)(2,1)S(1)}, u32[]{:S(2)}, u32[]{:S(2)}) collective-permute-start(bf16[256,128]{1,0:T(8,128)(2,1)} %reduce_sum.211), channel_id=1, source_target_pairs={{0,8},{8,0},{1,9},{9,1},{2,10},{10,2},{3,11},{11,3},{4,12},{12,4},... | collective-permute-start | bytes 196616 | tf_op jit(solution)/shard_map/ppermute | solution.py:34
  256.1 0.6 copy-start.13
  258.7 5.5 %copy-start.2 = (bf16[1,256,6144]{1,2,0:T(8,128)(2,1)S(1)}, bf16[1,256,6144]{1,2,0:T(8,128)(2,1)}, u32[]{:S(2)}) copy-start(bf16[1,256,6144]{1,2,0:T(8,128)(2,1)} %copy.46) | copy-start | bytes 9437188
  259.7 9.3 %all-to-all-start.14 = ((bf16[4,2,384,128]{3,2,0,1:T(8,128)(2,1)}), bf16[4,2,384,128]{3,2,0,1:T(8,128)(2,1)}, u32[]{:S(2)}, u32[]{:S(2)}) async-start(bf16[4,2,384,128]{3,2,0,1:T(8,128)(2,1)} %copy.58), calls=%async_computation.14 | async-start | bytes 1572864 | tf_op jit(solution)/shard_map/all_to_all | solution.py:61
  268.9 5.9 %copy-start.9 = (bf16[4,2,384,128]{3,2,0,1:T(8,128)(2,1)S(1)}, bf16[4,2,384,128]{3,2,0,1:T(8,128)(2,1)}, u32[]{:S(2)}) copy-start(bf16[4,2,384,128]{3,2,0,1:T(8,128)(2,1)} %copy.62) | copy-start | bytes 2359300
  269.0 5.8 %all-to-all-start.12 = ((bf16[4,2,384,128]{3,2,0,1:T(8,128)(2,1)}), bf16[4,2,384,128]{3,2,0,1:T(8,128)(2,1)S(1)}, u32[]{:S(2)}, u32[]{:S(2)}) async-start(bf16[4,2,384,128]{3,2,0,1:T(8,128)(2,1)} %copy.56), calls=%async_computation.12 | async-start | bytes 1572864 | tf_op jit(solution)/shard_map/all_to_all | solution.py:61
  285.0 11.7 %all-to-all-start.15 = ((bf16[4,384,128]{2,1,0:T(8,128)(2,1)}), bf16[4,384,128]{2,1,0:T(8,128)(2,1)S(1)}, u32[]{:S(2)}, u32[]{:S(2)}) async-start(bf16[4,384,128]{2,1,0:T(8,128)(2,1)} %reduce_sum.206), calls=%async_computation.15 | async-start | bytes 786432 | tf_op jit(solution)/shard_map/all_to_all | solution.py:63
  296.7 0.7 copy-start.10
  297.5 11.6 %all-to-all-start.13 = ((bf16[4,384,128]{2,1,0:T(8,128)(2,1)}), bf16[4,384,128]{2,1,0:T(8,128)(2,1)}, u32[]{:S(2)}, u32[]{:S(2)}) async-start(bf16[4,384,128]{2,1,0:T(8,128)(2,1)} %reduce_sum.204), calls=%async_computation.13 | async-start | bytes 786432 | tf_op jit(solution)/shard_map/all_to_all | solution.py:63
  303.0 23.1 %copy-start.4 = (bf16[256,4096]{0,1:T(8,128)(2,1)S(1)}, bf16[256,4096]{0,1:T(8,128)(2,1)}, u32[]{:S(2)}) copy-start(bf16[256,4096]{0,1:T(8,128)(2,1)} %copy-done.3) | copy-start | bytes 6291460
  303.0 23.1 %copy-start.8 = (bf16[16,256,128]{2,1,0:T(8,128)(2,1)S(1)}, bf16[16,256,128]{2,1,0:T(8,128)(2,1)}, u32[]{:S(2)}) copy-start(bf16[16,256,128]{2,1,0:T(8,128)(2,1)} %copy-done.7) | copy-start | bytes 3145732
  309.0 11.6 %all-to-all-start.23 = ((bf16[4,384,128]{2,1,0:T(8,128)(2,1)}), bf16[4,384,128]{2,1,0:T(8,128)(2,1)}, u32[]{:S(2)}, u32[]{:S(2)}) async-start(bf16[4,384,128]{2,1,0:T(8,128)(2,1)} %reduce_sum.214), calls=%async_computation.23 | async-start | bytes 786432 | tf_op jit(solution)/shard_map/all_to_all | solution.py:63
  320.6 24.7 %all-to-all-start.21 = ((bf16[4,384,128]{2,1,0:T(8,128)(2,1)}), bf16[4,384,128]{2,1,0:T(8,128)(2,1)}, u32[]{:S(2)}, u32[]{:S(2)}) async-start(bf16[4,384,128]{2,1,0:T(8,128)(2,1)} %reduce_sum.212), calls=%async_computation.21 | async-start | bytes 786432 | tf_op jit(solution)/shard_map/all_to_all | solution.py:63
  328.6 17.8 %collective-permute-start.13 = (bf16[384,128]{1,0:T(8,128)(2,1)S(1)}, bf16[384,128]{1,0:T(8,128)(2,1)S(1)}, u32[]{:S(2)}, u32[]{:S(2)}) collective-permute-start(bf16[384,128]{1,0:T(8,128)(2,1)S(1)} %reduce_sum.207), channel_id=1, source_target_pairs={{0,8},{8,0},{1,9},{9,1},{2,10},{10,2},{3,11},{11,3},{4,12},{12,4},... | collective-permute-start | bytes 294920 | tf_op jit(solution)/shard_map/ppermute | solution.py:34
  341.5 17.1 %collective-permute-start.15 = (bf16[384,128]{1,0:T(8,128)(2,1)S(1)}, bf16[384,128]{1,0:T(8,128)(2,1)S(1)}, u32[]{:S(2)}, u32[]{:S(2)}) collective-permute-start(bf16[384,128]{1,0:T(8,128)(2,1)S(1)} %reduce_sum.215), channel_id=1, source_target_pairs={{0,8},{8,0},{1,9},{9,1},{2,10},{10,2},{3,11},{11,3},{4,12},{12,4},... | collective-permute-start | bytes 294920 | tf_op jit(solution)/shard_map/ppermute | solution.py:34
  358.8 24.2 %collective-permute-start.2 = (bf16[384,256]{1,0:T(8,128)(2,1)S(1)}, bf16[384,256]{1,0:T(8,128)(2,1)S(1)}, u32[]{:S(2)}, u32[]{:S(2)}) collective-permute-start(bf16[384,256]{1,0:T(8,128)(2,1)S(1)} %convert_element_type.17), channel_id=1, source_target_pairs={{0,32},{16,48},{32,64},{48,80},{64,96},{80,112},{96,128},{112,144}... | collective-permute-start | bytes 589832 | tf_op jit(solution)/shard_map/cond/branch_1_fun/ppermute | solution.py:24
  363.8 20.7 %collective-permute-start.3 = (bf16[384,256]{1,0:T(8,128)(2,1)S(1)}, bf16[384,256]{1,0:T(8,128)(2,1)S(1)}, u32[]{:S(2)}, u32[]{:S(2)}) collective-permute-start(bf16[384,256]{1,0:T(8,128)(2,1)S(1)} %convert_element_type.17), channel_id=1, source_target_pairs={{0,480},{16,496},{32,0},{48,16},{64,32},{80,48},{96,64},{112,80},{... | collective-permute-start | bytes 589832 | tf_op jit(solution)/shard_map/cond/branch_1_fun/ppermute | solution.py:24
  384.5 0.7 copy-start.11

commit v5 on v3

--- a/solution.py
+++ b/solution.py
@@ -5,6 +5,7 @@
 from jax import lax
 from jax.sharding import Mesh
 from jax.sharding import PartitionSpec as P
+
 
 BLOCK = 64
 SEQ_AXES = ("zh", "y", "c")
@@ -67,8 +68,10 @@
 def scatter_halves(for_other, for_me):
     y_n, c_n = lax.axis_size("y"), lax.axis_size("c")
     shape = (y_n, c_n, for_other.shape[0] // (y_n * c_n)) + for_other.shape[1:]
-    got = swap_zh(reduce_half(for_other.reshape(shape)).astype(jnp.bfloat16))
-    return reduce_half(for_me.reshape(shape)) + got.astype(jnp.float32)
+    reduced = reduce_half(for_other.reshape(shape)).astype(jnp.bfloat16)
+    got = swap_zh(reduced)
+    kept = reduce_half(for_me.reshape(shape))
+    return kept + got.astype(jnp.float32)
 
 
 def fold_rows(tok_rows, row_piece):

time: 264 us -> 266 us (level)
  waiting for transfers between devices: 75 us -> 84.9 us
  starting transfers between devices: 131 us -> 123 us
    ppermute x2, waiting for transfers between devices: 5.74 us -> 15.6 us  [shifted(): return lax.ppermute(value, axis, pairs)]
    ppermute x2, starting transfers between devices: 35.3 us -> 26.6 us  [shifted(): return lax.ppermute(value, axis, pairs)]
where the time goes in v5:
time: 266 us; the launch traced here: 262 us
  starting transfers between devices  123 us (46%)
  waiting for transfers between devices  84.9 us (32%)
  local copies, waits for them, and re-layouts  19.4 us (7%)
  other arithmetic  12.5 us (5%)
  matrix products  11.1 us (4%)
  blocking collectives  9.75 us (4%)
    ppermute x4, starting transfers between devices, swap_zh(): return lax.ppermute(value, 'zh', [(0, 1), (1, 0)])  44.4 us
    all_to_all x4, waiting for transfers between devices, spread_half(): return lax.all_to_all(copies, ('y', 'c'), 0, 0, tiled=False)  38.3 us
    ppermute x2, starting transfers between devices, shifted(): return lax.ppermute(value, axis, pairs)  26.6 us
    all_to_all x4, starting transfers between devices, spread_half(): return lax.all_to_all(copies, ('y', 'c'), 0, 0, tiled=False)  24.6 us
    all_to_all x4, waiting for transfers between devices, reduce_half(): spread = lax.all_to_all(summed, 'y', 0, 0, tiled=False)  17.7 us
    all_to_all x4, starting transfers between devices, reduce_half(): spread = lax.all_to_all(summed, 'y', 0, 0, tiled=False)  16.4 us
    ppermute x2, waiting for transfers between devices, shifted(): return lax.ppermute(value, axis, pairs)  15.6 us
    ppermute x4, waiting for transfers between devices, swap_zh(): return lax.ppermute(value, 'zh', [(0, 1), (1, 0)])  13.3 us
  transfers between devices with their start and end apart: 16, of which 11 were waited for; matrix products, arithmetic and copies ran while one was open for 8% of the time, Pallas kernels for 0%

profile of v5, /device:TPU:1, one launch (start us, length us, event | category | flops | bytes accessed | tf_op | source)
XLA Modules:
  0.0 262.3 jit_solution(2579036588017752001)
XLA Ops:
  0.7 2.2 broadcast_in_dim.60
  2.9 10.3 %all-to-all-start = ((bf16[8,384,256]{2,1,0:T(8,128)(2,1)}), bf16[8,384,256]{2,1,0:T(8,128)(2,1)S(1)}, u32[]{:S(2)}, u32[]{:S(2)}) async-start(bf16[8,384,256]{2,1,0:T(8,128)(2,1)} %broadcast_in_dim.60), calls=%async_computation | async-start | bytes 3145728 | tf_op jit(solution)/shard_map/all_to_all | solution.py:41
  13.2 11.1 %collective-permute-start.8 = (bf16[384,256]{1,0:T(8,128)(2,1)S(1)}, bf16[384,256]{1,0:T(8,128)(2,1)S(1)}, u32[]{:S(2)}, u32[]{:S(2)}) collective-permute-start(bf16[384,256]{1,0:T(8,128)(2,1)S(1)} %bitcast.87), channel_id=1, source_target_pairs={{0,8},{8,0},{1,9},{9,1},{2,10},{10,2},{3,11},{11,3},{4,12},{12,4},... | collective-permute-start | bytes 589832 | tf_op jit(solution)/shard_map/ppermute | solution.py:35
  24.3 5.9 %collective-permute-done.8 = bf16[384,256]{1,0:T(8,128)(2,1)S(1)} collective-permute-done((bf16[384,256]{1,0:T(8,128)(2,1)S(1)}, bf16[384,256]{1,0:T(8,128)(2,1)S(1)}, u32[]{:S(2)}, u32[]{:S(2)}) %collective-permute-start.8) | collective-permute-done | bytes 196640 | tf_op jit(solution)/shard_map/ppermute | solution.py:35
  30.2 3.7 %all-to-all-done = bf16[8,384,256]{2,1,0:T(8,128)(2,1)S(1)} async-done(((bf16[8,384,256]{2,1,0:T(8,128)(2,1)}), bf16[8,384,256]{2,1,0:T(8,128)(2,1)S(1)}, u32[]{:S(2)}, u32[]{:S(2)}) %all-to-all-start) | async-done | bytes 1572896 | tf_op jit(solution)/shard_map/all_to_all | solution.py:41
  33.8 1.3 broadcast_in_dim.61
  35.1 4.4 %all-to-all-start.1 = ((bf16[8,384,256]{2,1,0:T(8,128)(2,1)}), bf16[8,384,256]{2,1,0:T(8,128)(2,1)S(1)}, u32[]{:S(2)}, u32[]{:S(2)}) async-start(bf16[8,384,256]{2,1,0:T(8,128)(2,1)} %broadcast_in_dim.61), calls=%async_computation.1 | async-start | bytes 3145728 | tf_op jit(solution)/shard_map/all_to_all | solution.py:41
  39.5 20.6 %all-to-all-done.1 = bf16[8,384,256]{2,1,0:T(8,128)(2,1)S(1)} async-done(((bf16[8,384,256]{2,1,0:T(8,128)(2,1)}), bf16[8,384,256]{2,1,0:T(8,128)(2,1)S(1)}, u32[]{:S(2)}, u32[]{:S(2)}) %all-to-all-start.1) | async-done | bytes 1572896 | tf_op jit(solution)/shard_map/all_to_all | solution.py:41
  60.7 1.6 copy-done.4
  62.3 1.0 fusion.17
  63.4 1.0 broadcast_in_dim.63
  64.4 4.4 %all-to-all-start.3 = ((bf16[8,256,256]{2,1,0:T(8,128)(2,1)}), bf16[8,256,256]{2,1,0:T(8,128)(2,1)S(1)}, u32[]{:S(2)}, u32[]{:S(2)}) async-start(bf16[8,256,256]{2,1,0:T(8,128)(2,1)} %broadcast_in_dim.63), calls=%async_computation.3 | async-start | bytes 2097152 | tf_op jit(solution)/shard_map/all_to_all | solution.py:41
  68.9 11.2 %collective-permute-start.9 = (bf16[256,256]{0,1:T(8,128)(2,1)S(1)}, bf16[256,256]{0,1:T(8,128)(2,1)S(1)}, u32[]{:S(2)}, u32[]{:S(2)}) collective-permute-start(bf16[256,256]{0,1:T(8,128)(2,1)S(1)} %fusion.17), channel_id=1, source_target_pairs={{0,8},{8,0},{1,9},{9,1},{2,10},{10,2},{3,11},{11,3},{4,12},{12,4},... | collective-permute-start | bytes 393224 | tf_op jit(solution)/shard_map/ppermute | solution.py:35
  80.1 4.4 %collective-permute-done.9 = bf16[256,256]{0,1:T(8,128)(2,1)S(1)} collective-permute-done((bf16[256,256]{0,1:T(8,128)(2,1)S(1)}, bf16[256,256]{0,1:T(8,128)(2,1)S(1)}, u32[]{:S(2)}, u32[]{:S(2)}) %collective-permute-start.9) | collective-permute-done | bytes 131104 | tf_op jit(solution)/shard_map/ppermute | solution.py:35
  84.6 1.0 broadcast_in_dim.62
  85.7 5.4 %all-to-all-start.2 = ((bf16[8,256,256]{2,1,0:T(8,128)(2,1)}), bf16[8,256,256]{2,1,0:T(8,128)(2,1)S(1)}, u32[]{:S(2)}, u32[]{:S(2)}) async-start(bf16[8,256,256]{2,1,0:T(8,128)(2,1)} %broadcast_in_dim.62), calls=%async_computation.2 | async-start | bytes 2097152 | tf_op jit(solution)/shard_map/all_to_all | solution.py:41
  92.0 14.0 %all-to-all-done.2 = bf16[8,256,256]{2,1,0:T(8,128)(2,1)S(1)} async-done(((bf16[8,256,256]{2,1,0:T(8,128)(2,1)}), bf16[8,256,256]{2,1,0:T(8,128)(2,1)S(1)}, u32[]{:S(2)}, u32[]{:S(2)}) %all-to-all-start.2) | async-done | bytes 1048608 | tf_op jit(solution)/shard_map/all_to_all | solution.py:41
  106.3 0.3 broadcast_in_dim.58
  106.5 1.2 fusion.39
  107.7 0.3 fusion.9
  108.1 0.8 convolution_convert_fusion
  108.9 0.6 fusion.20
  109.5 0.8 fusion.6
  110.3 0.8 convolution_convert_fusion.1
  111.3 0.3 copy-done.5
  111.6 0.8 reshape.95
  112.4 0.4 copy.63
  112.8 5.2 %all_to_all.60 = bf16[4,2,256,256]{2,0,3,1:T(4,128)(2,1)S(1)} all-to-all(bf16[4,2,256,256]{2,0,3,1:T(4,128)(2,1)S(1)} %copy.63), channel_id=1, replica_groups=mesh['rep'=32,'zh'=2,'y'=4,'c'=2] {'c'}, dimensions={1} | all-to-all | bytes 2097152 | tf_op jit(solution)/shard_map/all_to_all | solution.py:62
  118.0 1.1 reduce_sum.131
  119.1 0.9 copy.65
  120.0 0.8 reshape.94
  120.7 0.4 copy.59
  121.2 4.6 %all_to_all.61 = bf16[4,2,256,256]{2,0,3,1:T(4,128)(2,1)S(1)} all-to-all(bf16[4,2,256,256]{2,0,3,1:T(4,128)(2,1)S(1)} %copy.59), channel_id=1, replica_groups=mesh['rep'=32,'zh'=2,'y'=4,'c'=2] {'c'}, dimensions={1} | all-to-all | bytes 2097152 | tf_op jit(solution)/shard_map/all_to_all | solution.py:62
  125.7 3.6 %all-to-all-start.7 = ((bf16[4,256,256]{1,2,0:T(8,128)(2,1)}), bf16[4,256,256]{1,2,0:T(8,128)(2,1)S(1)}, u32[]{:S(2)}, u32[]{:S(2)}) async-start(bf16[4,256,256]{1,2,0:T(8,128)(2,1)} %copy.65), calls=%async_computation.7 | async-start | bytes 1048576 | tf_op jit(solution)/shard_map/all_to_all | solution.py:64
  129.4 1.1 reduce_sum.129
  130.5 0.9 copy.61
  131.4 7.0 %all-to-all-done.7 = bf16[4,256,256]{1,2,0:T(8,128)(2,1)S(1)} async-done(((bf16[4,256,256]{1,2,0:T(8,128)(2,1)}), bf16[4,256,256]{1,2,0:T(8,128)(2,1)S(1)}, u32[]{:S(2)}, u32[]{:S(2)}) %all-to-all-start.7) | async-done | bytes 524320 | tf_op jit(solution)/shard_map/all_to_all | solution.py:64
  138.4 4.1 %all-to-all-start.5 = ((bf16[4,256,256]{1,2,0:T(8,128)(2,1)}), bf16[4,256,256]{1,2,0:T(8,128)(2,1)}, u32[]{:S(2)}, u32[]{:S(2)}) async-start(bf16[4,256,256]{1,2,0:T(8,128)(2,1)} %copy.61), calls=%async_computation.5 | async-start | bytes 1048576 | tf_op jit(solution)/shard_map/all_to_all | solution.py:64
  142.5 3.2 %copy.53 = bf16[1,256,6144]{1,2,0:T(8,128)(2,1)S(1)} copy(bf16[1,256,6144]{2,1,0:T(8,128)(2,1)} %param.10) | data formatting | bytes 6291456 | tf_op args[0]
  145.7 1.8 reduce_sum.132
  147.5 11.1 %collective-permute-start.10 = (bf16[256,256]{0,1:T(8,128)(2,1)}, bf16[256,256]{0,1:T(8,128)(2,1)}, u32[]{:S(2)}, u32[]{:S(2)}) collective-permute-start(bf16[256,256]{0,1:T(8,128)(2,1)} %reduce_sum.132), channel_id=1, source_target_pairs={{0,8},{8,0},{1,9},{9,1},{2,10},{10,2},{3,11},{11,3},{4,12},{12,4},... | collective-permute-start | bytes 393224 | tf_op jit(solution)/shard_map/ppermute | solution.py:35
  158.6 1.1 convert_reduce_fusion
  159.8 2.5 collective-permute-done.10
  162.3 1.5 convolution_convert_fusion.2
  163.8 1.4 copy.69
  165.1 7.0 %all-to-all-start.10 = ((bf16[4,2,384,256]{3,2,0,1:T(8,128)(2,1)}), bf16[4,2,384,256]{3,2,0,1:T(8,128)(2,1)}, u32[]{:S(2)}, u32[]{:S(2)}) async-start(bf16[4,2,384,256]{3,2,0,1:T(8,128)(2,1)} %copy.69), calls=%async_computation.10 | async-start | bytes 3145728 | tf_op jit(solution)/shard_map/all_to_all | solution.py:62
  172.1 1.5 convolution_convert_fusion.3
  173.6 1.3 copy.67
  174.9 3.7 %all-to-all-start.8 = ((bf16[4,2,384,256]{3,2,0,1:T(8,128)(2,1)}), bf16[4,2,384,256]{3,2,0,1:T(8,128)(2,1)S(1)}, u32[]{:S(2)}, u32[]{:S(2)}) async-start(bf16[4,2,384,256]{3,2,0,1:T(8,128)(2,1)} %copy.67), calls=%async_computation.8 | async-start | bytes 3145728 | tf_op jit(solution)/shard_map/all_to_all | solution.py:62
  178.6 2.8 %reduce_sum.134 = bf16[4,384,256]{2,1,0:T(8,128)(2,1)} reduce(bf16[4,2,384,256]{3,2,0,1:T(8,128)(2,1)} %all-to-all-done.10, bf16[]{:T(256)} %constant.72.clone.1), dimensions={1}, to_apply=%region_8.9 | reduce | flops 393216 | bytes 2359298 | tf_op jit(solution)/shard_map/reduce_sum | solution.py:63
  181.3 4.5 %all-to-all-start.11 = ((bf16[4,384,256]{2,1,0:T(8,128)(2,1)}), bf16[4,384,256]{2,1,0:T(8,128)(2,1)S(1)}, u32[]{:S(2)}, u32[]{:S(2)}) async-start(bf16[4,384,256]{2,1,0:T(8,128)(2,1)} %reduce_sum.134), calls=%async_computation.11 | async-start | bytes 1572864 | tf_op jit(solution)/shard_map/all_to_all | solution.py:64
  185.8 1.4 reduce_sum.133
  187.2 10.7 %all-to-all-done.11 = bf16[4,384,256]{2,1,0:T(8,128)(2,1)S(1)} async-done(((bf16[4,384,256]{2,1,0:T(8,128)(2,1)}), bf16[4,384,256]{2,1,0:T(8,128)(2,1)S(1)}, u32[]{:S(2)}, u32[]{:S(2)}) %all-to-all-start.11) | async-done | bytes 786464 | tf_op jit(solution)/shard_map/all_to_all | solution.py:64
  197.9 4.2 %all-to-all-start.9 = ((bf16[4,384,256]{2,1,0:T(8,128)(2,1)}), bf16[4,384,256]{2,1,0:T(8,128)(2,1)}, u32[]{:S(2)}, u32[]{:S(2)}) async-start(bf16[4,384,256]{2,1,0:T(8,128)(2,1)} %reduce_sum.133), calls=%async_computation.9 | async-start | bytes 1572864 | tf_op jit(solution)/shard_map/all_to_all | solution.py:64
  202.9 11.1 %collective-permute-start.11 = (bf16[384,256]{1,0:T(8,128)(2,1)S(1)}, bf16[384,256]{1,0:T(8,128)(2,1)S(1)}, u32[]{:S(2)}, u32[]{:S(2)}) collective-permute-start(bf16[384,256]{1,0:T(8,128)(2,1)S(1)} %reduce_sum.135), channel_id=1, source_target_pairs={{0,8},{8,0},{1,9},{9,1},{2,10},{10,2},{3,11},{11,3},{4,12},{12,4},... | collective-permute-start | bytes 589832 | tf_op jit(solution)/shard_map/ppermute | solution.py:35
  214.0 3.0 %fusion.21 = bf16[1,256,128]{2,1,0:T(8,128)(2,1)} fusion(bf16[256,4096]{0,1:T(8,128)(2,1)} %copy-done.5, bf16[4096,256]{1,0:T(8,128)(2,1)S(1)} %bitcast.83), kind=kOutput, calls=%fused_computation.36 | convolution fusion | flops 268468224 | bytes 3211264 | tf_op jit(solution)/shard_map/dot_general | solution.py:150
  217.0 1.3 convert_element_type.101
  218.3 0.6 collective-permute-done.11
  218.8 42.5 %conditional.1 = (f32[1,384,256]{2,1,0:T(8,128)S(1)}) conditional(s32[]{:T(128)} %clamp.3, (f32[4,384,256]{2,1,0:T(8,128)S(1)}, f32[384,256]{1,0:T(8,128)S(1)}) %tuple.28, (f32[4,384,256]{2,1,0:T(8,128)S(1)}, f32[384,256]{1,0:T(8,128)S(1)}) %tuple.28, (f32[4,384,256]{2,1,0:T(8,128)S(1)}, ...), branch_computations={%region_10.12_spmd, %region_12.14_spmd, %region_14.16_spmd, %regio... | conditional | flops 983040 | bytes 6094940 | solution.py:169
  219.1 4.1 %collective-permute-start.2 = (bf16[384,256]{1,0:T(8,128)(2,1)S(1)}, bf16[384,256]{1,0:T(8,128)(2,1)S(1)}, u32[]{:S(2)}, u32[]{:S(2)}) collective-permute-start(bf16[384,256]{1,0:T(8,128)(2,1)S(1)} %get-tuple-element.46), channel_id=1, source_target_pairs={{0,32},{16,48},{32,64},{48,80},{64,96},{80,112},{96,128},{112,144}... | collective-permute-start | bytes 589832 | tf_op jit(solution)/shard_map/cond/branch_1_fun/ppermute | solution.py:25
  223.2 22.5 %collective-permute-start.3 = (bf16[384,256]{1,0:T(8,128)(2,1)S(1)}, bf16[384,256]{1,0:T(8,128)(2,1)S(1)}, u32[]{:S(2)}, u32[]{:S(2)}) collective-permute-start(bf16[384,256]{1,0:T(8,128)(2,1)S(1)} %get-tuple-element.46), channel_id=1, source_target_pairs={{0,480},{16,496},{32,0},{48,16},{64,32},{80,48},{96,64},{112,80},{... | collective-permute-start | bytes 589832 | tf_op jit(solution)/shard_map/cond/branch_1_fun/ppermute | solution.py:25
  245.7 11.1 %collective-permute-done.2 = bf16[384,256]{1,0:T(8,128)(2,1)S(1)} collective-permute-done((bf16[384,256]{1,0:T(8,128)(2,1)S(1)}, bf16[384,256]{1,0:T(8,128)(2,1)S(1)}, u32[]{:S(2)}, u32[]{:S(2)}) %collective-permute-start.2) | collective-permute-done | bytes 196640 | tf_op jit(solution)/shard_map/cond/branch_1_fun/ppermute | solution.py:25
  256.9 4.4 %collective-permute-done.3 = bf16[384,256]{1,0:T(8,128)(2,1)S(1)} collective-permute-done((bf16[384,256]{1,0:T(8,128)(2,1)S(1)}, bf16[384,256]{1,0:T(8,128)(2,1)S(1)}, u32[]{:S(2)}, u32[]{:S(2)}) %collective-permute-start.3) | collective-permute-done | bytes 196640 | tf_op jit(solution)/shard_map/cond/branch_1_fun/ppermute | solution.py:25
  261.4 0.7 copy-done.7
  (48 shorter events, 2.7 us)
Async XLA Ops:
  0.6 105.9 %copy-start = (bf16[1,256,128]{2,1,0:T(8,128)(2,1)S(1)}, bf16[1,256,128]{2,1,0:T(8,128)(2,1)}, u32[]{:S(2)}) copy-start(bf16[1,256,128]{2,1,0:T(8,128)(2,1)} %param.11) | copy-start | bytes 196612
  0.6 12.6 %copy-start.9 = (bf16[1,384,256]{2,1,0:T(8,128)(2,1)S(1)}, bf16[1,384,256]{2,1,0:T(8,128)(2,1)}, u32[]{:S(2)}) copy-start(bf16[1,384,256]{2,1,0:T(8,128)(2,1)} %param.13) | copy-start | bytes 589828
  2.9 30.9 %all-to-all-start = ((bf16[8,384,256]{2,1,0:T(8,128)(2,1)}), bf16[8,384,256]{2,1,0:T(8,128)(2,1)S(1)}, u32[]{:S(2)}, u32[]{:S(2)}) async-start(bf16[8,384,256]{2,1,0:T(8,128)(2,1)} %broadcast_in_dim.60), calls=%async_computation | async-start | bytes 3145728 | tf_op jit(solution)/shard_map/all_to_all | solution.py:41
  13.2 16.9 %collective-permute-start.8 = (bf16[384,256]{1,0:T(8,128)(2,1)S(1)}, bf16[384,256]{1,0:T(8,128)(2,1)S(1)}, u32[]{:S(2)}, u32[]{:S(2)}) collective-permute-start(bf16[384,256]{1,0:T(8,128)(2,1)S(1)} %bitcast.87), channel_id=1, source_target_pairs={{0,8},{8,0},{1,9},{9,1},{2,10},{10,2},{3,11},{11,3},{4,12},{12,4},... | collective-permute-start | bytes 589832 | tf_op jit(solution)/shard_map/ppermute | solution.py:35
  35.1 25.1 %all-to-all-start.1 = ((bf16[8,384,256]{2,1,0:T(8,128)(2,1)}), bf16[8,384,256]{2,1,0:T(8,128)(2,1)S(1)}, u32[]{:S(2)}, u32[]{:S(2)}) async-start(bf16[8,384,256]{2,1,0:T(8,128)(2,1)} %broadcast_in_dim.61), calls=%async_computation.1 | async-start | bytes 3145728 | tf_op jit(solution)/shard_map/all_to_all | solution.py:41
  60.4 1.9 copy-start.4
  64.4 20.2 %all-to-all-start.3 = ((bf16[8,256,256]{2,1,0:T(8,128)(2,1)}), bf16[8,256,256]{2,1,0:T(8,128)(2,1)S(1)}, u32[]{:S(2)}, u32[]{:S(2)}) async-start(bf16[8,256,256]{2,1,0:T(8,128)(2,1)} %broadcast_in_dim.63), calls=%async_computation.3 | async-start | bytes 2097152 | tf_op jit(solution)/shard_map/all_to_all | solution.py:41
  68.9 22.4 %copy-start.10 = (s32[64,3]{0,1:T(4,128)S(1)}, s32[64,3]{0,1:T(4,128)}, u32[]{:S(2)}) copy-start(s32[64,3]{0,1:T(4,128)} %param.14) | copy-start | bytes 2308
  68.9 23.0 %copy-start.8 = (bf16[1,256,128]{2,1,0:T(8,128)(2,1)S(1)}, bf16[1,256,128]{2,1,0:T(8,128)(2,1)}, u32[]{:S(2)}) copy-start(bf16[1,256,128]{2,1,0:T(8,128)(2,1)} %param.12) | copy-start | bytes 196612
  68.9 15.6 %collective-permute-start.9 = (bf16[256,256]{0,1:T(8,128)(2,1)S(1)}, bf16[256,256]{0,1:T(8,128)(2,1)S(1)}, u32[]{:S(2)}, u32[]{:S(2)}) collective-permute-start(bf16[256,256]{0,1:T(8,128)(2,1)S(1)} %fusion.17), channel_id=1, source_target_pairs={{0,8},{8,0},{1,9},{9,1},{2,10},{10,2},{3,11},{11,3},{4,12},{12,4},... | collective-permute-start | bytes 393224 | tf_op jit(solution)/shard_map/ppermute | solution.py:35
  85.7 20.4 %all-to-all-start.2 = ((bf16[8,256,256]{2,1,0:T(8,128)(2,1)}), bf16[8,256,256]{2,1,0:T(8,128)(2,1)S(1)}, u32[]{:S(2)}, u32[]{:S(2)}) async-start(bf16[8,256,256]{2,1,0:T(8,128)(2,1)} %broadcast_in_dim.62), calls=%async_computation.2 | async-start | bytes 2097152 | tf_op jit(solution)/shard_map/all_to_all | solution.py:41
  106.2 3.2 %copy-start.2 = (bf16[16,256,256]{2,1,0:T(8,128)(2,1)}, bf16[16,256,256]{2,1,0:T(8,128)(2,1)S(1)}, u32[]{:S(2)}) copy-start(bf16[16,256,256]{2,1,0:T(8,128)(2,1)S(1)} %pad_maximum_fusion.1) | copy-start | bytes 6291460
  110.3 1.3 copy-start.5
  125.7 12.6 %all-to-all-start.7 = ((bf16[4,256,256]{1,2,0:T(8,128)(2,1)}), bf16[4,256,256]{1,2,0:T(8,128)(2,1)S(1)}, u32[]{:S(2)}, u32[]{:S(2)}) async-start(bf16[4,256,256]{1,2,0:T(8,128)(2,1)} %copy.65), calls=%async_computation.7 | async-start | bytes 1048576 | tf_op jit(solution)/shard_map/all_to_all | solution.py:64
  138.4 4.2 %copy-start.6 = (bf16[4,256,256]{1,2,0:T(8,128)(2,1)}, bf16[4,256,256]{1,2,0:T(8,128)(2,1)S(1)}, u32[]{:S(2)}) copy-start(bf16[4,256,256]{1,2,0:T(8,128)(2,1)S(1)} %all-to-all-done.7) | copy-start | bytes 1572868
  138.4 20.2 %all-to-all-start.5 = ((bf16[4,256,256]{1,2,0:T(8,128)(2,1)}), bf16[4,256,256]{1,2,0:T(8,128)(2,1)}, u32[]{:S(2)}, u32[]{:S(2)}) async-start(bf16[4,256,256]{1,2,0:T(8,128)(2,1)} %copy.61), calls=%async_computation.5 | async-start | bytes 1048576 | tf_op jit(solution)/shard_map/all_to_all | solution.py:64
  147.5 14.7 %collective-permute-start.10 = (bf16[256,256]{0,1:T(8,128)(2,1)}, bf16[256,256]{0,1:T(8,128)(2,1)}, u32[]{:S(2)}, u32[]{:S(2)}) collective-permute-start(bf16[256,256]{0,1:T(8,128)(2,1)} %reduce_sum.132), channel_id=1, source_target_pairs={{0,8},{8,0},{1,9},{9,1},{2,10},{10,2},{3,11},{11,3},{4,12},{12,4},... | collective-permute-start | bytes 393224 | tf_op jit(solution)/shard_map/ppermute | solution.py:35
  165.1 9.8 %all-to-all-start.10 = ((bf16[4,2,384,256]{3,2,0,1:T(8,128)(2,1)}), bf16[4,2,384,256]{3,2,0,1:T(8,128)(2,1)}, u32[]{:S(2)}, u32[]{:S(2)}) async-start(bf16[4,2,384,256]{3,2,0,1:T(8,128)(2,1)} %copy.69), calls=%async_computation.10 | async-start | bytes 3145728 | tf_op jit(solution)/shard_map/all_to_all | solution.py:62
  174.9 6.5 %all-to-all-start.8 = ((bf16[4,2,384,256]{3,2,0,1:T(8,128)(2,1)}), bf16[4,2,384,256]{3,2,0,1:T(8,128)(2,1)S(1)}, u32[]{:S(2)}, u32[]{:S(2)}) async-start(bf16[4,2,384,256]{3,2,0,1:T(8,128)(2,1)} %copy.67), calls=%async_computation.8 | async-start | bytes 3145728 | tf_op jit(solution)/shard_map/all_to_all | solution.py:62
  181.3 16.5 %all-to-all-start.11 = ((bf16[4,384,256]{2,1,0:T(8,128)(2,1)}), bf16[4,384,256]{2,1,0:T(8,128)(2,1)S(1)}, u32[]{:S(2)}, u32[]{:S(2)}) async-start(bf16[4,384,256]{2,1,0:T(8,128)(2,1)} %reduce_sum.134), calls=%async_computation.11 | async-start | bytes 1572864 | tf_op jit(solution)/shard_map/all_to_all | solution.py:64
  187.2 26.8 %copy-start.3 = (bf16[16,256,256]{2,1,0:T(8,128)(2,1)S(1)}, bf16[16,256,256]{2,1,0:T(8,128)(2,1)}, u32[]{:S(2)}) copy-start(bf16[16,256,256]{2,1,0:T(8,128)(2,1)} %copy-done.2) | copy-start | bytes 6291460
  197.9 19.1 %all-to-all-start.9 = ((bf16[4,384,256]{2,1,0:T(8,128)(2,1)}), bf16[4,384,256]{2,1,0:T(8,128)(2,1)}, u32[]{:S(2)}, u32[]{:S(2)}) async-start(bf16[4,384,256]{2,1,0:T(8,128)(2,1)} %reduce_sum.133), calls=%async_computation.9 | async-start | bytes 1572864 | tf_op jit(solution)/shard_map/all_to_all | solution.py:64
  202.9 15.9 %collective-permute-start.11 = (bf16[384,256]{1,0:T(8,128)(2,1)S(1)}, bf16[384,256]{1,0:T(8,128)(2,1)S(1)}, u32[]{:S(2)}, u32[]{:S(2)}) collective-permute-start(bf16[384,256]{1,0:T(8,128)(2,1)S(1)} %reduce_sum.135), channel_id=1, source_target_pairs={{0,8},{8,0},{1,9},{9,1},{2,10},{10,2},{3,11},{11,3},{4,12},{12,4},... | collective-permute-start | bytes 589832 | tf_op jit(solution)/shard_map/ppermute | solution.py:35
  219.1 37.8 %collective-permute-start.2 = (bf16[384,256]{1,0:T(8,128)(2,1)S(1)}, bf16[384,256]{1,0:T(8,128)(2,1)S(1)}, u32[]{:S(2)}, u32[]{:S(2)}) collective-permute-start(bf16[384,256]{1,0:T(8,128)(2,1)S(1)} %get-tuple-element.46), channel_id=1, source_target_pairs={{0,32},{16,48},{32,64},{48,80},{64,96},{80,112},{96,128},{112,144}... | collective-permute-start | bytes 589832 | tf_op jit(solution)/shard_map/cond/branch_1_fun/ppermute | solution.py:25
  223.2 38.1 %collective-permute-start.3 = (bf16[384,256]{1,0:T(8,128)(2,1)S(1)}, bf16[384,256]{1,0:T(8,128)(2,1)S(1)}, u32[]{:S(2)}, u32[]{:S(2)}) collective-permute-start(bf16[384,256]{1,0:T(8,128)(2,1)S(1)} %get-tuple-element.46), channel_id=1, source_target_pairs={{0,480},{16,496},{32,0},{48,16},{64,32},{80,48},{96,64},{112,80},{... | collective-permute-start | bytes 589832 | tf_op jit(solution)/shard_map/cond/branch_1_fun/ppermute | solution.py:25
  261.4 0.7 copy-start.7
  261.4 0.9 copy-start.1

commit v6 on v5

--- a/solution.py
+++ b/solution.py
@@ -59,8 +59,11 @@
 
 
 def reduce_half(part):
-    paired = lax.all_to_all(part, "c", 1, 1, tiled=False)
-    summed = jnp.sum(paired.astype(jnp.float32), axis=1).astype(jnp.bfloat16)
+    first_core = lax.axis_index("c") == 0
+    keep = jnp.where(first_core, part[:, 0], part[:, 1])
+    send = jnp.where(first_core, part[:, 1], part[:, 0])
+    got = lax.ppermute(send, "c", [(0, 1), (1, 0)])
+    summed = (keep.astype(jnp.float32) + got.astype(jnp.float32)).astype(jnp.bfloat16)
     spread = lax.all_to_all(summed, "y", 0, 0, tiled=False)
     return jnp.sum(spread.astype(jnp.float32), axis=0)
 

time: 266 us -> 267 us (level)
  blocking collectives: 9.75 us -> 0 us
  local copies, waits for them, and re-layouts: 19.4 us -> 27.3 us
    ppermute x0 -> x4, starting transfers between devices: none -> 11.1 us  [reduce_half(): got = lax.ppermute(send, 'c', [(0, 1), (1, 0)])]
    all_to_all x2 -> x0, starting transfers between devices: 10.7 us -> none  [reduce_half(): paired = lax.all_to_all(part, 'c', 1, 1, tiled=False)]
    all_to_all x2 -> x0, blocking collectives: 9.75 us -> none  [reduce_half(): paired = lax.all_to_all(part, 'c', 1, 1, tiled=False)]
    unnamed x24 -> x30, local copies, waits for them, and re-layouts: 6.13 us -> 14.2 us
    convert_element_type x0 -> x4, other arithmetic: none -> 7.71 us  [reduce_half(): (keep.astype(jnp.float32) + got.astype(jnp.float32)).astype(jnp.bfloat16)]
    reduce_sum x4 -> x0, other arithmetic: 6.39 us -> none  [reduce_half(): summed = jnp.sum(paired.astype(jnp.float32), axis=1).astype(jnp.bfloat16)]
    slice x0 -> x2, local copies, waits for them, and re-layouts: none -> 4.8 us  [reduce_half(): keep = jnp.where(first_core, part[:, 0], part[:, 1])]
    select_n x0 -> x4, other arithmetic: none -> 2.97 us  [reduce_half(): send = jnp.where(first_core, part[:, 1], part[:, 0])]
  transfers between devices with their start and end apart: 16 -> 18, of which waited for: 11 -> 11; matrix products, arithmetic and copies ran while one was open for 8% -> 10% of each run, Pallas kernels for 0% -> 0%
where the time goes in v6:
time: 267 us; the launch traced here: 263 us
  starting transfers between devices  122 us (46%)
  waiting for transfers between devices  86.4 us (32%)
  local copies, waits for them, and re-layouts  27.3 us (10%)
  other arithmetic  14 us (5%)
  matrix products  12.1 us (5%)
    ppermute x4, starting transfers between devices, swap_zh(): return lax.ppermute(value, 'zh', [(0, 1), (1, 0)])  44.6 us
    all_to_all x4, waiting for transfers between devices, spread_half(): return lax.all_to_all(copies, ('y', 'c'), 0, 0, tiled=False)  38.3 us
    ppermute x2, starting transfers between devices, shifted(): return lax.ppermute(value, axis, pairs)  26.5 us
    all_to_all x4, starting transfers between devices, spread_half(): return lax.all_to_all(copies, ('y', 'c'), 0, 0, tiled=False)  24.6 us
    all_to_all x4, waiting for transfers between devices, reduce_half(): spread = lax.all_to_all(summed, 'y', 0, 0, tiled=False)  17.4 us
    ppermute x2, waiting for transfers between devices, shifted(): return lax.ppermute(value, axis, pairs)  16.2 us
    all_to_all x4, starting transfers between devices, reduce_half(): spread = lax.all_to_all(summed, 'y', 0, 0, tiled=False)  14.9 us
    ppermute x4, waiting for transfers between devices, swap_zh(): return lax.ppermute(value, 'zh', [(0, 1), (1, 0)])  14.5 us
  transfers between devices with their start and end apart: 18, of which 11 were waited for; matrix products, arithmetic and copies ran while one was open for 10% of the time, Pallas kernels for 0%

profile of v6, /device:TPU:1, one launch (start us, length us, event | category | flops | bytes accessed | tf_op | source)
XLA Modules:
  0.0 263.4 jit_solution(10322881446498219289)
XLA Ops:
  0.7 2.3 broadcast_in_dim.60
  2.9 10.3 %all-to-all-start = ((bf16[8,384,256]{2,1,0:T(8,128)(2,1)}), bf16[8,384,256]{2,1,0:T(8,128)(2,1)S(1)}, u32[]{:S(2)}, u32[]{:S(2)}) async-start(bf16[8,384,256]{2,1,0:T(8,128)(2,1)} %broadcast_in_dim.60), calls=%async_computation | async-start | bytes 3145728 | tf_op jit(solution)/shard_map/all_to_all | solution.py:41
  13.3 11.1 %collective-permute-start.8 = (bf16[384,256]{1,0:T(8,128)(2,1)S(1)}, bf16[384,256]{1,0:T(8,128)(2,1)S(1)}, u32[]{:S(2)}, u32[]{:S(2)}) collective-permute-start(bf16[384,256]{1,0:T(8,128)(2,1)S(1)} %bitcast.133), channel_id=1, source_target_pairs={{0,8},{8,0},{1,9},{9,1},{2,10},{10,2},{3,11},{11,3},{4,12},{12,4},... | collective-permute-start | bytes 589832 | tf_op jit(solution)/shard_map/ppermute | solution.py:35
  24.3 5.9 %collective-permute-done.8 = bf16[384,256]{1,0:T(8,128)(2,1)S(1)} collective-permute-done((bf16[384,256]{1,0:T(8,128)(2,1)S(1)}, bf16[384,256]{1,0:T(8,128)(2,1)S(1)}, u32[]{:S(2)}, u32[]{:S(2)}) %collective-permute-start.8) | collective-permute-done | bytes 196640 | tf_op jit(solution)/shard_map/ppermute | solution.py:35
  30.2 3.7 %all-to-all-done = bf16[8,384,256]{2,1,0:T(8,128)(2,1)S(1)} async-done(((bf16[8,384,256]{2,1,0:T(8,128)(2,1)}), bf16[8,384,256]{2,1,0:T(8,128)(2,1)S(1)}, u32[]{:S(2)}, u32[]{:S(2)}) %all-to-all-start) | async-done | bytes 1572896 | tf_op jit(solution)/shard_map/all_to_all | solution.py:41
  33.9 1.3 broadcast_in_dim.61
  35.2 4.4 %all-to-all-start.1 = ((bf16[8,384,256]{2,1,0:T(8,128)(2,1)}), bf16[8,384,256]{2,1,0:T(8,128)(2,1)S(1)}, u32[]{:S(2)}, u32[]{:S(2)}) async-start(bf16[8,384,256]{2,1,0:T(8,128)(2,1)} %broadcast_in_dim.61), calls=%async_computation.1 | async-start | bytes 3145728 | tf_op jit(solution)/shard_map/all_to_all | solution.py:41
  39.6 20.6 %all-to-all-done.1 = bf16[8,384,256]{2,1,0:T(8,128)(2,1)S(1)} async-done(((bf16[8,384,256]{2,1,0:T(8,128)(2,1)}), bf16[8,384,256]{2,1,0:T(8,128)(2,1)S(1)}, u32[]{:S(2)}, u32[]{:S(2)}) %all-to-all-start.1) | async-done | bytes 1572896 | tf_op jit(solution)/shard_map/all_to_all | solution.py:41
  60.7 1.6 copy-done.5
  62.3 1.0 fusion.19
  63.5 1.1 broadcast_in_dim.63
  64.5 4.4 %all-to-all-start.3 = ((bf16[8,256,256]{2,1,0:T(8,128)(2,1)}), bf16[8,256,256]{2,1,0:T(8,128)(2,1)S(1)}, u32[]{:S(2)}, u32[]{:S(2)}) async-start(bf16[8,256,256]{2,1,0:T(8,128)(2,1)} %broadcast_in_dim.63), calls=%async_computation.3 | async-start | bytes 2097152 | tf_op jit(solution)/shard_map/all_to_all | solution.py:41
  69.0 11.2 %collective-permute-start.9 = (bf16[256,256]{0,1:T(8,128)(2,1)S(1)}, bf16[256,256]{0,1:T(8,128)(2,1)S(1)}, u32[]{:S(2)}, u32[]{:S(2)}) collective-permute-start(bf16[256,256]{0,1:T(8,128)(2,1)S(1)} %fusion.19), channel_id=1, source_target_pairs={{0,8},{8,0},{1,9},{9,1},{2,10},{10,2},{3,11},{11,3},{4,12},{12,4},... | collective-permute-start | bytes 393224 | tf_op jit(solution)/shard_map/ppermute | solution.py:35
  80.3 4.4 %collective-permute-done.9 = bf16[256,256]{0,1:T(8,128)(2,1)S(1)} collective-permute-done((bf16[256,256]{0,1:T(8,128)(2,1)S(1)}, bf16[256,256]{0,1:T(8,128)(2,1)S(1)}, u32[]{:S(2)}, u32[]{:S(2)}) %collective-permute-start.9) | collective-permute-done | bytes 131104 | tf_op jit(solution)/shard_map/ppermute | solution.py:35
  84.7 1.1 broadcast_in_dim.62
  85.8 5.4 %all-to-all-start.2 = ((bf16[8,256,256]{2,1,0:T(8,128)(2,1)}), bf16[8,256,256]{2,1,0:T(8,128)(2,1)S(1)}, u32[]{:S(2)}, u32[]{:S(2)}) async-start(bf16[8,256,256]{2,1,0:T(8,128)(2,1)} %broadcast_in_dim.62), calls=%async_computation.2 | async-start | bytes 2097152 | tf_op jit(solution)/shard_map/all_to_all | solution.py:41
  92.2 14.0 %all-to-all-done.2 = bf16[8,256,256]{2,1,0:T(8,128)(2,1)S(1)} async-done(((bf16[8,256,256]{2,1,0:T(8,128)(2,1)}), bf16[8,256,256]{2,1,0:T(8,128)(2,1)S(1)}, u32[]{:S(2)}, u32[]{:S(2)}) %all-to-all-start.2) | async-done | bytes 1048608 | tf_op jit(solution)/shard_map/all_to_all | solution.py:41
  106.7 1.2 fusion.45
  107.9 0.3 fusion.9
  108.2 0.8 convolution_convert_fusion
  109.0 0.6 fusion.22
  109.6 0.8 fusion.6
  110.4 0.8 convolution_convert_fusion.1
  111.4 0.3 copy-done.6
  111.8 0.8 reshape.119
  112.6 2.5 fusion.43
  115.1 2.4 copy.66
  117.5 0.9 copy.67
  118.4 0.9 select_bitcast_fusion.2
  119.3 2.9 %collective-permute-start.11 = (bf16[4,256,256]{2,1,0:T(8,128)(2,1)}, bf16[4,256,256]{2,1,0:T(8,128)(2,1)}, u32[]{:S(2)}, u32[]{:S(2)}) collective-permute-start(bf16[4,256,256]{2,1,0:T(8,128)(2,1)} %select_bitcast_fusion.2), channel_id=1, source_target_pairs={{0,1},{1,0},{2,3},{3,2},{4,5},{5,4},{6,7},{7,6},{8,9},{9,8},{10,11... | collective-permute-start | bytes 1572872 | tf_op jit(solution)/shard_map/ppermute | solution.py:65
  122.1 0.8 reshape.118
  122.9 2.3 fusion.44
  125.2 2.3 copy.64
  127.6 0.9 copy.65
  128.6 1.9 collective-permute-start.10
  130.5 2.0 fusion.25
  132.5 3.5 %all-to-all-start.5 = ((bf16[4,256,256]{2,1,0:T(8,128)(2,1)}), bf16[4,256,256]{2,1,0:T(8,128)(2,1)S(1)}, u32[]{:S(2)}, u32[]{:S(2)}) async-start(bf16[4,256,256]{2,1,0:T(8,128)(2,1)} %fusion.25), calls=%async_computation.5 | async-start | bytes 1048576 | tf_op jit(solution)/shard_map/all_to_all | solution.py:67
  136.0 1.0 fusion.26
  137.0 8.0 %all-to-all-done.5 = bf16[4,256,256]{2,1,0:T(8,128)(2,1)S(1)} async-done(((bf16[4,256,256]{2,1,0:T(8,128)(2,1)}), bf16[4,256,256]{2,1,0:T(8,128)(2,1)S(1)}, u32[]{:S(2)}, u32[]{:S(2)}) %all-to-all-start.5) | async-done | bytes 524320 | tf_op jit(solution)/shard_map/all_to_all | solution.py:67
  145.0 3.5 %all-to-all-start.4 = ((bf16[4,256,256]{2,1,0:T(8,128)(2,1)}), bf16[4,256,256]{2,1,0:T(8,128)(2,1)S(1)}, u32[]{:S(2)}, u32[]{:S(2)}) async-start(bf16[4,256,256]{2,1,0:T(8,128)(2,1)} %fusion.26), calls=%async_computation.4 | async-start | bytes 1048576 | tf_op jit(solution)/shard_map/all_to_all | solution.py:67
  148.5 4.7 %copy.49 = bf16[1,256,6144]{1,2,0:T(8,128)(2,1)} copy(bf16[1,256,6144]{2,1,0:T(8,128)(2,1)} %param.10) | data formatting | bytes 6291456 | tf_op args[0]
  153.3 11.3 %collective-permute-start.12 = (bf16[256,256]{1,0:T(8,128)(2,1)S(1)}, bf16[256,256]{1,0:T(8,128)(2,1)S(1)}, u32[]{:S(2)}, u32[]{:S(2)}) collective-permute-start(bf16[256,256]{1,0:T(8,128)(2,1)S(1)} %reduce_sum.82), channel_id=1, source_target_pairs={{0,8},{8,0},{1,9},{9,1},{2,10},{10,2},{3,11},{11,3},{4,12},{12,4},... | collective-permute-start | bytes 393224 | tf_op jit(solution)/shard_map/ppermute | solution.py:35
  164.6 3.1 %collective-permute-done.12 = bf16[256,256]{1,0:T(8,128)(2,1)S(1)} collective-permute-done((bf16[256,256]{1,0:T(8,128)(2,1)S(1)}, bf16[256,256]{1,0:T(8,128)(2,1)S(1)}, u32[]{:S(2)}, u32[]{:S(2)}) %collective-permute-start.12) | collective-permute-done | bytes 131104 | tf_op jit(solution)/shard_map/ppermute | solution.py:35
  167.7 2.0 convolution_convert_fusion.2
  169.7 1.0 select_bitcast_fusion
  170.7 4.4 %collective-permute-start.14 = (bf16[4,384,256]{2,1,0:T(8,128)(2,1)}, bf16[4,384,256]{2,1,0:T(8,128)(2,1)}, u32[]{:S(2)}, u32[]{:S(2)}) collective-permute-start(bf16[4,384,256]{2,1,0:T(8,128)(2,1)} %select_bitcast_fusion), channel_id=1, source_target_pairs={{0,1},{1,0},{2,3},{3,2},{4,5},{5,4},{6,7},{7,6},{8,9},{9,8},{10,11... | collective-permute-start | bytes 2359304 | tf_op jit(solution)/shard_map/ppermute | solution.py:65
  175.2 2.0 convolution_convert_fusion.3
  177.1 1.0 select_bitcast_fusion.1
  178.2 1.9 collective-permute-start.13
  180.1 2.3 fusion.12
  182.4 4.5 %all-to-all-start.7 = ((bf16[4,384,256]{2,1,0:T(8,128)(2,1)}), bf16[4,384,256]{2,1,0:T(8,128)(2,1)}, u32[]{:S(2)}, u32[]{:S(2)}) async-start(bf16[4,384,256]{2,1,0:T(8,128)(2,1)} %fusion.12), calls=%async_computation.7 | async-start | bytes 1572864 | tf_op jit(solution)/shard_map/all_to_all | solution.py:67
  186.9 2.4 fusion.13
  189.3 9.3 %all-to-all-done.7 = bf16[4,384,256]{2,1,0:T(8,128)(2,1)} async-done(((bf16[4,384,256]{2,1,0:T(8,128)(2,1)}), bf16[4,384,256]{2,1,0:T(8,128)(2,1)}, u32[]{:S(2)}, u32[]{:S(2)}) %all-to-all-start.7) | async-done | bytes 786464 | tf_op jit(solution)/shard_map/all_to_all | solution.py:67
  198.6 3.5 %all-to-all-start.6 = ((bf16[4,384,256]{2,1,0:T(8,128)(2,1)}), bf16[4,384,256]{2,1,0:T(8,128)(2,1)S(1)}, u32[]{:S(2)}, u32[]{:S(2)}) async-start(bf16[4,384,256]{2,1,0:T(8,128)(2,1)} %fusion.13), calls=%async_computation.6 | async-start | bytes 1572864 | tf_op jit(solution)/shard_map/all_to_all | solution.py:67
  202.8 1.3 reduce_sum.83
  204.1 11.1 %collective-permute-start.15 = (bf16[384,256]{1,0:T(8,128)(2,1)S(1)}, bf16[384,256]{1,0:T(8,128)(2,1)S(1)}, u32[]{:S(2)}, u32[]{:S(2)}) collective-permute-start(bf16[384,256]{1,0:T(8,128)(2,1)S(1)} %reduce_sum.83), channel_id=1, source_target_pairs={{0,8},{8,0},{1,9},{9,1},{2,10},{10,2},{3,11},{11,3},{4,12},{12,4},... | collective-permute-start | bytes 589832 | tf_op jit(solution)/shard_map/ppermute | solution.py:35
  215.2 3.0 %fusion.23 = bf16[1,256,128]{2,1,0:T(8,128)(2,1)} fusion(bf16[256,4096]{0,1:T(8,128)(2,1)} %copy-done.6, bf16[4096,256]{1,0:T(8,128)(2,1)S(1)} %bitcast.129), kind=kOutput, calls=%fused_computation.40 | convolution fusion | flops 268468224 | bytes 3211264 | tf_op jit(solution)/shard_map/dot_general | solution.py:153
  218.3 1.2 collective-permute-done.15
  219.5 42.9 %conditional.1 = (f32[1,384,256]{2,1,0:T(8,128)S(1)}) conditional(s32[]{:T(128)} %clamp.3, (f32[4,384,256]{2,1,0:T(8,128)S(1)}, f32[384,256]{1,0:T(8,128)S(1)}) %tuple.28, (f32[4,384,256]{2,1,0:T(8,128)S(1)}, f32[384,256]{1,0:T(8,128)S(1)}) %tuple.28, (f32[4,384,256]{2,1,0:T(8,128)S(1)}, ...), branch_computations={%region_6.8_spmd, %region_8.10_spmd, %region_10.12_spmd, %region_1... | conditional | flops 983040 | bytes 6094940 | solution.py:172
  219.8 3.7 %collective-permute-start.2 = (bf16[384,256]{1,0:T(8,128)(2,1)S(1)}, bf16[384,256]{1,0:T(8,128)(2,1)S(1)}, u32[]{:S(2)}, u32[]{:S(2)}) collective-permute-start(bf16[384,256]{1,0:T(8,128)(2,1)S(1)} %get-tuple-element.46), channel_id=1, source_target_pairs={{0,32},{16,48},{32,64},{48,80},{64,96},{80,112},{96,128},{112,144}... | collective-permute-start | bytes 589832 | tf_op jit(solution)/shard_map/cond/branch_1_fun/ppermute | solution.py:25
  223.5 22.8 %collective-permute-start.3 = (bf16[384,256]{1,0:T(8,128)(2,1)S(1)}, bf16[384,256]{1,0:T(8,128)(2,1)S(1)}, u32[]{:S(2)}, u32[]{:S(2)}) collective-permute-start(bf16[384,256]{1,0:T(8,128)(2,1)S(1)} %get-tuple-element.46), channel_id=1, source_target_pairs={{0,480},{16,496},{32,0},{48,16},{64,32},{80,48},{96,64},{112,80},{... | collective-permute-start | bytes 589832 | tf_op jit(solution)/shard_map/cond/branch_1_fun/ppermute | solution.py:25
  246.2 11.8 %collective-permute-done.2 = bf16[384,256]{1,0:T(8,128)(2,1)S(1)} collective-permute-done((bf16[384,256]{1,0:T(8,128)(2,1)S(1)}, bf16[384,256]{1,0:T(8,128)(2,1)S(1)}, u32[]{:S(2)}, u32[]{:S(2)}) %collective-permute-start.2) | collective-permute-done | bytes 196640 | tf_op jit(solution)/shard_map/cond/branch_1_fun/ppermute | solution.py:25
  258.0 4.4 %collective-permute-done.3 = bf16[384,256]{1,0:T(8,128)(2,1)S(1)} collective-permute-done((bf16[384,256]{1,0:T(8,128)(2,1)S(1)}, bf16[384,256]{1,0:T(8,128)(2,1)S(1)}, u32[]{:S(2)}, u32[]{:S(2)}) %collective-permute-start.3) | collective-permute-done | bytes 196640 | tf_op jit(solution)/shard_map/cond/branch_1_fun/ppermute | solution.py:25
  262.5 0.7 copy-done.8
  (56 shorter events, 3.1 us)
Async XLA Ops:
  0.6 106.1 %copy-start = (bf16[1,256,128]{2,1,0:T(8,128)(2,1)S(1)}, bf16[1,256,128]{2,1,0:T(8,128)(2,1)}, u32[]{:S(2)}) copy-start(bf16[1,256,128]{2,1,0:T(8,128)(2,1)} %param.11) | copy-start | bytes 196612
  0.6 12.6 %copy-start.10 = (bf16[1,384,256]{2,1,0:T(8,128)(2,1)S(1)}, bf16[1,384,256]{2,1,0:T(8,128)(2,1)}, u32[]{:S(2)}) copy-start(bf16[1,384,256]{2,1,0:T(8,128)(2,1)} %param.13) | copy-start | bytes 589828
  2.9 30.9 %all-to-all-start = ((bf16[8,384,256]{2,1,0:T(8,128)(2,1)}), bf16[8,384,256]{2,1,0:T(8,128)(2,1)S(1)}, u32[]{:S(2)}, u32[]{:S(2)}) async-start(bf16[8,384,256]{2,1,0:T(8,128)(2,1)} %broadcast_in_dim.60), calls=%async_computation | async-start | bytes 3145728 | tf_op jit(solution)/shard_map/all_to_all | solution.py:41
  13.3 16.9 %collective-permute-start.8 = (bf16[384,256]{1,0:T(8,128)(2,1)S(1)}, bf16[384,256]{1,0:T(8,128)(2,1)S(1)}, u32[]{:S(2)}, u32[]{:S(2)}) collective-permute-start(bf16[384,256]{1,0:T(8,128)(2,1)S(1)} %bitcast.133), channel_id=1, source_target_pairs={{0,8},{8,0},{1,9},{9,1},{2,10},{10,2},{3,11},{11,3},{4,12},{12,4},... | collective-permute-start | bytes 589832 | tf_op jit(solution)/shard_map/ppermute | solution.py:35
  35.2 25.1 %all-to-all-start.1 = ((bf16[8,384,256]{2,1,0:T(8,128)(2,1)}), bf16[8,384,256]{2,1,0:T(8,128)(2,1)S(1)}, u32[]{:S(2)}, u32[]{:S(2)}) async-start(bf16[8,384,256]{2,1,0:T(8,128)(2,1)} %broadcast_in_dim.61), calls=%async_computation.1 | async-start | bytes 3145728 | tf_op jit(solution)/shard_map/all_to_all | solution.py:41
  60.4 1.9 copy-start.5
  64.5 20.2 %all-to-all-start.3 = ((bf16[8,256,256]{2,1,0:T(8,128)(2,1)}), bf16[8,256,256]{2,1,0:T(8,128)(2,1)S(1)}, u32[]{:S(2)}, u32[]{:S(2)}) async-start(bf16[8,256,256]{2,1,0:T(8,128)(2,1)} %broadcast_in_dim.63), calls=%async_computation.3 | async-start | bytes 2097152 | tf_op jit(solution)/shard_map/all_to_all | solution.py:41
  69.0 22.5 %copy-start.11 = (s32[64,3]{0,1:T(4,128)S(1)}, s32[64,3]{0,1:T(4,128)}, u32[]{:S(2)}) copy-start(s32[64,3]{0,1:T(4,128)} %param.14) | copy-start | bytes 2308
  69.0 23.1 %copy-start.9 = (bf16[1,256,128]{2,1,0:T(8,128)(2,1)S(1)}, bf16[1,256,128]{2,1,0:T(8,128)(2,1)}, u32[]{:S(2)}) copy-start(bf16[1,256,128]{2,1,0:T(8,128)(2,1)} %param.12) | copy-start | bytes 196612
  69.0 15.6 %collective-permute-start.9 = (bf16[256,256]{0,1:T(8,128)(2,1)S(1)}, bf16[256,256]{0,1:T(8,128)(2,1)S(1)}, u32[]{:S(2)}, u32[]{:S(2)}) collective-permute-start(bf16[256,256]{0,1:T(8,128)(2,1)S(1)} %fusion.19), channel_id=1, source_target_pairs={{0,8},{8,0},{1,9},{9,1},{2,10},{10,2},{3,11},{11,3},{4,12},{12,4},... | collective-permute-start | bytes 393224 | tf_op jit(solution)/shard_map/ppermute | solution.py:35
  85.8 20.4 %all-to-all-start.2 = ((bf16[8,256,256]{2,1,0:T(8,128)(2,1)}), bf16[8,256,256]{2,1,0:T(8,128)(2,1)S(1)}, u32[]{:S(2)}, u32[]{:S(2)}) async-start(bf16[8,256,256]{2,1,0:T(8,128)(2,1)} %broadcast_in_dim.62), calls=%async_computation.2 | async-start | bytes 2097152 | tf_op jit(solution)/shard_map/all_to_all | solution.py:41
  106.4 3.2 %copy-start.2 = (bf16[16,256,256]{2,1,0:T(8,128)(2,1)}, bf16[16,256,256]{2,1,0:T(8,128)(2,1)S(1)}, u32[]{:S(2)}) copy-start(bf16[16,256,256]{2,1,0:T(8,128)(2,1)S(1)} %pad_maximum_fusion.1) | copy-start | bytes 6291460
  110.4 1.4 copy-start.6
  115.1 2.4 copy-start.4
  119.3 11.2 %collective-permute-start.11 = (bf16[4,256,256]{2,1,0:T(8,128)(2,1)}, bf16[4,256,256]{2,1,0:T(8,128)(2,1)}, u32[]{:S(2)}, u32[]{:S(2)}) collective-permute-start(bf16[4,256,256]{2,1,0:T(8,128)(2,1)} %select_bitcast_fusion.2), channel_id=1, source_target_pairs={{0,1},{1,0},{2,3},{3,2},{4,5},{5,4},{6,7},{7,6},{8,9},{9,8},{10,11... | collective-permute-start | bytes 1572872 | tf_op jit(solution)/shard_map/ppermute | solution.py:65
  128.6 7.5 %collective-permute-start.10 = (bf16[4,256,256]{2,1,0:T(8,128)(2,1)S(1)}, bf16[4,256,256]{2,1,0:T(8,128)(2,1)S(1)}, u32[]{:S(2)}, u32[]{:S(2)}) collective-permute-start(bf16[4,256,256]{2,1,0:T(8,128)(2,1)S(1)} %select_bitcast_fusion.3), channel_id=1, source_target_pairs={{0,1},{1,0},{2,3},{3,2},{4,5},{5,4},{6,7},{7,6},{8,9},{9,8},{10,11... | collective-permute-start | bytes 1572872 | tf_op jit(solution)/shard_map/ppermute | solution.py:65
  132.5 12.5 %all-to-all-start.5 = ((bf16[4,256,256]{2,1,0:T(8,128)(2,1)}), bf16[4,256,256]{2,1,0:T(8,128)(2,1)S(1)}, u32[]{:S(2)}, u32[]{:S(2)}) async-start(bf16[4,256,256]{2,1,0:T(8,128)(2,1)} %fusion.25), calls=%async_computation.5 | async-start | bytes 1048576 | tf_op jit(solution)/shard_map/all_to_all | solution.py:67
  145.0 19.5 %all-to-all-start.4 = ((bf16[4,256,256]{2,1,0:T(8,128)(2,1)}), bf16[4,256,256]{2,1,0:T(8,128)(2,1)S(1)}, u32[]{:S(2)}, u32[]{:S(2)}) async-start(bf16[4,256,256]{2,1,0:T(8,128)(2,1)} %fusion.26), calls=%async_computation.4 | async-start | bytes 1048576 | tf_op jit(solution)/shard_map/all_to_all | solution.py:67
  153.3 14.4 %collective-permute-start.12 = (bf16[256,256]{1,0:T(8,128)(2,1)S(1)}, bf16[256,256]{1,0:T(8,128)(2,1)S(1)}, u32[]{:S(2)}, u32[]{:S(2)}) collective-permute-start(bf16[256,256]{1,0:T(8,128)(2,1)S(1)} %reduce_sum.82), channel_id=1, source_target_pairs={{0,8},{8,0},{1,9},{9,1},{2,10},{10,2},{3,11},{11,3},{4,12},{12,4},... | collective-permute-start | bytes 393224 | tf_op jit(solution)/shard_map/ppermute | solution.py:35
  167.7 3.1 %copy-start.7 = (bf16[256,256]{1,0:T(8,128)(2,1)}, bf16[256,256]{1,0:T(8,128)(2,1)S(1)}, u32[]{:S(2)}) copy-start(bf16[256,256]{1,0:T(8,128)(2,1)S(1)} %collective-permute-done.12) | copy-start | bytes 393220
  170.7 9.4 %collective-permute-start.14 = (bf16[4,384,256]{2,1,0:T(8,128)(2,1)}, bf16[4,384,256]{2,1,0:T(8,128)(2,1)}, u32[]{:S(2)}, u32[]{:S(2)}) collective-permute-start(bf16[4,384,256]{2,1,0:T(8,128)(2,1)} %select_bitcast_fusion), channel_id=1, source_target_pairs={{0,1},{1,0},{2,3},{3,2},{4,5},{5,4},{6,7},{7,6},{8,9},{9,8},{10,11... | collective-permute-start | bytes 2359304 | tf_op jit(solution)/shard_map/ppermute | solution.py:65
  178.2 8.7 %collective-permute-start.13 = (bf16[4,384,256]{2,1,0:T(8,128)(2,1)}, bf16[4,384,256]{2,1,0:T(8,128)(2,1)}, u32[]{:S(2)}, u32[]{:S(2)}) collective-permute-start(bf16[4,384,256]{2,1,0:T(8,128)(2,1)} %select_bitcast_fusion.1), channel_id=1, source_target_pairs={{0,1},{1,0},{2,3},{3,2},{4,5},{5,4},{6,7},{7,6},{8,9},{9,8},{10,11... | collective-permute-start | bytes 2359304 | tf_op jit(solution)/shard_map/ppermute | solution.py:65
  182.4 16.2 %all-to-all-start.7 = ((bf16[4,384,256]{2,1,0:T(8,128)(2,1)}), bf16[4,384,256]{2,1,0:T(8,128)(2,1)}, u32[]{:S(2)}, u32[]{:S(2)}) async-start(bf16[4,384,256]{2,1,0:T(8,128)(2,1)} %fusion.12), calls=%async_computation.7 | async-start | bytes 1572864 | tf_op jit(solution)/shard_map/all_to_all | solution.py:67
  189.3 25.9 %copy-start.3 = (bf16[16,256,256]{2,1,0:T(8,128)(2,1)S(1)}, bf16[16,256,256]{2,1,0:T(8,128)(2,1)}, u32[]{:S(2)}) copy-start(bf16[16,256,256]{2,1,0:T(8,128)(2,1)} %copy-done.2) | copy-start | bytes 6291460
  198.6 19.5 %all-to-all-start.6 = ((bf16[4,384,256]{2,1,0:T(8,128)(2,1)}), bf16[4,384,256]{2,1,0:T(8,128)(2,1)S(1)}, u32[]{:S(2)}, u32[]{:S(2)}) async-start(bf16[4,384,256]{2,1,0:T(8,128)(2,1)} %fusion.13), calls=%async_computation.6 | async-start | bytes 1572864 | tf_op jit(solution)/shard_map/all_to_all | solution.py:67
  204.1 15.4 %collective-permute-start.15 = (bf16[384,256]{1,0:T(8,128)(2,1)S(1)}, bf16[384,256]{1,0:T(8,128)(2,1)S(1)}, u32[]{:S(2)}, u32[]{:S(2)}) collective-permute-start(bf16[384,256]{1,0:T(8,128)(2,1)S(1)} %reduce_sum.83), channel_id=1, source_target_pairs={{0,8},{8,0},{1,9},{9,1},{2,10},{10,2},{3,11},{11,3},{4,12},{12,4},... | collective-permute-start | bytes 589832 | tf_op jit(solution)/shard_map/ppermute | solution.py:35
  219.8 38.3 %collective-permute-start.2 = (bf16[384,256]{1,0:T(8,128)(2,1)S(1)}, bf16[384,256]{1,0:T(8,128)(2,1)S(1)}, u32[]{:S(2)}, u32[]{:S(2)}) collective-permute-start(bf16[384,256]{1,0:T(8,128)(2,1)S(1)} %get-tuple-element.46), channel_id=1, source_target_pairs={{0,32},{16,48},{32,64},{48,80},{64,96},{80,112},{96,128},{112,144}... | collective-permute-start | bytes 589832 | tf_op jit(solution)/shard_map/cond/branch_1_fun/ppermute | solution.py:25
  223.5 39.0 %collective-permute-start.3 = (bf16[384,256]{1,0:T(8,128)(2,1)S(1)}, bf16[384,256]{1,0:T(8,128)(2,1)S(1)}, u32[]{:S(2)}, u32[]{:S(2)}) collective-permute-start(bf16[384,256]{1,0:T(8,128)(2,1)S(1)} %get-tuple-element.46), channel_id=1, source_target_pairs={{0,480},{16,496},{32,0},{48,16},{64,32},{80,48},{96,64},{112,80},{... | collective-permute-start | bytes 589832 | tf_op jit(solution)/shard_map/cond/branch_1_fun/ppermute | solution.py:25
  262.5 0.7 copy-start.8
  262.5 0.9 copy-start.1

commit v7 on v6

--- a/solution.py
+++ b/solution.py
@@ -39,16 +39,6 @@
     count = lax.axis_size("y") * lax.axis_size("c")
     copies = jnp.broadcast_to(piece[None], (count,) + piece.shape)
     return lax.all_to_all(copies, ("y", "c"), 0, 0, tiled=False)
-
-
-def gather_seq(piece):
-    from_other = swap_zh(piece)
-    own_half = spread_half(piece)
-    other_half = spread_half(from_other)
-    first_own = lax.axis_index("zh") == 0
-    low = jnp.where(first_own, own_half, other_half)
-    high = jnp.where(first_own, other_half, own_half)
-    return jnp.concatenate([low, high]).reshape((-1,) + piece.shape[1:])
 
 
 def gather_other_first(piece):
@@ -130,12 +120,19 @@
     blk_size = BLOCK
     blocks_dev = tok_count // blk_size
     inv_root = head_size ** (-0.5)
-    kv_here = fold_rows(tokens_here, gather_seq(weight_here)).astype(jnp.bfloat16)
+    my_half = lax.axis_index("zh")
+    tok_view = tokens_here.reshape(tok_count, 2, -1)
+    tok_other = lax.dynamic_index_in_dim(tok_view, 1 - my_half, 1, keepdims=False)
+    tok_mine = lax.dynamic_index_in_dim(tok_view, my_half, 1, keepdims=False)
+    weight_rows = gather_other_first(weight_here)
+    half_d = weight_rows.shape[0] // 2
+    kv_here = (
+        fold_rows(tok_other, weight_rows[:half_d]) + fold_rows(tok_mine, weight_rows[half_d:])
+    ).astype(jnp.bfloat16)
     kv_all = gather_other_first(kv_here)
     keys_all = kv_all[:, :head_size]
     values_all = kv_all[:, head_size:]
     half_n = seq_count // 2
-    my_half = lax.axis_index("zh")
     order = jnp.concatenate([(1 - my_half) * half_n + jnp.arange(half_n), my_half * half_n + jnp.arange(half_n)])
     every_block = (order[:, None] * blocks_dev + jnp.arange(blocks_dev)[None, :]).reshape(-1).astype(jnp.int32)
     blocks_here = seq_index * blocks_dev + jnp.arange(blocks_dev, dtype=jnp.int32)
@@ -158,9 +155,6 @@
     grad_terms = jnp.concatenate([key_terms, value_terms], axis=1).astype(jnp.bfloat16)
     half_rows = grad_terms.shape[0] // 2
     kv_grad = scatter_halves(grad_terms[:half_rows], grad_terms[half_rows:]).astype(jnp.bfloat16)
-    tok_view = tokens_here.reshape(tok_count, 2, -1)
-    tok_other = lax.dynamic_index_in_dim(tok_view, 1 - my_half, 1, keepdims=False)
-    tok_mine = lax.dynamic_index_in_dim(tok_view, my_half, 1, keepdims=False)
     grad_slice = scatter_halves(
         contract_rows(tok_other, kv_grad).astype(jnp.bfloat16),
         contract_rows(tok_mine, kv_grad).astype(jnp.bfloat16),

time: 267 us -> 284 us (1.064)
  the two profiles are of different devices: /device:TPU:1 before, /device:TPU:264 now
where the time goes in v7:
time: 284 us; the launch traced here: 282 us
  waiting for transfers between devices  106 us (37%)
  starting transfers between devices  101 us (36%)
  local copies, waits for them, and re-layouts  36.8 us (13%)
  other arithmetic  20.7 us (7%)
  matrix products  15.6 us (5%)
    ppermute x4, waiting for transfers between devices, swap_zh(): return lax.ppermute(value, 'zh', [(0, 1), (1, 0)])  42 us
    ppermute x2, starting transfers between devices, shifted(): return lax.ppermute(value, axis, pairs)  36.7 us
    all_to_all x4, waiting for transfers between devices, spread_half(): return lax.all_to_all(copies, ('y', 'c'), 0, 0, tiled=False)  28.1 us
    all_to_all x4, starting transfers between devices, reduce_half(): spread = lax.all_to_all(summed, 'y', 0, 0, tiled=False)  21.5 us
    all_to_all x4, waiting for transfers between devices, reduce_half(): spread = lax.all_to_all(summed, 'y', 0, 0, tiled=False)  21.5 us
    all_to_all x4, starting transfers between devices, spread_half(): return lax.all_to_all(copies, ('y', 'c'), 0, 0, tiled=False)  20.9 us
    unnamed x28, local copies, waits for them, and re-layouts  18.2 us
    ppermute x2, waiting for transfers between devices, shifted(): return lax.ppermute(value, axis, pairs)  14.6 us
  transfers between devices with their start and end apart: 18, of which 13 were waited for; matrix products, arithmetic and copies ran while one was open for 13% of the time, Pallas kernels for 0%

profile of v7, /device:TPU:264, one launch (start us, length us, event | category | flops | bytes accessed | tf_op | source)
XLA Modules:
  0.0 282.0 jit_solution(15281704112946700242)
XLA Ops:
  0.7 2.3 broadcast_in_dim.58
  2.9 4.9 %all-to-all-start.1 = ((bf16[8,384,256]{2,1,0:T(8,128)(2,1)}), bf16[8,384,256]{2,1,0:T(8,128)(2,1)S(1)}, u32[]{:S(2)}, u32[]{:S(2)}) async-start(bf16[8,384,256]{2,1,0:T(8,128)(2,1)} %broadcast_in_dim.58), calls=%async_computation.1 | async-start | bytes 3145728 | tf_op jit(solution)/shard_map/all_to_all | solution.py:41
  7.8 3.2 %collective-permute-start.8 = (bf16[384,256]{1,0:T(8,128)(2,1)S(1)}, bf16[384,256]{1,0:T(8,128)(2,1)S(1)}, u32[]{:S(2)}, u32[]{:S(2)}) collective-permute-start(bf16[384,256]{1,0:T(8,128)(2,1)S(1)} %bitcast.138), channel_id=1, source_target_pairs={{0,8},{8,0},{1,9},{9,1},{2,10},{10,2},{3,11},{11,3},{4,12},{12,4},... | collective-permute-start | bytes 589832 | tf_op jit(solution)/shard_map/ppermute | solution.py:35
  11.0 15.6 %collective-permute-done.8 = bf16[384,256]{1,0:T(8,128)(2,1)S(1)} collective-permute-done((bf16[384,256]{1,0:T(8,128)(2,1)S(1)}, bf16[384,256]{1,0:T(8,128)(2,1)S(1)}, u32[]{:S(2)}, u32[]{:S(2)}) %collective-permute-start.8) | collective-permute-done | bytes 196640 | tf_op jit(solution)/shard_map/ppermute | solution.py:35
  26.6 1.3 all-to-all-done.1
  27.9 1.3 broadcast_in_dim.57
  29.6 5.6 %all-to-all-start = ((bf16[8,384,256]{2,1,0:T(8,128)(2,1)}), bf16[8,384,256]{2,1,0:T(8,128)(2,1)}, u32[]{:S(2)}, u32[]{:S(2)}) async-start(bf16[8,384,256]{2,1,0:T(8,128)(2,1)} %broadcast_in_dim.57), calls=%async_computation | async-start | bytes 3145728 | tf_op jit(solution)/shard_map/all_to_all | solution.py:41
  35.2 3.2 %copy.43 = bf16[1,256,6144]{1,2,0:T(8,128)(2,1)S(1)} copy(bf16[1,256,6144]{2,1,0:T(8,128)(2,1)} %param.10) | data formatting | bytes 6291456 | tf_op args[0]
  38.4 3.9 %fusion.8 = f32[256,256]{1,0:T(8,128)} fusion(bf16[3072,256]{1,0:T(8,128)(2,1)} %bitcast.136, bf16[256,2,3072]{0,2,1:T(8,128)(2,1)S(1)} %bitcast.127, s32[]{:T(128)S(6)} %select_n.79), kind=kOutput, calls=%fused_computation.22 | convolution fusion | flops 402653184 | bytes 3407876 | tf_op jit(solution)/shard_map/dot_general | solution.py:71
  42.2 13.2 %all-to-all-done = bf16[8,384,256]{2,1,0:T(8,128)(2,1)} async-done(((bf16[8,384,256]{2,1,0:T(8,128)(2,1)}), bf16[8,384,256]{2,1,0:T(8,128)(2,1)}, u32[]{:S(2)}, u32[]{:S(2)}) %all-to-all-start) | async-done | bytes 1572896 | tf_op jit(solution)/shard_map/all_to_all | solution.py:41
  55.4 2.0 fusion.23
  57.5 1.1 broadcast_in_dim.60
  58.5 5.6 %all-to-all-start.3 = ((bf16[8,256,256]{2,1,0:T(8,128)(2,1)}), bf16[8,256,256]{2,1,0:T(8,128)(2,1)}, u32[]{:S(2)}, u32[]{:S(2)}) async-start(bf16[8,256,256]{2,1,0:T(8,128)(2,1)} %broadcast_in_dim.60), calls=%async_computation.3 | async-start | bytes 2097152 | tf_op jit(solution)/shard_map/all_to_all | solution.py:41
  64.1 3.4 %collective-permute-start.9 = (bf16[256,256]{1,0:T(8,128)(2,1)S(1)}, bf16[256,256]{1,0:T(8,128)(2,1)S(1)}, u32[]{:S(2)}, u32[]{:S(2)}) collective-permute-start(bf16[256,256]{1,0:T(8,128)(2,1)S(1)} %fusion.23), channel_id=1, source_target_pairs={{0,8},{8,0},{1,9},{9,1},{2,10},{10,2},{3,11},{11,3},{4,12},{12,4},... | collective-permute-start | bytes 393224 | tf_op jit(solution)/shard_map/ppermute | solution.py:35
  67.6 12.9 %collective-permute-done.9 = bf16[256,256]{1,0:T(8,128)(2,1)S(1)} collective-permute-done((bf16[256,256]{1,0:T(8,128)(2,1)S(1)}, bf16[256,256]{1,0:T(8,128)(2,1)S(1)}, u32[]{:S(2)}, u32[]{:S(2)}) %collective-permute-start.9) | collective-permute-done | bytes 131104 | tf_op jit(solution)/shard_map/ppermute | solution.py:35
  80.5 1.1 broadcast_in_dim.59
  81.5 4.8 %all-to-all-start.2 = ((bf16[8,256,256]{2,1,0:T(8,128)(2,1)}), bf16[8,256,256]{2,1,0:T(8,128)(2,1)}, u32[]{:S(2)}, u32[]{:S(2)}) async-start(bf16[8,256,256]{2,1,0:T(8,128)(2,1)} %broadcast_in_dim.59), calls=%async_computation.2 | async-start | bytes 2097152 | tf_op jit(solution)/shard_map/all_to_all | solution.py:41
  87.3 13.6 %all-to-all-done.2 = bf16[8,256,256]{2,1,0:T(8,128)(2,1)} async-done(((bf16[8,256,256]{2,1,0:T(8,128)(2,1)}), bf16[8,256,256]{2,1,0:T(8,128)(2,1)}, u32[]{:S(2)}, u32[]{:S(2)}) %all-to-all-start.2) | async-done | bytes 1048608 | tf_op jit(solution)/shard_map/all_to_all | solution.py:41
  100.9 1.7 pad_maximum_fusion
  102.9 1.2 fusion.51
  104.4 0.8 convolution_convert_fusion
  106.6 0.8 convolution_convert_fusion.1
  107.5 1.5 pad_maximum_fusion.1
  109.0 2.7 reshape.117
  111.7 2.6 reshape.118
  114.3 4.4 %fusion.49 = (bf16[4,1,256,256]{2,1,0,3:T(2,128)(2,1)}, bf16[4,1,256,256]{2,1,0,3:T(2,128)(2,1)}) fusion(bf16[4,2,256,256]{2,1,0,3:T(2,128)(2,1)} %reshape.118), kind=kLoop, calls=%fused_computation.85 | loop fusion | bytes 2097152 | tf_op jit(solution)/shard_map/slice | solution.py:53
  118.6 3.5 %copy.59 = bf16[4,1,256,256]{3,2,0,1:T(8,128)(2,1)} copy(bf16[4,1,256,256]{2,1,0,3:T(2,128)(2,1)} %get-tuple-element.55) | data formatting | bytes 1048576
  122.1 3.5 %copy.58 = bf16[4,1,256,256]{3,2,0,1:T(8,128)(2,1)} copy(bf16[4,1,256,256]{2,1,0,3:T(2,128)(2,1)} %get-tuple-element.54) | data formatting | bytes 1048576
  125.6 2.0 select_bitcast_fusion.2
  127.5 1.9 collective-permute-start.11
  129.5 2.5 fusion.50
  132.0 3.5 %copy.57 = bf16[4,1,256,256]{3,2,0,1:T(8,128)(2,1)} copy(bf16[4,1,256,256]{2,1,0,3:T(2,128)(2,1)} %get-tuple-element.57) | data formatting | bytes 1048576
  135.4 3.5 %copy.56 = bf16[4,1,256,256]{3,2,0,1:T(8,128)(2,1)} copy(bf16[4,1,256,256]{2,1,0,3:T(2,128)(2,1)} %get-tuple-element.56) | data formatting | bytes 1048576
  138.9 1.9 select_bitcast_fusion.3
  140.8 2.4 collective-permute-start.10
  143.2 2.2 fusion.29
  145.4 5.6 %all-to-all-start.5 = ((bf16[4,256,256]{2,1,0:T(8,128)(2,1)}), bf16[4,256,256]{2,1,0:T(8,128)(2,1)}, u32[]{:S(2)}, u32[]{:S(2)}) async-start(bf16[4,256,256]{2,1,0:T(8,128)(2,1)} %fusion.29), calls=%async_computation.5 | async-start | bytes 1048576 | tf_op jit(solution)/shard_map/all_to_all | solution.py:57
  150.9 2.2 fusion.30
  153.2 6.3 %all-to-all-done.5 = bf16[4,256,256]{2,1,0:T(8,128)(2,1)} async-done(((bf16[4,256,256]{2,1,0:T(8,128)(2,1)}), bf16[4,256,256]{2,1,0:T(8,128)(2,1)}, u32[]{:S(2)}, u32[]{:S(2)}) %all-to-all-start.5) | async-done | bytes 524320 | tf_op jit(solution)/shard_map/all_to_all | solution.py:57
  159.5 5.6 %all-to-all-start.4 = ((bf16[4,256,256]{2,1,0:T(8,128)(2,1)}), bf16[4,256,256]{2,1,0:T(8,128)(2,1)}, u32[]{:S(2)}, u32[]{:S(2)}) async-start(bf16[4,256,256]{2,1,0:T(8,128)(2,1)} %fusion.30), calls=%async_computation.4 | async-start | bytes 1048576 | tf_op jit(solution)/shard_map/all_to_all | solution.py:57
  165.1 1.1 reduce_sum.82
  166.2 3.3 %collective-permute-start.12 = (bf16[256,256]{1,0:T(8,128)(2,1)S(1)}, bf16[256,256]{1,0:T(8,128)(2,1)S(1)}, u32[]{:S(2)}, u32[]{:S(2)}) collective-permute-start(bf16[256,256]{1,0:T(8,128)(2,1)S(1)} %reduce_sum.82), channel_id=1, source_target_pairs={{0,8},{8,0},{1,9},{9,1},{2,10},{10,2},{3,11},{11,3},{4,12},{12,4},... | collective-permute-start | bytes 393224 | tf_op jit(solution)/shard_map/ppermute | solution.py:35
  169.6 3.3 %all-to-all-done.4 = bf16[4,256,256]{2,1,0:T(8,128)(2,1)} async-done(((bf16[4,256,256]{2,1,0:T(8,128)(2,1)}), bf16[4,256,256]{2,1,0:T(8,128)(2,1)}, u32[]{:S(2)}, u32[]{:S(2)}) %all-to-all-start.4) | async-done | bytes 524320 | tf_op jit(solution)/shard_map/all_to_all | solution.py:57
  172.8 1.1 convert_reduce_fusion
  173.9 7.8 %collective-permute-done.12 = bf16[256,256]{1,0:T(8,128)(2,1)S(1)} collective-permute-done((bf16[256,256]{1,0:T(8,128)(2,1)S(1)}, bf16[256,256]{1,0:T(8,128)(2,1)S(1)}, u32[]{:S(2)}, u32[]{:S(2)}) %collective-permute-start.12) | collective-permute-done | bytes 131104 | tf_op jit(solution)/shard_map/ppermute | solution.py:35
  182.5 1.9 collective-permute-start.14
  184.4 2.0 convolution_convert_fusion.3
  186.4 1.0 select_bitcast_fusion.1
  187.4 2.4 collective-permute-start.13
  189.8 1.2 fusion.14
  191.0 4.8 %all-to-all-start.7 = ((bf16[4,384,256]{2,1,0:T(8,128)(2,1)}), bf16[4,384,256]{2,1,0:T(8,128)(2,1)S(1)}, u32[]{:S(2)}, u32[]{:S(2)}) async-start(bf16[4,384,256]{2,1,0:T(8,128)(2,1)} %fusion.14), calls=%async_computation.7 | async-start | bytes 1572864 | tf_op jit(solution)/shard_map/all_to_all | solution.py:57
  195.8 2.3 fusion.15
  198.1 8.7 %all-to-all-done.7 = bf16[4,384,256]{2,1,0:T(8,128)(2,1)S(1)} async-done(((bf16[4,384,256]{2,1,0:T(8,128)(2,1)}), bf16[4,384,256]{2,1,0:T(8,128)(2,1)S(1)}, u32[]{:S(2)}, u32[]{:S(2)}) %all-to-all-start.7) | async-done | bytes 786464 | tf_op jit(solution)/shard_map/all_to_all | solution.py:57
  206.8 5.6 %all-to-all-start.6 = ((bf16[4,384,256]{2,1,0:T(8,128)(2,1)}), bf16[4,384,256]{2,1,0:T(8,128)(2,1)}, u32[]{:S(2)}, u32[]{:S(2)}) async-start(bf16[4,384,256]{2,1,0:T(8,128)(2,1)} %fusion.15), calls=%async_computation.6 | async-start | bytes 1572864 | tf_op jit(solution)/shard_map/all_to_all | solution.py:57
  213.2 3.2 %collective-permute-start.15 = (bf16[384,256]{1,0:T(8,128)(2,1)S(1)}, bf16[384,256]{1,0:T(8,128)(2,1)S(1)}, u32[]{:S(2)}, u32[]{:S(2)}) collective-permute-start(bf16[384,256]{1,0:T(8,128)(2,1)S(1)} %reduce_sum.83), channel_id=1, source_target_pairs={{0,8},{8,0},{1,9},{9,1},{2,10},{10,2},{3,11},{11,3},{4,12},{12,4},... | collective-permute-start | bytes 589832 | tf_op jit(solution)/shard_map/ppermute | solution.py:35
  216.5 3.0 %fusion.27 = bf16[1,256,128]{2,1,0:T(8,128)(2,1)} fusion(bf16[256,4096]{0,1:T(8,128)(2,1)} %copy-done.5, bf16[4096,256]{1,0:T(8,128)(2,1)S(1)} %bitcast.134), kind=kOutput, calls=%fused_computation.41 | convolution fusion | flops 268468224 | bytes 3211264 | tf_op jit(solution)/shard_map/dot_general | solution.py:150
  219.4 3.2 %all-to-all-done.6 = bf16[4,384,256]{2,1,0:T(8,128)(2,1)} async-done(((bf16[4,384,256]{2,1,0:T(8,128)(2,1)}), bf16[4,384,256]{2,1,0:T(8,128)(2,1)}, u32[]{:S(2)}, u32[]{:S(2)}) %all-to-all-start.6) | async-done | bytes 786464 | tf_op jit(solution)/shard_map/all_to_all | solution.py:57
  222.6 1.3 convert_element_type.149
  223.9 5.7 %collective-permute-done.15 = bf16[384,256]{1,0:T(8,128)(2,1)S(1)} collective-permute-done((bf16[384,256]{1,0:T(8,128)(2,1)S(1)}, bf16[384,256]{1,0:T(8,128)(2,1)S(1)}, u32[]{:S(2)}, u32[]{:S(2)}) %collective-permute-start.15) | collective-permute-done | bytes 196640 | tf_op jit(solution)/shard_map/ppermute | solution.py:35
  229.6 51.6 %conditional.1 = (f32[1,384,256]{2,1,0:T(8,128)S(1)}) conditional(s32[]{:T(128)} %clamp.3, (f32[4,384,256]{2,1,0:T(8,128)S(1)}, f32[384,256]{1,0:T(8,128)S(1)}) %tuple.28, (f32[4,384,256]{2,1,0:T(8,128)S(1)}, f32[384,256]{1,0:T(8,128)S(1)}) %tuple.28, (f32[4,384,256]{2,1,0:T(8,128)S(1)}, ...), branch_computations={%region_6.8_spmd, %region_8.10_spmd, %region_10.12_spmd, %region_1... | conditional | flops 983040 | bytes 6094940 | solution.py:166
  229.8 34.8 %collective-permute-start.3 = (bf16[384,256]{1,0:T(8,128)(2,1)S(1)}, bf16[384,256]{1,0:T(8,128)(2,1)S(1)}, u32[]{:S(2)}, u32[]{:S(2)}) collective-permute-start(bf16[384,256]{1,0:T(8,128)(2,1)S(1)} %get-tuple-element.46), channel_id=1, source_target_pairs={{0,480},{16,496},{32,0},{48,16},{64,32},{80,48},{96,64},{112,80},{... | collective-permute-start | bytes 589832 | tf_op jit(solution)/shard_map/cond/branch_1_fun/ppermute | solution.py:25
  264.6 1.9 collective-permute-start.2
  266.5 1.2 collective-permute-done.3
  267.8 13.4 %collective-permute-done.2 = bf16[384,256]{1,0:T(8,128)(2,1)S(1)} collective-permute-done((bf16[384,256]{1,0:T(8,128)(2,1)S(1)}, bf16[384,256]{1,0:T(8,128)(2,1)S(1)}, u32[]{:S(2)}, u32[]{:S(2)}) %collective-permute-start.2) | collective-permute-done | bytes 196640 | tf_op jit(solution)/shard_map/cond/branch_1_fun/ppermute | solution.py:25
  (52 shorter events, 5.1 us)
Async XLA Ops:
  0.6 102.3 %copy-start = (bf16[1,256,128]{2,1,0:T(8,128)(2,1)S(1)}, bf16[1,256,128]{2,1,0:T(8,128)(2,1)}, u32[]{:S(2)}) copy-start(bf16[1,256,128]{2,1,0:T(8,128)(2,1)} %param.11) | copy-start | bytes 196612
  0.6 7.2 %copy-start.9 = (bf16[1,384,256]{2,1,0:T(8,128)(2,1)S(1)}, bf16[1,384,256]{2,1,0:T(8,128)(2,1)}, u32[]{:S(2)}) copy-start(bf16[1,384,256]{2,1,0:T(8,128)(2,1)} %param.13) | copy-start | bytes 589828
  2.9 25.0 %all-to-all-start.1 = ((bf16[8,384,256]{2,1,0:T(8,128)(2,1)}), bf16[8,384,256]{2,1,0:T(8,128)(2,1)S(1)}, u32[]{:S(2)}, u32[]{:S(2)}) async-start(bf16[8,384,256]{2,1,0:T(8,128)(2,1)} %broadcast_in_dim.58), calls=%async_computation.1 | async-start | bytes 3145728 | tf_op jit(solution)/shard_map/all_to_all | solution.py:41
  7.8 18.8 %collective-permute-start.8 = (bf16[384,256]{1,0:T(8,128)(2,1)S(1)}, bf16[384,256]{1,0:T(8,128)(2,1)S(1)}, u32[]{:S(2)}, u32[]{:S(2)}) collective-permute-start(bf16[384,256]{1,0:T(8,128)(2,1)S(1)} %bitcast.138), channel_id=1, source_target_pairs={{0,8},{8,0},{1,9},{9,1},{2,10},{10,2},{3,11},{11,3},{4,12},{12,4},... | collective-permute-start | bytes 589832 | tf_op jit(solution)/shard_map/ppermute | solution.py:35
  27.9 1.6 copy-start.6
  29.6 25.9 %all-to-all-start = ((bf16[8,384,256]{2,1,0:T(8,128)(2,1)}), bf16[8,384,256]{2,1,0:T(8,128)(2,1)}, u32[]{:S(2)}, u32[]{:S(2)}) async-start(bf16[8,384,256]{2,1,0:T(8,128)(2,1)} %broadcast_in_dim.57), calls=%async_computation | async-start | bytes 3145728 | tf_op jit(solution)/shard_map/all_to_all | solution.py:41
  38.4 143.4 %copy-start.1 = (bf16[1,256,6144]{1,2,0:T(8,128)(2,1)}, bf16[1,256,6144]{1,2,0:T(8,128)(2,1)S(1)}, u32[]{:S(2)}) copy-start(bf16[1,256,6144]{1,2,0:T(8,128)(2,1)S(1)} %copy.43) | copy-start | bytes 9437188
  58.5 21.9 %all-to-all-start.3 = ((bf16[8,256,256]{2,1,0:T(8,128)(2,1)}), bf16[8,256,256]{2,1,0:T(8,128)(2,1)}, u32[]{:S(2)}, u32[]{:S(2)}) async-start(bf16[8,256,256]{2,1,0:T(8,128)(2,1)} %broadcast_in_dim.60), calls=%async_computation.3 | async-start | bytes 2097152 | tf_op jit(solution)/shard_map/all_to_all | solution.py:41
  64.1 22.4 %copy-start.10 = (s32[64,3]{0,1:T(4,128)S(1)}, s32[64,3]{0,1:T(4,128)}, u32[]{:S(2)}) copy-start(s32[64,3]{0,1:T(4,128)} %param.14) | copy-start | bytes 2308
  64.1 23.1 %copy-start.8 = (bf16[1,256,128]{2,1,0:T(8,128)(2,1)S(1)}, bf16[1,256,128]{2,1,0:T(8,128)(2,1)}, u32[]{:S(2)}) copy-start(bf16[1,256,128]{2,1,0:T(8,128)(2,1)} %param.12) | copy-start | bytes 196612
  64.1 16.4 %collective-permute-start.9 = (bf16[256,256]{1,0:T(8,128)(2,1)S(1)}, bf16[256,256]{1,0:T(8,128)(2,1)S(1)}, u32[]{:S(2)}, u32[]{:S(2)}) collective-permute-start(bf16[256,256]{1,0:T(8,128)(2,1)S(1)} %fusion.23), channel_id=1, source_target_pairs={{0,8},{8,0},{1,9},{9,1},{2,10},{10,2},{3,11},{11,3},{4,12},{12,4},... | collective-permute-start | bytes 393224 | tf_op jit(solution)/shard_map/ppermute | solution.py:35
  81.5 19.4 %all-to-all-start.2 = ((bf16[8,256,256]{2,1,0:T(8,128)(2,1)}), bf16[8,256,256]{2,1,0:T(8,128)(2,1)}, u32[]{:S(2)}, u32[]{:S(2)}) async-start(bf16[8,256,256]{2,1,0:T(8,128)(2,1)} %broadcast_in_dim.59), calls=%async_computation.2 | async-start | bytes 2097152 | tf_op jit(solution)/shard_map/all_to_all | solution.py:41
  102.6 3.2 %copy-start.3 = (bf16[16,256,256]{2,1,0:T(8,128)(2,1)}, bf16[16,256,256]{2,1,0:T(8,128)(2,1)S(1)}, u32[]{:S(2)}) copy-start(bf16[16,256,256]{2,1,0:T(8,128)(2,1)S(1)} %pad_maximum_fusion) | copy-start | bytes 6291460
  106.6 2.4 copy-start.5
  125.6 3.9 %copy-start.2 = (bf16[4,2,256,256]{2,1,0,3:T(2,128)(2,1)S(1)}, bf16[4,2,256,256]{2,1,0,3:T(2,128)(2,1)}, u32[]{:S(2)}) copy-start(bf16[4,2,256,256]{2,1,0,3:T(2,128)(2,1)} %reshape.117) | copy-start | bytes 3145732
  127.5 15.6 %collective-permute-start.11 = (bf16[4,256,256]{2,1,0:T(8,128)(2,1)}, bf16[4,256,256]{2,1,0:T(8,128)(2,1)}, u32[]{:S(2)}, u32[]{:S(2)}) collective-permute-start(bf16[4,256,256]{2,1,0:T(8,128)(2,1)} %select_bitcast_fusion.2), channel_id=1, source_target_pairs={{0,1},{1,0},{2,3},{3,2},{4,5},{5,4},{6,7},{7,6},{8,9},{9,8},{10,11... | collective-permute-start | bytes 1572872 | tf_op jit(solution)/shard_map/ppermute | solution.py:55
  140.8 10.2 %collective-permute-start.10 = (bf16[4,256,256]{2,1,0:T(8,128)(2,1)}, bf16[4,256,256]{2,1,0:T(8,128)(2,1)}, u32[]{:S(2)}, u32[]{:S(2)}) collective-permute-start(bf16[4,256,256]{2,1,0:T(8,128)(2,1)} %select_bitcast_fusion.3), channel_id=1, source_target_pairs={{0,1},{1,0},{2,3},{3,2},{4,5},{5,4},{6,7},{7,6},{8,9},{9,8},{10,11... | collective-permute-start | bytes 1572872 | tf_op jit(solution)/shard_map/ppermute | solution.py:55
  145.4 14.1 %all-to-all-start.5 = ((bf16[4,256,256]{2,1,0:T(8,128)(2,1)}), bf16[4,256,256]{2,1,0:T(8,128)(2,1)}, u32[]{:S(2)}, u32[]{:S(2)}) async-start(bf16[4,256,256]{2,1,0:T(8,128)(2,1)} %fusion.29), calls=%async_computation.5 | async-start | bytes 1048576 | tf_op jit(solution)/shard_map/all_to_all | solution.py:57
  159.5 13.3 %all-to-all-start.4 = ((bf16[4,256,256]{2,1,0:T(8,128)(2,1)}), bf16[4,256,256]{2,1,0:T(8,128)(2,1)}, u32[]{:S(2)}, u32[]{:S(2)}) async-start(bf16[4,256,256]{2,1,0:T(8,128)(2,1)} %fusion.30), calls=%async_computation.4 | async-start | bytes 1048576 | tf_op jit(solution)/shard_map/all_to_all | solution.py:57
  166.2 15.6 %collective-permute-start.12 = (bf16[256,256]{1,0:T(8,128)(2,1)S(1)}, bf16[256,256]{1,0:T(8,128)(2,1)S(1)}, u32[]{:S(2)}, u32[]{:S(2)}) collective-permute-start(bf16[256,256]{1,0:T(8,128)(2,1)S(1)} %reduce_sum.82), channel_id=1, source_target_pairs={{0,8},{8,0},{1,9},{9,1},{2,10},{10,2},{3,11},{11,3},{4,12},{12,4},... | collective-permute-start | bytes 393224 | tf_op jit(solution)/shard_map/ppermute | solution.py:35
  182.5 7.3 %collective-permute-start.14 = (bf16[4,384,256]{2,1,0:T(8,128)(2,1)S(1)}, bf16[4,384,256]{2,1,0:T(8,128)(2,1)S(1)}, u32[]{:S(2)}, u32[]{:S(2)}) collective-permute-start(bf16[4,384,256]{2,1,0:T(8,128)(2,1)S(1)} %select_bitcast_fusion), channel_id=1, source_target_pairs={{0,1},{1,0},{2,3},{3,2},{4,5},{5,4},{6,7},{7,6},{8,9},{9,8},{10,11... | collective-permute-start | bytes 2359304 | tf_op jit(solution)/shard_map/ppermute | solution.py:55
  187.4 8.4 %collective-permute-start.13 = (bf16[4,384,256]{2,1,0:T(8,128)(2,1)}, bf16[4,384,256]{2,1,0:T(8,128)(2,1)}, u32[]{:S(2)}, u32[]{:S(2)}) collective-permute-start(bf16[4,384,256]{2,1,0:T(8,128)(2,1)} %select_bitcast_fusion.1), channel_id=1, source_target_pairs={{0,1},{1,0},{2,3},{3,2},{4,5},{5,4},{6,7},{7,6},{8,9},{9,8},{10,11... | collective-permute-start | bytes 2359304 | tf_op jit(solution)/shard_map/ppermute | solution.py:55
  191.0 15.8 %all-to-all-start.7 = ((bf16[4,384,256]{2,1,0:T(8,128)(2,1)}), bf16[4,384,256]{2,1,0:T(8,128)(2,1)S(1)}, u32[]{:S(2)}, u32[]{:S(2)}) async-start(bf16[4,384,256]{2,1,0:T(8,128)(2,1)} %fusion.14), calls=%async_computation.7 | async-start | bytes 1572864 | tf_op jit(solution)/shard_map/all_to_all | solution.py:57
  198.1 18.4 %copy-start.4 = (bf16[16,256,256]{2,1,0:T(8,128)(2,1)S(1)}, bf16[16,256,256]{2,1,0:T(8,128)(2,1)}, u32[]{:S(2)}) copy-start(bf16[16,256,256]{2,1,0:T(8,128)(2,1)} %copy-done.3) | copy-start | bytes 6291460
  206.8 15.9 %all-to-all-start.6 = ((bf16[4,384,256]{2,1,0:T(8,128)(2,1)}), bf16[4,384,256]{2,1,0:T(8,128)(2,1)}, u32[]{:S(2)}, u32[]{:S(2)}) async-start(bf16[4,384,256]{2,1,0:T(8,128)(2,1)} %fusion.15), calls=%async_computation.6 | async-start | bytes 1572864 | tf_op jit(solution)/shard_map/all_to_all | solution.py:57
  213.2 16.4 %collective-permute-start.15 = (bf16[384,256]{1,0:T(8,128)(2,1)S(1)}, bf16[384,256]{1,0:T(8,128)(2,1)S(1)}, u32[]{:S(2)}, u32[]{:S(2)}) collective-permute-start(bf16[384,256]{1,0:T(8,128)(2,1)S(1)} %reduce_sum.83), channel_id=1, source_target_pairs={{0,8},{8,0},{1,9},{9,1},{2,10},{10,2},{3,11},{11,3},{4,12},{12,4},... | collective-permute-start | bytes 589832 | tf_op jit(solution)/shard_map/ppermute | solution.py:35
  229.8 37.9 %collective-permute-start.3 = (bf16[384,256]{1,0:T(8,128)(2,1)S(1)}, bf16[384,256]{1,0:T(8,128)(2,1)S(1)}, u32[]{:S(2)}, u32[]{:S(2)}) collective-permute-start(bf16[384,256]{1,0:T(8,128)(2,1)S(1)} %get-tuple-element.46), channel_id=1, source_target_pairs={{0,480},{16,496},{32,0},{48,16},{64,32},{80,48},{96,64},{112,80},{... | collective-permute-start | bytes 589832 | tf_op jit(solution)/shard_map/cond/branch_1_fun/ppermute | solution.py:25
  264.6 16.6 %collective-permute-start.2 = (bf16[384,256]{1,0:T(8,128)(2,1)S(1)}, bf16[384,256]{1,0:T(8,128)(2,1)S(1)}, u32[]{:S(2)}, u32[]{:S(2)}) collective-permute-start(bf16[384,256]{1,0:T(8,128)(2,1)S(1)} %get-tuple-element.46), channel_id=1, source_target_pairs={{0,32},{16,48},{32,64},{48,80},{64,96},{80,112},{96,128},{112,144}... | collective-permute-start | bytes 589832 | tf_op jit(solution)/shard_map/cond/branch_1_fun/ppermute | solution.py:25
  281.3 0.7 copy-start.7

commit v8 on v6

--- a/solution.py
+++ b/solution.py
@@ -153,11 +153,17 @@
     query_grad = jnp.dot(score_grad, keys_all, preferred_element_type=jnp.float32).astype(
         jnp.bfloat16
     )
-    key_terms = contract_rows(score_grad, query_here)
-    value_terms = contract_rows(prob_low, grad_here)
-    grad_terms = jnp.concatenate([key_terms, value_terms], axis=1).astype(jnp.bfloat16)
-    half_rows = grad_terms.shape[0] // 2
-    kv_grad = scatter_halves(grad_terms[:half_rows], grad_terms[half_rows:]).astype(jnp.bfloat16)
+    half_keys = score_grad.shape[1] // 2
+
+    def terms_for(cols):
+        return jnp.concatenate(
+            [contract_rows(score_grad[:, cols], query_here), contract_rows(prob_low[:, cols], grad_here)],
+            axis=1,
+        ).astype(jnp.bfloat16)
+
+    kv_grad = scatter_halves(
+        terms_for(slice(0, half_keys)), terms_for(slice(half_keys, None))
+    ).astype(jnp.bfloat16)
     tok_view = tokens_here.reshape(tok_count, 2, -1)
     tok_other = lax.dynamic_index_in_dim(tok_view, 1 - my_half, 1, keepdims=False)
     tok_mine = lax.dynamic_index_in_dim(tok_view, my_half, 1, keepdims=False)

time: 267 us -> 254 us (0.951)
  local copies, waits for them, and re-layouts: 27.3 us -> 15.3 us
    unnamed x30 -> x22, local copies, waits for them, and re-layouts: 14.2 us -> 8.34 us
    slice x2, local copies, waits for them, and re-layouts: 4.8 us -> 0.27 us  [the longest x1 0.14 us: terms_for(): score_grad[:, cols]]
    dot_general x4 -> x6, matrix products: 5.64 us -> 5.99 us  [contract_rows(): lax.dot_general(matrix_a, matrix_b, (((0,), (0,)), ((), ())), preferred_e...]
  transfers between devices with their start and end apart: 18 -> 18, of which waited for: 11 -> 11; matrix products, arithmetic and copies ran while one was open for 10% -> 8% of each run, Pallas kernels for 0% -> 0%
where the time goes in v8:
time: 254 us; the launch traced here: 250 us
  starting transfers between devices  122 us (48%)
  waiting for transfers between devices  86.6 us (34%)
  local copies, waits for them, and re-layouts  15.3 us (6%)
  matrix products  12.5 us (5%)
  other arithmetic  12.1 us (5%)
    ppermute x4, starting transfers between devices, swap_zh(): return lax.ppermute(value, 'zh', [(0, 1), (1, 0)])  44.4 us
    all_to_all x4, waiting for transfers between devices, spread_half(): return lax.all_to_all(copies, ('y', 'c'), 0, 0, tiled=False)  38.3 us
    ppermute x2, starting transfers between devices, shifted(): return lax.ppermute(value, axis, pairs)  26.5 us
    all_to_all x4, starting transfers between devices, spread_half(): return lax.all_to_all(copies, ('y', 'c'), 0, 0, tiled=False)  24.6 us
    all_to_all x4, waiting for transfers between devices, reduce_half(): spread = lax.all_to_all(summed, 'y', 0, 0, tiled=False)  17.4 us
    ppermute x2, waiting for transfers between devices, shifted(): return lax.ppermute(value, axis, pairs)  16.2 us
    all_to_all x4, starting transfers between devices, reduce_half(): spread = lax.all_to_all(summed, 'y', 0, 0, tiled=False)  15.1 us
    ppermute x4, waiting for transfers between devices, swap_zh(): return lax.ppermute(value, 'zh', [(0, 1), (1, 0)])  14.7 us
  transfers between devices with their start and end apart: 18, of which 11 were waited for; matrix products, arithmetic and copies ran while one was open for 8% of the time, Pallas kernels for 0%

profile of v8, /device:TPU:1, one launch (start us, length us, event | category | flops | bytes accessed | tf_op | source)
XLA Modules:
  0.0 250.0 jit_solution(6972919854402417178)
XLA Ops:
  0.7 2.3 broadcast_in_dim.60
  2.9 10.3 %all-to-all-start = ((bf16[8,384,256]{2,1,0:T(8,128)(2,1)}), bf16[8,384,256]{2,1,0:T(8,128)(2,1)S(1)}, u32[]{:S(2)}, u32[]{:S(2)}) async-start(bf16[8,384,256]{2,1,0:T(8,128)(2,1)} %broadcast_in_dim.60), calls=%async_computation | async-start | bytes 3145728 | tf_op jit(solution)/shard_map/all_to_all | solution.py:41
  13.2 11.1 %collective-permute-start.8 = (bf16[384,256]{1,0:T(8,128)(2,1)S(1)}, bf16[384,256]{1,0:T(8,128)(2,1)S(1)}, u32[]{:S(2)}, u32[]{:S(2)}) collective-permute-start(bf16[384,256]{1,0:T(8,128)(2,1)S(1)} %bitcast.175), channel_id=1, source_target_pairs={{0,8},{8,0},{1,9},{9,1},{2,10},{10,2},{3,11},{11,3},{4,12},{12,4},... | collective-permute-start | bytes 589832 | tf_op jit(solution)/shard_map/ppermute | solution.py:35
  24.3 5.9 %collective-permute-done.8 = bf16[384,256]{1,0:T(8,128)(2,1)S(1)} collective-permute-done((bf16[384,256]{1,0:T(8,128)(2,1)S(1)}, bf16[384,256]{1,0:T(8,128)(2,1)S(1)}, u32[]{:S(2)}, u32[]{:S(2)}) %collective-permute-start.8) | collective-permute-done | bytes 196640 | tf_op jit(solution)/shard_map/ppermute | solution.py:35
  30.2 3.7 %all-to-all-done = bf16[8,384,256]{2,1,0:T(8,128)(2,1)S(1)} async-done(((bf16[8,384,256]{2,1,0:T(8,128)(2,1)}), bf16[8,384,256]{2,1,0:T(8,128)(2,1)S(1)}, u32[]{:S(2)}, u32[]{:S(2)}) %all-to-all-start) | async-done | bytes 1572896 | tf_op jit(solution)/shard_map/all_to_all | solution.py:41
  33.8 1.3 broadcast_in_dim.61
  35.1 4.4 %all-to-all-start.1 = ((bf16[8,384,256]{2,1,0:T(8,128)(2,1)}), bf16[8,384,256]{2,1,0:T(8,128)(2,1)S(1)}, u32[]{:S(2)}, u32[]{:S(2)}) async-start(bf16[8,384,256]{2,1,0:T(8,128)(2,1)} %broadcast_in_dim.61), calls=%async_computation.1 | async-start | bytes 3145728 | tf_op jit(solution)/shard_map/all_to_all | solution.py:41
  39.6 20.6 %all-to-all-done.1 = bf16[8,384,256]{2,1,0:T(8,128)(2,1)S(1)} async-done(((bf16[8,384,256]{2,1,0:T(8,128)(2,1)}), bf16[8,384,256]{2,1,0:T(8,128)(2,1)S(1)}, u32[]{:S(2)}, u32[]{:S(2)}) %all-to-all-start.1) | async-done | bytes 1572896 | tf_op jit(solution)/shard_map/all_to_all | solution.py:41
  60.2 0.2 broadcast_select_fusion.1
  60.4 0.3 pad_maximum_fusion
  60.7 1.6 copy-done.3
  62.3 1.0 fusion.19
  63.4 1.1 broadcast_in_dim.63
  64.5 4.4 %all-to-all-start.3 = ((bf16[8,256,256]{2,1,0:T(8,128)(2,1)}), bf16[8,256,256]{2,1,0:T(8,128)(2,1)S(1)}, u32[]{:S(2)}, u32[]{:S(2)}) async-start(bf16[8,256,256]{2,1,0:T(8,128)(2,1)} %broadcast_in_dim.63), calls=%async_computation.3 | async-start | bytes 2097152 | tf_op jit(solution)/shard_map/all_to_all | solution.py:41
  68.9 11.2 %collective-permute-start.9 = (bf16[256,256]{0,1:T(8,128)(2,1)S(1)}, bf16[256,256]{0,1:T(8,128)(2,1)S(1)}, u32[]{:S(2)}, u32[]{:S(2)}) collective-permute-start(bf16[256,256]{0,1:T(8,128)(2,1)S(1)} %fusion.19), channel_id=1, source_target_pairs={{0,8},{8,0},{1,9},{9,1},{2,10},{10,2},{3,11},{11,3},{4,12},{12,4},... | collective-permute-start | bytes 393224 | tf_op jit(solution)/shard_map/ppermute | solution.py:35
  80.2 4.4 %collective-permute-done.9 = bf16[256,256]{0,1:T(8,128)(2,1)S(1)} collective-permute-done((bf16[256,256]{0,1:T(8,128)(2,1)S(1)}, bf16[256,256]{0,1:T(8,128)(2,1)S(1)}, u32[]{:S(2)}, u32[]{:S(2)}) %collective-permute-start.9) | collective-permute-done | bytes 131104 | tf_op jit(solution)/shard_map/ppermute | solution.py:35
  84.7 1.1 broadcast_in_dim.62
  85.7 5.4 %all-to-all-start.2 = ((bf16[8,256,256]{2,1,0:T(8,128)(2,1)}), bf16[8,256,256]{2,1,0:T(8,128)(2,1)S(1)}, u32[]{:S(2)}, u32[]{:S(2)}) async-start(bf16[8,256,256]{2,1,0:T(8,128)(2,1)} %broadcast_in_dim.62), calls=%async_computation.2 | async-start | bytes 2097152 | tf_op jit(solution)/shard_map/all_to_all | solution.py:41
  91.7 0.1 broadcast_in_dim.57
  92.1 14.0 %all-to-all-done.2 = bf16[8,256,256]{2,1,0:T(8,128)(2,1)S(1)} async-done(((bf16[8,256,256]{2,1,0:T(8,128)(2,1)}), bf16[8,256,256]{2,1,0:T(8,128)(2,1)S(1)}, u32[]{:S(2)}, u32[]{:S(2)}) %all-to-all-start.2) | async-done | bytes 1048608 | tf_op jit(solution)/shard_map/all_to_all | solution.py:41
  106.1 0.2 pad_maximum_fusion.1
  106.3 0.3 broadcast_in_dim.58
  106.6 1.2 fusion.52
  107.8 0.3 fusion.9
  108.1 0.1 fusion.51
  108.3 0.6 fusion.22
  108.9 0.8 fusion.6
  109.6 0.1 fusion.50
  109.8 1.2 copy-done.4
  111.0 0.5 convolution_convert_fusion.3
  111.5 0.5 convolution_convert_fusion.2
  112.1 2.9 %collective-permute-start.11 = (bf16[4,256,256]{1,2,0:T(8,128)(2,1)S(1)}, bf16[4,256,256]{1,2,0:T(8,128)(2,1)S(1)}, u32[]{:S(2)}, u32[]{:S(2)}) collective-permute-start(bf16[4,256,256]{1,2,0:T(8,128)(2,1)S(1)} %select_bitcast_fusion.2), channel_id=1, source_target_pairs={{0,1},{1,0},{2,3},{3,2},{4,5},{5,4},{6,7},{7,6},{8,9},{9,8},{10,11... | collective-permute-start | bytes 1572872 | tf_op jit(solution)/shard_map/ppermute | solution.py:65
  115.0 0.5 convolution_convert_fusion.5
  115.5 0.5 convolution_convert_fusion.4
  116.1 1.9 collective-permute-start.10
  118.0 1.0 fusion.24
  119.0 3.5 %all-to-all-start.5 = ((bf16[4,256,256]{1,2,0:T(8,128)(2,1)}), bf16[4,256,256]{1,2,0:T(8,128)(2,1)S(1)}, u32[]{:S(2)}, u32[]{:S(2)}) async-start(bf16[4,256,256]{1,2,0:T(8,128)(2,1)} %fusion.24), calls=%async_computation.5 | async-start | bytes 1048576 | tf_op jit(solution)/shard_map/all_to_all | solution.py:67
  122.5 1.0 fusion.25
  123.5 8.1 %all-to-all-done.5 = bf16[4,256,256]{1,2,0:T(8,128)(2,1)S(1)} async-done(((bf16[4,256,256]{1,2,0:T(8,128)(2,1)}), bf16[4,256,256]{1,2,0:T(8,128)(2,1)S(1)}, u32[]{:S(2)}, u32[]{:S(2)}) %all-to-all-start.5) | async-done | bytes 524320 | tf_op jit(solution)/shard_map/all_to_all | solution.py:67
  131.6 3.5 %all-to-all-start.4 = ((bf16[4,256,256]{1,2,0:T(8,128)(2,1)}), bf16[4,256,256]{1,2,0:T(8,128)(2,1)S(1)}, u32[]{:S(2)}, u32[]{:S(2)}) async-start(bf16[4,256,256]{1,2,0:T(8,128)(2,1)} %fusion.25), calls=%async_computation.4 | async-start | bytes 1048576 | tf_op jit(solution)/shard_map/all_to_all | solution.py:67
  135.0 4.7 %copy.78 = bf16[1,256,6144]{1,2,0:T(8,128)(2,1)} copy(bf16[1,256,6144]{2,1,0:T(8,128)(2,1)} %param.10) | data formatting | bytes 6291456 | tf_op args[0]
  139.8 11.1 %collective-permute-start.12 = (bf16[256,256]{0,1:T(8,128)(2,1)S(1)}, bf16[256,256]{0,1:T(8,128)(2,1)S(1)}, u32[]{:S(2)}, u32[]{:S(2)}) collective-permute-start(bf16[256,256]{0,1:T(8,128)(2,1)S(1)} %reduce_sum.82), channel_id=1, source_target_pairs={{0,8},{8,0},{1,9},{9,1},{2,10},{10,2},{3,11},{11,3},{4,12},{12,4},... | collective-permute-start | bytes 393224 | tf_op jit(solution)/shard_map/ppermute | solution.py:35
  150.9 3.3 %collective-permute-done.12 = bf16[256,256]{0,1:T(8,128)(2,1)S(1)} collective-permute-done((bf16[256,256]{0,1:T(8,128)(2,1)S(1)}, bf16[256,256]{0,1:T(8,128)(2,1)S(1)}, u32[]{:S(2)}, u32[]{:S(2)}) %collective-permute-start.12) | collective-permute-done | bytes 131104 | tf_op jit(solution)/shard_map/ppermute | solution.py:35
  154.2 2.1 convolution_convert_fusion
  156.2 1.0 select_bitcast_fusion
  157.3 4.4 %collective-permute-start.14 = (bf16[4,384,256]{2,1,0:T(8,128)(2,1)}, bf16[4,384,256]{2,1,0:T(8,128)(2,1)}, u32[]{:S(2)}, u32[]{:S(2)}) collective-permute-start(bf16[4,384,256]{2,1,0:T(8,128)(2,1)} %select_bitcast_fusion), channel_id=1, source_target_pairs={{0,1},{1,0},{2,3},{3,2},{4,5},{5,4},{6,7},{7,6},{8,9},{9,8},{10,11... | collective-permute-start | bytes 2359304 | tf_op jit(solution)/shard_map/ppermute | solution.py:65
  161.7 2.0 convolution_convert_fusion.1
  163.7 1.0 select_bitcast_fusion.1
  164.7 1.9 collective-permute-start.13
  166.7 2.3 fusion.12
  169.0 4.5 %all-to-all-start.7 = ((bf16[4,384,256]{2,1,0:T(8,128)(2,1)}), bf16[4,384,256]{2,1,0:T(8,128)(2,1)}, u32[]{:S(2)}, u32[]{:S(2)}) async-start(bf16[4,384,256]{2,1,0:T(8,128)(2,1)} %fusion.12), calls=%async_computation.7 | async-start | bytes 1572864 | tf_op jit(solution)/shard_map/all_to_all | solution.py:67
  173.4 2.3 fusion.13
  175.8 9.4 %all-to-all-done.7 = bf16[4,384,256]{2,1,0:T(8,128)(2,1)} async-done(((bf16[4,384,256]{2,1,0:T(8,128)(2,1)}), bf16[4,384,256]{2,1,0:T(8,128)(2,1)}, u32[]{:S(2)}, u32[]{:S(2)}) %all-to-all-start.7) | async-done | bytes 786464 | tf_op jit(solution)/shard_map/all_to_all | solution.py:67
  185.1 3.7 %all-to-all-start.6 = ((bf16[4,384,256]{2,1,0:T(8,128)(2,1)}), bf16[4,384,256]{2,1,0:T(8,128)(2,1)S(1)}, u32[]{:S(2)}, u32[]{:S(2)}) async-start(bf16[4,384,256]{2,1,0:T(8,128)(2,1)} %fusion.13), calls=%async_computation.6 | async-start | bytes 1572864 | tf_op jit(solution)/shard_map/all_to_all | solution.py:67
  189.5 1.3 reduce_sum.83
  190.8 11.1 %collective-permute-start.15 = (bf16[384,256]{1,0:T(8,128)(2,1)S(1)}, bf16[384,256]{1,0:T(8,128)(2,1)S(1)}, u32[]{:S(2)}, u32[]{:S(2)}) collective-permute-start(bf16[384,256]{1,0:T(8,128)(2,1)S(1)} %reduce_sum.83), channel_id=1, source_target_pairs={{0,8},{8,0},{1,9},{9,1},{2,10},{10,2},{3,11},{11,3},{4,12},{12,4},... | collective-permute-start | bytes 589832 | tf_op jit(solution)/shard_map/ppermute | solution.py:35
  201.9 3.0 %fusion.23 = bf16[1,256,128]{2,1,0:T(8,128)(2,1)} fusion(bf16[256,4096]{0,1:T(8,128)(2,1)} %copy-done.4, bf16[4096,256]{1,0:T(8,128)(2,1)S(1)} %bitcast.167), kind=kOutput, calls=%fused_computation.40 | convolution fusion | flops 268468224 | bytes 3211264 | tf_op jit(solution)/shard_map/dot_general | solution.py:153
  205.0 1.2 collective-permute-done.15
  206.3 42.9 %conditional.1 = (f32[1,384,256]{2,1,0:T(8,128)S(1)}) conditional(s32[]{:T(128)} %clamp.3, (f32[4,384,256]{2,1,0:T(8,128)S(1)}, f32[384,256]{1,0:T(8,128)S(1)}) %tuple.28, (f32[4,384,256]{2,1,0:T(8,128)S(1)}, f32[384,256]{1,0:T(8,128)S(1)}) %tuple.28, (f32[4,384,256]{2,1,0:T(8,128)S(1)}, ...), branch_computations={%region_6.8_spmd, %region_8.10_spmd, %region_10.12_spmd, %region_1... | conditional | flops 983040 | bytes 6094940 | solution.py:178
  206.5 3.7 %collective-permute-start.2 = (bf16[384,256]{1,0:T(8,128)(2,1)S(1)}, bf16[384,256]{1,0:T(8,128)(2,1)S(1)}, u32[]{:S(2)}, u32[]{:S(2)}) collective-permute-start(bf16[384,256]{1,0:T(8,128)(2,1)S(1)} %get-tuple-element.46), channel_id=1, source_target_pairs={{0,32},{16,48},{32,64},{48,80},{64,96},{80,112},{96,128},{112,144}... | collective-permute-start | bytes 589832 | tf_op jit(solution)/shard_map/cond/branch_1_fun/ppermute | solution.py:25
  210.2 22.8 %collective-permute-start.3 = (bf16[384,256]{1,0:T(8,128)(2,1)S(1)}, bf16[384,256]{1,0:T(8,128)(2,1)S(1)}, u32[]{:S(2)}, u32[]{:S(2)}) collective-permute-start(bf16[384,256]{1,0:T(8,128)(2,1)S(1)} %get-tuple-element.46), channel_id=1, source_target_pairs={{0,480},{16,496},{32,0},{48,16},{64,32},{80,48},{96,64},{112,80},{... | collective-permute-start | bytes 589832 | tf_op jit(solution)/shard_map/cond/branch_1_fun/ppermute | solution.py:25
  233.0 11.8 %collective-permute-done.2 = bf16[384,256]{1,0:T(8,128)(2,1)S(1)} collective-permute-done((bf16[384,256]{1,0:T(8,128)(2,1)S(1)}, bf16[384,256]{1,0:T(8,128)(2,1)S(1)}, u32[]{:S(2)}, u32[]{:S(2)}) %collective-permute-start.2) | collective-permute-done | bytes 196640 | tf_op jit(solution)/shard_map/cond/branch_1_fun/ppermute | solution.py:25
  244.8 4.4 %collective-permute-done.3 = bf16[384,256]{1,0:T(8,128)(2,1)S(1)} collective-permute-done((bf16[384,256]{1,0:T(8,128)(2,1)S(1)}, bf16[384,256]{1,0:T(8,128)(2,1)S(1)}, u32[]{:S(2)}, u32[]{:S(2)}) %collective-permute-start.3) | collective-permute-done | bytes 196640 | tf_op jit(solution)/shard_map/cond/branch_1_fun/ppermute | solution.py:25
  249.2 0.7 copy-done.7
  (47 shorter events, 1.9 us)
Async XLA Ops:
  0.6 106.0 %copy-start = (bf16[1,256,128]{2,1,0:T(8,128)(2,1)S(1)}, bf16[1,256,128]{2,1,0:T(8,128)(2,1)}, u32[]{:S(2)}) copy-start(bf16[1,256,128]{2,1,0:T(8,128)(2,1)} %param.11) | copy-start | bytes 196612
  0.6 12.6 %copy-start.8 = (bf16[1,384,256]{2,1,0:T(8,128)(2,1)S(1)}, bf16[1,384,256]{2,1,0:T(8,128)(2,1)}, u32[]{:S(2)}) copy-start(bf16[1,384,256]{2,1,0:T(8,128)(2,1)} %param.13) | copy-start | bytes 589828
  2.9 30.9 %all-to-all-start = ((bf16[8,384,256]{2,1,0:T(8,128)(2,1)}), bf16[8,384,256]{2,1,0:T(8,128)(2,1)S(1)}, u32[]{:S(2)}, u32[]{:S(2)}) async-start(bf16[8,384,256]{2,1,0:T(8,128)(2,1)} %broadcast_in_dim.60), calls=%async_computation | async-start | bytes 3145728 | tf_op jit(solution)/shard_map/all_to_all | solution.py:41
  13.2 16.9 %collective-permute-start.8 = (bf16[384,256]{1,0:T(8,128)(2,1)S(1)}, bf16[384,256]{1,0:T(8,128)(2,1)S(1)}, u32[]{:S(2)}, u32[]{:S(2)}) collective-permute-start(bf16[384,256]{1,0:T(8,128)(2,1)S(1)} %bitcast.175), channel_id=1, source_target_pairs={{0,8},{8,0},{1,9},{9,1},{2,10},{10,2},{3,11},{11,3},{4,12},{12,4},... | collective-permute-start | bytes 589832 | tf_op jit(solution)/shard_map/ppermute | solution.py:35
  35.1 25.1 %all-to-all-start.1 = ((bf16[8,384,256]{2,1,0:T(8,128)(2,1)}), bf16[8,384,256]{2,1,0:T(8,128)(2,1)S(1)}, u32[]{:S(2)}, u32[]{:S(2)}) async-start(bf16[8,384,256]{2,1,0:T(8,128)(2,1)} %broadcast_in_dim.61), calls=%async_computation.1 | async-start | bytes 3145728 | tf_op jit(solution)/shard_map/all_to_all | solution.py:41
  60.4 1.9 copy-start.3
  64.5 20.2 %all-to-all-start.3 = ((bf16[8,256,256]{2,1,0:T(8,128)(2,1)}), bf16[8,256,256]{2,1,0:T(8,128)(2,1)S(1)}, u32[]{:S(2)}, u32[]{:S(2)}) async-start(bf16[8,256,256]{2,1,0:T(8,128)(2,1)} %broadcast_in_dim.63), calls=%async_computation.3 | async-start | bytes 2097152 | tf_op jit(solution)/shard_map/all_to_all | solution.py:41
  68.9 22.4 %copy-start.9 = (s32[64,3]{0,1:T(4,128)S(1)}, s32[64,3]{0,1:T(4,128)}, u32[]{:S(2)}) copy-start(s32[64,3]{0,1:T(4,128)} %param.14) | copy-start | bytes 2308
  68.9 23.1 %copy-start.5 = (bf16[1,256,128]{2,1,0:T(8,128)(2,1)S(1)}, bf16[1,256,128]{2,1,0:T(8,128)(2,1)}, u32[]{:S(2)}) copy-start(bf16[1,256,128]{2,1,0:T(8,128)(2,1)} %param.12) | copy-start | bytes 196612
  68.9 15.6 %collective-permute-start.9 = (bf16[256,256]{0,1:T(8,128)(2,1)S(1)}, bf16[256,256]{0,1:T(8,128)(2,1)S(1)}, u32[]{:S(2)}, u32[]{:S(2)}) collective-permute-start(bf16[256,256]{0,1:T(8,128)(2,1)S(1)} %fusion.19), channel_id=1, source_target_pairs={{0,8},{8,0},{1,9},{9,1},{2,10},{10,2},{3,11},{11,3},{4,12},{12,4},... | collective-permute-start | bytes 393224 | tf_op jit(solution)/shard_map/ppermute | solution.py:35
  85.7 20.4 %all-to-all-start.2 = ((bf16[8,256,256]{2,1,0:T(8,128)(2,1)}), bf16[8,256,256]{2,1,0:T(8,128)(2,1)S(1)}, u32[]{:S(2)}, u32[]{:S(2)}) async-start(bf16[8,256,256]{2,1,0:T(8,128)(2,1)} %broadcast_in_dim.62), calls=%async_computation.2 | async-start | bytes 2097152 | tf_op jit(solution)/shard_map/all_to_all | solution.py:41
  106.3 2.5 %copy-start.1 = (bf16[16,256,256]{2,1,0:T(8,128)(2,1)}, bf16[16,256,256]{2,1,0:T(8,128)(2,1)S(1)}, u32[]{:S(2)}) copy-start(bf16[16,256,256]{2,1,0:T(8,128)(2,1)S(1)} %pad_maximum_fusion.1) | copy-start | bytes 6291460
  109.6 1.4 copy-start.4
  112.1 5.9 %collective-permute-start.11 = (bf16[4,256,256]{1,2,0:T(8,128)(2,1)S(1)}, bf16[4,256,256]{1,2,0:T(8,128)(2,1)S(1)}, u32[]{:S(2)}, u32[]{:S(2)}) collective-permute-start(bf16[4,256,256]{1,2,0:T(8,128)(2,1)S(1)} %select_bitcast_fusion.2), channel_id=1, source_target_pairs={{0,1},{1,0},{2,3},{3,2},{4,5},{5,4},{6,7},{7,6},{8,9},{9,8},{10,11... | collective-permute-start | bytes 1572872 | tf_op jit(solution)/shard_map/ppermute | solution.py:65
  116.1 6.4 %collective-permute-start.10 = (bf16[4,256,256]{1,2,0:T(8,128)(2,1)S(1)}, bf16[4,256,256]{1,2,0:T(8,128)(2,1)S(1)}, u32[]{:S(2)}, u32[]{:S(2)}) collective-permute-start(bf16[4,256,256]{1,2,0:T(8,128)(2,1)S(1)} %fusion.32), channel_id=1, source_target_pairs={{0,1},{1,0},{2,3},{3,2},{4,5},{5,4},{6,7},{7,6},{8,9},{9,8},{10,11... | collective-permute-start | bytes 1572872 | tf_op jit(solution)/shard_map/ppermute | solution.py:65
  119.0 12.5 %all-to-all-start.5 = ((bf16[4,256,256]{1,2,0:T(8,128)(2,1)}), bf16[4,256,256]{1,2,0:T(8,128)(2,1)S(1)}, u32[]{:S(2)}, u32[]{:S(2)}) async-start(bf16[4,256,256]{1,2,0:T(8,128)(2,1)} %fusion.24), calls=%async_computation.5 | async-start | bytes 1048576 | tf_op jit(solution)/shard_map/all_to_all | solution.py:67
  131.6 19.3 %all-to-all-start.4 = ((bf16[4,256,256]{1,2,0:T(8,128)(2,1)}), bf16[4,256,256]{1,2,0:T(8,128)(2,1)S(1)}, u32[]{:S(2)}, u32[]{:S(2)}) async-start(bf16[4,256,256]{1,2,0:T(8,128)(2,1)} %fusion.25), calls=%async_computation.4 | async-start | bytes 1048576 | tf_op jit(solution)/shard_map/all_to_all | solution.py:67
  139.8 14.4 %collective-permute-start.12 = (bf16[256,256]{0,1:T(8,128)(2,1)S(1)}, bf16[256,256]{0,1:T(8,128)(2,1)S(1)}, u32[]{:S(2)}, u32[]{:S(2)}) collective-permute-start(bf16[256,256]{0,1:T(8,128)(2,1)S(1)} %reduce_sum.82), channel_id=1, source_target_pairs={{0,8},{8,0},{1,9},{9,1},{2,10},{10,2},{3,11},{11,3},{4,12},{12,4},... | collective-permute-start | bytes 393224 | tf_op jit(solution)/shard_map/ppermute | solution.py:35
  154.2 3.1 %copy-start.6 = (bf16[256,256]{0,1:T(8,128)(2,1)}, bf16[256,256]{0,1:T(8,128)(2,1)S(1)}, u32[]{:S(2)}) copy-start(bf16[256,256]{0,1:T(8,128)(2,1)S(1)} %collective-permute-done.12) | copy-start | bytes 393220
  157.3 9.4 %collective-permute-start.14 = (bf16[4,384,256]{2,1,0:T(8,128)(2,1)}, bf16[4,384,256]{2,1,0:T(8,128)(2,1)}, u32[]{:S(2)}, u32[]{:S(2)}) collective-permute-start(bf16[4,384,256]{2,1,0:T(8,128)(2,1)} %select_bitcast_fusion), channel_id=1, source_target_pairs={{0,1},{1,0},{2,3},{3,2},{4,5},{5,4},{6,7},{7,6},{8,9},{9,8},{10,11... | collective-permute-start | bytes 2359304 | tf_op jit(solution)/shard_map/ppermute | solution.py:65
  164.7 8.7 %collective-permute-start.13 = (bf16[4,384,256]{2,1,0:T(8,128)(2,1)}, bf16[4,384,256]{2,1,0:T(8,128)(2,1)}, u32[]{:S(2)}, u32[]{:S(2)}) collective-permute-start(bf16[4,384,256]{2,1,0:T(8,128)(2,1)} %select_bitcast_fusion.1), channel_id=1, source_target_pairs={{0,1},{1,0},{2,3},{3,2},{4,5},{5,4},{6,7},{7,6},{8,9},{9,8},{10,11... | collective-permute-start | bytes 2359304 | tf_op jit(solution)/shard_map/ppermute | solution.py:65
  169.0 16.2 %all-to-all-start.7 = ((bf16[4,384,256]{2,1,0:T(8,128)(2,1)}), bf16[4,384,256]{2,1,0:T(8,128)(2,1)}, u32[]{:S(2)}, u32[]{:S(2)}) async-start(bf16[4,384,256]{2,1,0:T(8,128)(2,1)} %fusion.12), calls=%async_computation.7 | async-start | bytes 1572864 | tf_op jit(solution)/shard_map/all_to_all | solution.py:67
  175.8 26.1 %copy-start.2 = (bf16[16,256,256]{2,1,0:T(8,128)(2,1)S(1)}, bf16[16,256,256]{2,1,0:T(8,128)(2,1)}, u32[]{:S(2)}) copy-start(bf16[16,256,256]{2,1,0:T(8,128)(2,1)} %copy-done.1) | copy-start | bytes 6291460
  185.1 19.7 %all-to-all-start.6 = ((bf16[4,384,256]{2,1,0:T(8,128)(2,1)}), bf16[4,384,256]{2,1,0:T(8,128)(2,1)S(1)}, u32[]{:S(2)}, u32[]{:S(2)}) async-start(bf16[4,384,256]{2,1,0:T(8,128)(2,1)} %fusion.13), calls=%async_computation.6 | async-start | bytes 1572864 | tf_op jit(solution)/shard_map/all_to_all | solution.py:67
  190.8 15.4 %collective-permute-start.15 = (bf16[384,256]{1,0:T(8,128)(2,1)S(1)}, bf16[384,256]{1,0:T(8,128)(2,1)S(1)}, u32[]{:S(2)}, u32[]{:S(2)}) collective-permute-start(bf16[384,256]{1,0:T(8,128)(2,1)S(1)} %reduce_sum.83), channel_id=1, source_target_pairs={{0,8},{8,0},{1,9},{9,1},{2,10},{10,2},{3,11},{11,3},{4,12},{12,4},... | collective-permute-start | bytes 589832 | tf_op jit(solution)/shard_map/ppermute | solution.py:35
  206.5 38.3 %collective-permute-start.2 = (bf16[384,256]{1,0:T(8,128)(2,1)S(1)}, bf16[384,256]{1,0:T(8,128)(2,1)S(1)}, u32[]{:S(2)}, u32[]{:S(2)}) collective-permute-start(bf16[384,256]{1,0:T(8,128)(2,1)S(1)} %get-tuple-element.46), channel_id=1, source_target_pairs={{0,32},{16,48},{32,64},{48,80},{64,96},{80,112},{96,128},{112,144}... | collective-permute-start | bytes 589832 | tf_op jit(solution)/shard_map/cond/branch_1_fun/ppermute | solution.py:25
  210.2 39.0 %collective-permute-start.3 = (bf16[384,256]{1,0:T(8,128)(2,1)S(1)}, bf16[384,256]{1,0:T(8,128)(2,1)S(1)}, u32[]{:S(2)}, u32[]{:S(2)}) collective-permute-start(bf16[384,256]{1,0:T(8,128)(2,1)S(1)} %get-tuple-element.46), channel_id=1, source_target_pairs={{0,480},{16,496},{32,0},{48,16},{64,32},{80,48},{96,64},{112,80},{... | collective-permute-start | bytes 589832 | tf_op jit(solution)/shard_map/cond/branch_1_fun/ppermute | solution.py:25
  249.2 0.7 copy-start.7

commit v9 on v8

--- a/solution.py
+++ b/solution.py
@@ -100,19 +100,12 @@
     return jnp.repeat(jnp.repeat(allowed, blk_size, axis=0), blk_size, axis=1)
 
 
-def gossip(update, distance, rep_count):
+def gossip(pair, distance, rep_count):
+    update, sent = pair
     if distance == 0:
         return update
-    from_low = jax.tree.map(
-        lambda part, own: part.astype(own.dtype),
-        shifted(for_sending(update), "rep", distance),
-        update,
-    )
-    from_high = jax.tree.map(
-        lambda part, own: part.astype(own.dtype),
-        shifted(for_sending(update), "rep", rep_count - distance),
-        update,
-    )
+    from_low = shifted(sent, "rep", distance).astype(update.dtype)
+    from_high = shifted(sent, "rep", rep_count - distance).astype(update.dtype)
     return (update + from_low + from_high) / 3.0
 
 
@@ -175,7 +168,7 @@
         partial(gossip, distance=(1 << level_idx) % rep_count, rep_count=rep_count)
         for level_idx in range(4)
     ]
-    mixed_update = lax.switch(step_count[0] % 4, branches, grad_slice)
+    mixed_update = lax.switch(step_count[0] % 4, branches, (grad_slice, for_sending(grad_slice)))
     return (mixed_update[None], query_grad[None])
 
 

time: 254 us -> 254 us (level)
  no operation moved by 1% of the time
where the time goes in v9:
time: 254 us; the launch traced here: 250 us
  starting transfers between devices  122 us (48%)
  waiting for transfers between devices  86.6 us (34%)
  local copies, waits for them, and re-layouts  15.3 us (6%)
  matrix products  12.5 us (5%)
  other arithmetic  12 us (5%)
    ppermute x4, starting transfers between devices, swap_zh(): return lax.ppermute(value, 'zh', [(0, 1), (1, 0)])  44.4 us
    all_to_all x4, waiting for transfers between devices, spread_half(): return lax.all_to_all(copies, ('y', 'c'), 0, 0, tiled=False)  38.3 us
    ppermute x2, starting transfers between devices, shifted(): return lax.ppermute(value, axis, pairs)  26.5 us
    all_to_all x4, starting transfers between devices, spread_half(): return lax.all_to_all(copies, ('y', 'c'), 0, 0, tiled=False)  24.6 us
    all_to_all x4, waiting for transfers between devices, reduce_half(): spread = lax.all_to_all(summed, 'y', 0, 0, tiled=False)  17.4 us
    ppermute x2, waiting for transfers between devices, shifted(): return lax.ppermute(value, axis, pairs)  16.2 us
    all_to_all x4, starting transfers between devices, reduce_half(): spread = lax.all_to_all(summed, 'y', 0, 0, tiled=False)  14.9 us
    ppermute x4, waiting for transfers between devices, swap_zh(): return lax.ppermute(value, 'zh', [(0, 1), (1, 0)])  14.7 us
  transfers between devices with their start and end apart: 18, of which 11 were waited for; matrix products, arithmetic and copies ran while one was open for 8% of the time, Pallas kernels for 0%

profile of v9, /device:TPU:1, one launch (start us, length us, event | category | flops | bytes accessed | tf_op | source)
XLA Modules:
  0.0 249.7 jit_solution(3210076816301002074)
XLA Ops:
  0.7 2.3 broadcast_in_dim.60
  2.9 10.3 %all-to-all-start = ((bf16[8,384,256]{2,1,0:T(8,128)(2,1)}), bf16[8,384,256]{2,1,0:T(8,128)(2,1)S(1)}, u32[]{:S(2)}, u32[]{:S(2)}) async-start(bf16[8,384,256]{2,1,0:T(8,128)(2,1)} %broadcast_in_dim.60), calls=%async_computation | async-start | bytes 3145728 | tf_op jit(solution)/shard_map/all_to_all | solution.py:41
  13.2 11.1 %collective-permute-start.8 = (bf16[384,256]{1,0:T(8,128)(2,1)S(1)}, bf16[384,256]{1,0:T(8,128)(2,1)S(1)}, u32[]{:S(2)}, u32[]{:S(2)}) collective-permute-start(bf16[384,256]{1,0:T(8,128)(2,1)S(1)} %bitcast.179), channel_id=1, source_target_pairs={{0,8},{8,0},{1,9},{9,1},{2,10},{10,2},{3,11},{11,3},{4,12},{12,4},... | collective-permute-start | bytes 589832 | tf_op jit(solution)/shard_map/ppermute | solution.py:35
  24.3 5.9 %collective-permute-done.8 = bf16[384,256]{1,0:T(8,128)(2,1)S(1)} collective-permute-done((bf16[384,256]{1,0:T(8,128)(2,1)S(1)}, bf16[384,256]{1,0:T(8,128)(2,1)S(1)}, u32[]{:S(2)}, u32[]{:S(2)}) %collective-permute-start.8) | collective-permute-done | bytes 196640 | tf_op jit(solution)/shard_map/ppermute | solution.py:35
  30.2 3.7 %all-to-all-done = bf16[8,384,256]{2,1,0:T(8,128)(2,1)S(1)} async-done(((bf16[8,384,256]{2,1,0:T(8,128)(2,1)}), bf16[8,384,256]{2,1,0:T(8,128)(2,1)S(1)}, u32[]{:S(2)}, u32[]{:S(2)}) %all-to-all-start) | async-done | bytes 1572896 | tf_op jit(solution)/shard_map/all_to_all | solution.py:41
  33.9 1.3 broadcast_in_dim.61
  35.1 4.4 %all-to-all-start.1 = ((bf16[8,384,256]{2,1,0:T(8,128)(2,1)}), bf16[8,384,256]{2,1,0:T(8,128)(2,1)S(1)}, u32[]{:S(2)}, u32[]{:S(2)}) async-start(bf16[8,384,256]{2,1,0:T(8,128)(2,1)} %broadcast_in_dim.61), calls=%async_computation.1 | async-start | bytes 3145728 | tf_op jit(solution)/shard_map/all_to_all | solution.py:41
  39.6 20.6 %all-to-all-done.1 = bf16[8,384,256]{2,1,0:T(8,128)(2,1)S(1)} async-done(((bf16[8,384,256]{2,1,0:T(8,128)(2,1)}), bf16[8,384,256]{2,1,0:T(8,128)(2,1)S(1)}, u32[]{:S(2)}, u32[]{:S(2)}) %all-to-all-start.1) | async-done | bytes 1572896 | tf_op jit(solution)/shard_map/all_to_all | solution.py:41
  60.2 0.2 broadcast_select_fusion.1
  60.4 0.3 pad_maximum_fusion
  60.7 1.6 copy-done.3
  62.3 1.0 fusion.19
  63.4 1.1 broadcast_in_dim.63
  64.5 4.4 %all-to-all-start.3 = ((bf16[8,256,256]{2,1,0:T(8,128)(2,1)}), bf16[8,256,256]{2,1,0:T(8,128)(2,1)S(1)}, u32[]{:S(2)}, u32[]{:S(2)}) async-start(bf16[8,256,256]{2,1,0:T(8,128)(2,1)} %broadcast_in_dim.63), calls=%async_computation.3 | async-start | bytes 2097152 | tf_op jit(solution)/shard_map/all_to_all | solution.py:41
  68.9 11.2 %collective-permute-start.9 = (bf16[256,256]{0,1:T(8,128)(2,1)S(1)}, bf16[256,256]{0,1:T(8,128)(2,1)S(1)}, u32[]{:S(2)}, u32[]{:S(2)}) collective-permute-start(bf16[256,256]{0,1:T(8,128)(2,1)S(1)} %fusion.19), channel_id=1, source_target_pairs={{0,8},{8,0},{1,9},{9,1},{2,10},{10,2},{3,11},{11,3},{4,12},{12,4},... | collective-permute-start | bytes 393224 | tf_op jit(solution)/shard_map/ppermute | solution.py:35
  80.2 4.4 %collective-permute-done.9 = bf16[256,256]{0,1:T(8,128)(2,1)S(1)} collective-permute-done((bf16[256,256]{0,1:T(8,128)(2,1)S(1)}, bf16[256,256]{0,1:T(8,128)(2,1)S(1)}, u32[]{:S(2)}, u32[]{:S(2)}) %collective-permute-start.9) | collective-permute-done | bytes 131104 | tf_op jit(solution)/shard_map/ppermute | solution.py:35
  84.7 1.1 broadcast_in_dim.62
  85.8 5.4 %all-to-all-start.2 = ((bf16[8,256,256]{2,1,0:T(8,128)(2,1)}), bf16[8,256,256]{2,1,0:T(8,128)(2,1)S(1)}, u32[]{:S(2)}, u32[]{:S(2)}) async-start(bf16[8,256,256]{2,1,0:T(8,128)(2,1)} %broadcast_in_dim.62), calls=%async_computation.2 | async-start | bytes 2097152 | tf_op jit(solution)/shard_map/all_to_all | solution.py:41
  91.8 0.1 broadcast_in_dim.57
  92.2 14.0 %all-to-all-done.2 = bf16[8,256,256]{2,1,0:T(8,128)(2,1)S(1)} async-done(((bf16[8,256,256]{2,1,0:T(8,128)(2,1)}), bf16[8,256,256]{2,1,0:T(8,128)(2,1)S(1)}, u32[]{:S(2)}, u32[]{:S(2)}) %all-to-all-start.2) | async-done | bytes 1048608 | tf_op jit(solution)/shard_map/all_to_all | solution.py:41
  106.2 0.2 pad_maximum_fusion.1
  106.4 0.3 broadcast_in_dim.58
  106.7 1.2 fusion.51
  107.8 0.3 fusion.9
  108.2 0.1 fusion.50
  108.3 0.6 fusion.22
  108.9 0.8 fusion.6
  109.7 0.1 fusion.49
  109.8 1.2 copy-done.4
  111.1 0.5 convolution_convert_fusion.3
  111.5 0.5 convolution_convert_fusion.2
  112.2 2.9 %collective-permute-start.11 = (bf16[4,256,256]{1,2,0:T(8,128)(2,1)S(1)}, bf16[4,256,256]{1,2,0:T(8,128)(2,1)S(1)}, u32[]{:S(2)}, u32[]{:S(2)}) collective-permute-start(bf16[4,256,256]{1,2,0:T(8,128)(2,1)S(1)} %select_bitcast_fusion.1), channel_id=1, source_target_pairs={{0,1},{1,0},{2,3},{3,2},{4,5},{5,4},{6,7},{7,6},{8,9},{9,8},{10,11... | collective-permute-start | bytes 1572872 | tf_op jit(solution)/shard_map/ppermute | solution.py:65
  115.1 0.5 convolution_convert_fusion.5
  115.5 0.5 convolution_convert_fusion.4
  116.2 1.9 collective-permute-start.10
  118.1 1.0 fusion.24
  119.1 3.5 %all-to-all-start.5 = ((bf16[4,256,256]{1,2,0:T(8,128)(2,1)}), bf16[4,256,256]{1,2,0:T(8,128)(2,1)S(1)}, u32[]{:S(2)}, u32[]{:S(2)}) async-start(bf16[4,256,256]{1,2,0:T(8,128)(2,1)} %fusion.24), calls=%async_computation.5 | async-start | bytes 1048576 | tf_op jit(solution)/shard_map/all_to_all | solution.py:67
  122.6 1.0 fusion.25
  123.6 8.0 %all-to-all-done.5 = bf16[4,256,256]{1,2,0:T(8,128)(2,1)S(1)} async-done(((bf16[4,256,256]{1,2,0:T(8,128)(2,1)}), bf16[4,256,256]{1,2,0:T(8,128)(2,1)S(1)}, u32[]{:S(2)}, u32[]{:S(2)}) %all-to-all-start.5) | async-done | bytes 524320 | tf_op jit(solution)/shard_map/all_to_all | solution.py:67
  131.6 3.5 %all-to-all-start.4 = ((bf16[4,256,256]{1,2,0:T(8,128)(2,1)}), bf16[4,256,256]{1,2,0:T(8,128)(2,1)S(1)}, u32[]{:S(2)}, u32[]{:S(2)}) async-start(bf16[4,256,256]{1,2,0:T(8,128)(2,1)} %fusion.25), calls=%async_computation.4 | async-start | bytes 1048576 | tf_op jit(solution)/shard_map/all_to_all | solution.py:67
  135.1 4.7 %copy.86 = bf16[1,256,6144]{1,2,0:T(8,128)(2,1)} copy(bf16[1,256,6144]{2,1,0:T(8,128)(2,1)} %param.10) | data formatting | bytes 6291456 | tf_op args[0]
  139.8 11.1 %collective-permute-start.12 = (bf16[256,256]{0,1:T(8,128)(2,1)S(1)}, bf16[256,256]{0,1:T(8,128)(2,1)S(1)}, u32[]{:S(2)}, u32[]{:S(2)}) collective-permute-start(bf16[256,256]{0,1:T(8,128)(2,1)S(1)} %reduce_sum.63), channel_id=1, source_target_pairs={{0,8},{8,0},{1,9},{9,1},{2,10},{10,2},{3,11},{11,3},{4,12},{12,4},... | collective-permute-start | bytes 393224 | tf_op jit(solution)/shard_map/ppermute | solution.py:35
  151.0 3.3 %collective-permute-done.12 = bf16[256,256]{0,1:T(8,128)(2,1)S(1)} collective-permute-done((bf16[256,256]{0,1:T(8,128)(2,1)S(1)}, bf16[256,256]{0,1:T(8,128)(2,1)S(1)}, u32[]{:S(2)}, u32[]{:S(2)}) %collective-permute-start.12) | collective-permute-done | bytes 131104 | tf_op jit(solution)/shard_map/ppermute | solution.py:35
  154.3 2.1 convolution_convert_fusion
  156.3 1.0 select_bitcast_fusion
  157.4 4.4 %collective-permute-start.14 = (bf16[4,384,256]{2,1,0:T(8,128)(2,1)}, bf16[4,384,256]{2,1,0:T(8,128)(2,1)}, u32[]{:S(2)}, u32[]{:S(2)}) collective-permute-start(bf16[4,384,256]{2,1,0:T(8,128)(2,1)} %select_bitcast_fusion), channel_id=1, source_target_pairs={{0,1},{1,0},{2,3},{3,2},{4,5},{5,4},{6,7},{7,6},{8,9},{9,8},{10,11... | collective-permute-start | bytes 2359304 | tf_op jit(solution)/shard_map/ppermute | solution.py:65
  161.8 2.0 convolution_convert_fusion.1
  163.8 1.0 fusion.32
  164.8 1.9 collective-permute-start.13
  166.7 2.3 fusion.12
  169.1 4.5 %all-to-all-start.7 = ((bf16[4,384,256]{2,1,0:T(8,128)(2,1)}), bf16[4,384,256]{2,1,0:T(8,128)(2,1)}, u32[]{:S(2)}, u32[]{:S(2)}) async-start(bf16[4,384,256]{2,1,0:T(8,128)(2,1)} %fusion.12), calls=%async_computation.7 | async-start | bytes 1572864 | tf_op jit(solution)/shard_map/all_to_all | solution.py:67
  173.6 2.3 fusion.13
  175.9 9.4 %all-to-all-done.7 = bf16[4,384,256]{2,1,0:T(8,128)(2,1)} async-done(((bf16[4,384,256]{2,1,0:T(8,128)(2,1)}), bf16[4,384,256]{2,1,0:T(8,128)(2,1)}, u32[]{:S(2)}, u32[]{:S(2)}) %all-to-all-start.7) | async-done | bytes 786464 | tf_op jit(solution)/shard_map/all_to_all | solution.py:67
  185.3 3.5 %all-to-all-start.6 = ((bf16[4,384,256]{2,1,0:T(8,128)(2,1)}), bf16[4,384,256]{2,1,0:T(8,128)(2,1)S(1)}, u32[]{:S(2)}, u32[]{:S(2)}) async-start(bf16[4,384,256]{2,1,0:T(8,128)(2,1)} %fusion.13), calls=%async_computation.6 | async-start | bytes 1572864 | tf_op jit(solution)/shard_map/all_to_all | solution.py:67
  189.4 1.3 reduce_sum.65
  190.7 11.1 %collective-permute-start.15 = (bf16[384,256]{1,0:T(8,128)(2,1)S(1)}, bf16[384,256]{1,0:T(8,128)(2,1)S(1)}, u32[]{:S(2)}, u32[]{:S(2)}) collective-permute-start(bf16[384,256]{1,0:T(8,128)(2,1)S(1)} %reduce_sum.65), channel_id=1, source_target_pairs={{0,8},{8,0},{1,9},{9,1},{2,10},{10,2},{3,11},{11,3},{4,12},{12,4},... | collective-permute-start | bytes 589832 | tf_op jit(solution)/shard_map/ppermute | solution.py:35
  201.8 3.0 %fusion.23 = bf16[1,256,128]{2,1,0:T(8,128)(2,1)} fusion(bf16[256,4096]{0,1:T(8,128)(2,1)} %copy-done.4, bf16[4096,256]{1,0:T(8,128)(2,1)S(1)} %bitcast.171), kind=kOutput, calls=%fused_computation.42 | convolution fusion | flops 268468224 | bytes 3211264 | tf_op jit(solution)/shard_map/dot_general | solution.py:146
  204.9 1.2 collective-permute-done.15
  206.2 42.8 %conditional.1 = (f32[1,384,256]{2,1,0:T(8,128)S(1)}) conditional(s32[]{:T(128)} %clamp.3, (bf16[384,256]{1,0:T(8,128)(2,1)S(1)}, f32[384,256]{1,0:T(8,128)S(1)}) %fusion.48, (bf16[384,256]{1,0:T(8,128)(2,1)S(1)}, f32[384,256]{1,0:T(8,128)S(1)}) %fusion.48, (bf16[384,256]{1,0:T(8,128)(2,1)S(1)}, ...), branch_computations={%region_7.8_spmd, %region_8.9_spmd, %region_9.10_spmd, %region_10.... | conditional | flops 491520 | bytes 2752600 | solution.py:171
  206.2 3.7 %collective-permute-start.2 = (bf16[384,256]{1,0:T(8,128)(2,1)S(1)}, bf16[384,256]{1,0:T(8,128)(2,1)S(1)}, u32[]{:S(2)}, u32[]{:S(2)}) collective-permute-start(bf16[384,256]{1,0:T(8,128)(2,1)S(1)} %get-tuple-element.25), channel_id=1, source_target_pairs={{0,32},{16,48},{32,64},{48,80},{64,96},{80,112},{96,128},{112,144}... | collective-permute-start | bytes 589832 | tf_op jit(solution)/shard_map/cond/branch_1_fun/ppermute | solution.py:25
  209.9 22.8 %collective-permute-start.3 = (bf16[384,256]{1,0:T(8,128)(2,1)S(1)}, bf16[384,256]{1,0:T(8,128)(2,1)S(1)}, u32[]{:S(2)}, u32[]{:S(2)}) collective-permute-start(bf16[384,256]{1,0:T(8,128)(2,1)S(1)} %get-tuple-element.25), channel_id=1, source_target_pairs={{0,480},{16,496},{32,0},{48,16},{64,32},{80,48},{96,64},{112,80},{... | collective-permute-start | bytes 589832 | tf_op jit(solution)/shard_map/cond/branch_1_fun/ppermute | solution.py:25
  232.7 12.0 %collective-permute-done.2 = bf16[384,256]{1,0:T(8,128)(2,1)S(1)} collective-permute-done((bf16[384,256]{1,0:T(8,128)(2,1)S(1)}, bf16[384,256]{1,0:T(8,128)(2,1)S(1)}, u32[]{:S(2)}, u32[]{:S(2)}) %collective-permute-start.2) | collective-permute-done | bytes 196640 | tf_op jit(solution)/shard_map/cond/branch_1_fun/ppermute | solution.py:25
  244.7 4.2 %collective-permute-done.3 = bf16[384,256]{1,0:T(8,128)(2,1)S(1)} collective-permute-done((bf16[384,256]{1,0:T(8,128)(2,1)S(1)}, bf16[384,256]{1,0:T(8,128)(2,1)S(1)}, u32[]{:S(2)}, u32[]{:S(2)}) %collective-permute-start.3) | collective-permute-done | bytes 196640 | tf_op jit(solution)/shard_map/cond/branch_1_fun/ppermute | solution.py:25
  249.0 0.7 copy-done.7
  (45 shorter events, 1.7 us)
Async XLA Ops:
  0.6 106.0 %copy-start = (bf16[1,256,128]{2,1,0:T(8,128)(2,1)S(1)}, bf16[1,256,128]{2,1,0:T(8,128)(2,1)}, u32[]{:S(2)}) copy-start(bf16[1,256,128]{2,1,0:T(8,128)(2,1)} %param.11) | copy-start | bytes 196612
  0.6 12.6 %copy-start.8 = (bf16[1,384,256]{2,1,0:T(8,128)(2,1)S(1)}, bf16[1,384,256]{2,1,0:T(8,128)(2,1)}, u32[]{:S(2)}) copy-start(bf16[1,384,256]{2,1,0:T(8,128)(2,1)} %param.13) | copy-start | bytes 589828
  2.9 30.9 %all-to-all-start = ((bf16[8,384,256]{2,1,0:T(8,128)(2,1)}), bf16[8,384,256]{2,1,0:T(8,128)(2,1)S(1)}, u32[]{:S(2)}, u32[]{:S(2)}) async-start(bf16[8,384,256]{2,1,0:T(8,128)(2,1)} %broadcast_in_dim.60), calls=%async_computation | async-start | bytes 3145728 | tf_op jit(solution)/shard_map/all_to_all | solution.py:41
  13.2 16.9 %collective-permute-start.8 = (bf16[384,256]{1,0:T(8,128)(2,1)S(1)}, bf16[384,256]{1,0:T(8,128)(2,1)S(1)}, u32[]{:S(2)}, u32[]{:S(2)}) collective-permute-start(bf16[384,256]{1,0:T(8,128)(2,1)S(1)} %bitcast.179), channel_id=1, source_target_pairs={{0,8},{8,0},{1,9},{9,1},{2,10},{10,2},{3,11},{11,3},{4,12},{12,4},... | collective-permute-start | bytes 589832 | tf_op jit(solution)/shard_map/ppermute | solution.py:35
  35.1 25.1 %all-to-all-start.1 = ((bf16[8,384,256]{2,1,0:T(8,128)(2,1)}), bf16[8,384,256]{2,1,0:T(8,128)(2,1)S(1)}, u32[]{:S(2)}, u32[]{:S(2)}) async-start(bf16[8,384,256]{2,1,0:T(8,128)(2,1)} %broadcast_in_dim.61), calls=%async_computation.1 | async-start | bytes 3145728 | tf_op jit(solution)/shard_map/all_to_all | solution.py:41
  60.4 1.9 copy-start.3
  64.5 20.2 %all-to-all-start.3 = ((bf16[8,256,256]{2,1,0:T(8,128)(2,1)}), bf16[8,256,256]{2,1,0:T(8,128)(2,1)S(1)}, u32[]{:S(2)}, u32[]{:S(2)}) async-start(bf16[8,256,256]{2,1,0:T(8,128)(2,1)} %broadcast_in_dim.63), calls=%async_computation.3 | async-start | bytes 2097152 | tf_op jit(solution)/shard_map/all_to_all | solution.py:41
  68.9 22.5 %copy-start.9 = (s32[64,3]{0,1:T(4,128)S(1)}, s32[64,3]{0,1:T(4,128)}, u32[]{:S(2)}) copy-start(s32[64,3]{0,1:T(4,128)} %param.14) | copy-start | bytes 2308
  68.9 23.1 %copy-start.5 = (bf16[1,256,128]{2,1,0:T(8,128)(2,1)S(1)}, bf16[1,256,128]{2,1,0:T(8,128)(2,1)}, u32[]{:S(2)}) copy-start(bf16[1,256,128]{2,1,0:T(8,128)(2,1)} %param.12) | copy-start | bytes 196612
  68.9 15.6 %collective-permute-start.9 = (bf16[256,256]{0,1:T(8,128)(2,1)S(1)}, bf16[256,256]{0,1:T(8,128)(2,1)S(1)}, u32[]{:S(2)}, u32[]{:S(2)}) collective-permute-start(bf16[256,256]{0,1:T(8,128)(2,1)S(1)} %fusion.19), channel_id=1, source_target_pairs={{0,8},{8,0},{1,9},{9,1},{2,10},{10,2},{3,11},{11,3},{4,12},{12,4},... | collective-permute-start | bytes 393224 | tf_op jit(solution)/shard_map/ppermute | solution.py:35
  85.8 20.4 %all-to-all-start.2 = ((bf16[8,256,256]{2,1,0:T(8,128)(2,1)}), bf16[8,256,256]{2,1,0:T(8,128)(2,1)S(1)}, u32[]{:S(2)}, u32[]{:S(2)}) async-start(bf16[8,256,256]{2,1,0:T(8,128)(2,1)} %broadcast_in_dim.62), calls=%async_computation.2 | async-start | bytes 2097152 | tf_op jit(solution)/shard_map/all_to_all | solution.py:41
  106.4 2.5 %copy-start.1 = (bf16[16,256,256]{2,1,0:T(8,128)(2,1)}, bf16[16,256,256]{2,1,0:T(8,128)(2,1)S(1)}, u32[]{:S(2)}) copy-start(bf16[16,256,256]{2,1,0:T(8,128)(2,1)S(1)} %pad_maximum_fusion.1) | copy-start | bytes 6291460
  109.7 1.4 copy-start.4
  112.2 5.9 %collective-permute-start.11 = (bf16[4,256,256]{1,2,0:T(8,128)(2,1)S(1)}, bf16[4,256,256]{1,2,0:T(8,128)(2,1)S(1)}, u32[]{:S(2)}, u32[]{:S(2)}) collective-permute-start(bf16[4,256,256]{1,2,0:T(8,128)(2,1)S(1)} %select_bitcast_fusion.1), channel_id=1, source_target_pairs={{0,1},{1,0},{2,3},{3,2},{4,5},{5,4},{6,7},{7,6},{8,9},{9,8},{10,11... | collective-permute-start | bytes 1572872 | tf_op jit(solution)/shard_map/ppermute | solution.py:65
  116.2 6.4 %collective-permute-start.10 = (bf16[4,256,256]{1,2,0:T(8,128)(2,1)S(1)}, bf16[4,256,256]{1,2,0:T(8,128)(2,1)S(1)}, u32[]{:S(2)}, u32[]{:S(2)}) collective-permute-start(bf16[4,256,256]{1,2,0:T(8,128)(2,1)S(1)} %fusion.34), channel_id=1, source_target_pairs={{0,1},{1,0},{2,3},{3,2},{4,5},{5,4},{6,7},{7,6},{8,9},{9,8},{10,11... | collective-permute-start | bytes 1572872 | tf_op jit(solution)/shard_map/ppermute | solution.py:65
  119.1 12.5 %all-to-all-start.5 = ((bf16[4,256,256]{1,2,0:T(8,128)(2,1)}), bf16[4,256,256]{1,2,0:T(8,128)(2,1)S(1)}, u32[]{:S(2)}, u32[]{:S(2)}) async-start(bf16[4,256,256]{1,2,0:T(8,128)(2,1)} %fusion.24), calls=%async_computation.5 | async-start | bytes 1048576 | tf_op jit(solution)/shard_map/all_to_all | solution.py:67
  131.6 19.3 %all-to-all-start.4 = ((bf16[4,256,256]{1,2,0:T(8,128)(2,1)}), bf16[4,256,256]{1,2,0:T(8,128)(2,1)S(1)}, u32[]{:S(2)}, u32[]{:S(2)}) async-start(bf16[4,256,256]{1,2,0:T(8,128)(2,1)} %fusion.25), calls=%async_computation.4 | async-start | bytes 1048576 | tf_op jit(solution)/shard_map/all_to_all | solution.py:67
  139.8 14.4 %collective-permute-start.12 = (bf16[256,256]{0,1:T(8,128)(2,1)S(1)}, bf16[256,256]{0,1:T(8,128)(2,1)S(1)}, u32[]{:S(2)}, u32[]{:S(2)}) collective-permute-start(bf16[256,256]{0,1:T(8,128)(2,1)S(1)} %reduce_sum.63), channel_id=1, source_target_pairs={{0,8},{8,0},{1,9},{9,1},{2,10},{10,2},{3,11},{11,3},{4,12},{12,4},... | collective-permute-start | bytes 393224 | tf_op jit(solution)/shard_map/ppermute | solution.py:35
  154.3 3.1 %copy-start.6 = (bf16[256,256]{0,1:T(8,128)(2,1)}, bf16[256,256]{0,1:T(8,128)(2,1)S(1)}, u32[]{:S(2)}) copy-start(bf16[256,256]{0,1:T(8,128)(2,1)S(1)} %collective-permute-done.12) | copy-start | bytes 393220
  157.4 9.4 %collective-permute-start.14 = (bf16[4,384,256]{2,1,0:T(8,128)(2,1)}, bf16[4,384,256]{2,1,0:T(8,128)(2,1)}, u32[]{:S(2)}, u32[]{:S(2)}) collective-permute-start(bf16[4,384,256]{2,1,0:T(8,128)(2,1)} %select_bitcast_fusion), channel_id=1, source_target_pairs={{0,1},{1,0},{2,3},{3,2},{4,5},{5,4},{6,7},{7,6},{8,9},{9,8},{10,11... | collective-permute-start | bytes 2359304 | tf_op jit(solution)/shard_map/ppermute | solution.py:65
  164.8 8.7 %collective-permute-start.13 = (bf16[4,384,256]{2,1,0:T(8,128)(2,1)}, bf16[4,384,256]{2,1,0:T(8,128)(2,1)}, u32[]{:S(2)}, u32[]{:S(2)}) collective-permute-start(bf16[4,384,256]{2,1,0:T(8,128)(2,1)} %fusion.32), channel_id=1, source_target_pairs={{0,1},{1,0},{2,3},{3,2},{4,5},{5,4},{6,7},{7,6},{8,9},{9,8},{10,11... | collective-permute-start | bytes 2359304 | tf_op jit(solution)/shard_map/ppermute | solution.py:65
  169.1 16.2 %all-to-all-start.7 = ((bf16[4,384,256]{2,1,0:T(8,128)(2,1)}), bf16[4,384,256]{2,1,0:T(8,128)(2,1)}, u32[]{:S(2)}, u32[]{:S(2)}) async-start(bf16[4,384,256]{2,1,0:T(8,128)(2,1)} %fusion.12), calls=%async_computation.7 | async-start | bytes 1572864 | tf_op jit(solution)/shard_map/all_to_all | solution.py:67
  175.9 25.9 %copy-start.2 = (bf16[16,256,256]{2,1,0:T(8,128)(2,1)S(1)}, bf16[16,256,256]{2,1,0:T(8,128)(2,1)}, u32[]{:S(2)}) copy-start(bf16[16,256,256]{2,1,0:T(8,128)(2,1)} %copy-done.1) | copy-start | bytes 6291460
  185.3 19.5 %all-to-all-start.6 = ((bf16[4,384,256]{2,1,0:T(8,128)(2,1)}), bf16[4,384,256]{2,1,0:T(8,128)(2,1)S(1)}, u32[]{:S(2)}, u32[]{:S(2)}) async-start(bf16[4,384,256]{2,1,0:T(8,128)(2,1)} %fusion.13), calls=%async_computation.6 | async-start | bytes 1572864 | tf_op jit(solution)/shard_map/all_to_all | solution.py:67
  190.7 15.4 %collective-permute-start.15 = (bf16[384,256]{1,0:T(8,128)(2,1)S(1)}, bf16[384,256]{1,0:T(8,128)(2,1)S(1)}, u32[]{:S(2)}, u32[]{:S(2)}) collective-permute-start(bf16[384,256]{1,0:T(8,128)(2,1)S(1)} %reduce_sum.65), channel_id=1, source_target_pairs={{0,8},{8,0},{1,9},{9,1},{2,10},{10,2},{3,11},{11,3},{4,12},{12,4},... | collective-permute-start | bytes 589832 | tf_op jit(solution)/shard_map/ppermute | solution.py:35
  206.2 38.5 %collective-permute-start.2 = (bf16[384,256]{1,0:T(8,128)(2,1)S(1)}, bf16[384,256]{1,0:T(8,128)(2,1)S(1)}, u32[]{:S(2)}, u32[]{:S(2)}) collective-permute-start(bf16[384,256]{1,0:T(8,128)(2,1)S(1)} %get-tuple-element.25), channel_id=1, source_target_pairs={{0,32},{16,48},{32,64},{48,80},{64,96},{80,112},{96,128},{112,144}... | collective-permute-start | bytes 589832 | tf_op jit(solution)/shard_map/cond/branch_1_fun/ppermute | solution.py:25
  209.9 39.0 %collective-permute-start.3 = (bf16[384,256]{1,0:T(8,128)(2,1)S(1)}, bf16[384,256]{1,0:T(8,128)(2,1)S(1)}, u32[]{:S(2)}, u32[]{:S(2)}) collective-permute-start(bf16[384,256]{1,0:T(8,128)(2,1)S(1)} %get-tuple-element.25), channel_id=1, source_target_pairs={{0,480},{16,496},{32,0},{48,16},{64,32},{80,48},{96,64},{112,80},{... | collective-permute-start | bytes 589832 | tf_op jit(solution)/shard_map/cond/branch_1_fun/ppermute | solution.py:25
  249.0 0.7 copy-start.7

commit v10 on v8

--- a/solution.py
+++ b/solution.py
@@ -164,12 +164,12 @@
     kv_grad = scatter_halves(
         terms_for(slice(0, half_keys)), terms_for(slice(half_keys, None))
     ).astype(jnp.bfloat16)
-    tok_view = tokens_here.reshape(tok_count, 2, -1)
-    tok_other = lax.dynamic_index_in_dim(tok_view, 1 - my_half, 1, keepdims=False)
-    tok_mine = lax.dynamic_index_in_dim(tok_view, my_half, 1, keepdims=False)
+    weight_terms = contract_rows(tokens_here, kv_grad).astype(jnp.bfloat16)
+    half_d = weight_terms.shape[0] // 2
+    low_rows, high_rows = weight_terms[:half_d], weight_terms[half_d:]
+    first_own = my_half == 0
     grad_slice = scatter_halves(
-        contract_rows(tok_other, kv_grad).astype(jnp.bfloat16),
-        contract_rows(tok_mine, kv_grad).astype(jnp.bfloat16),
+        jnp.where(first_own, high_rows, low_rows), jnp.where(first_own, low_rows, high_rows)
     )
     branches = [
         partial(gossip, distance=(1 << level_idx) % rep_count, rep_count=rep_count)

time: 254 us -> 279 us (1.098)
  local copies, waits for them, and re-layouts: 15.3 us -> 34.8 us
  other arithmetic: 12.1 us -> 21.3 us
  matrix products: 12.5 us -> 9.45 us
    unnamed x22 -> x29, local copies, waits for them, and re-layouts: 8.34 us -> 15.9 us
    slice x0 -> x2, local copies, waits for them, and re-layouts: none -> 6.62 us  [reduce_half(): keep = jnp.where(first_core, part[:, 0], part[:, 1])]
    reshape x0 -> x2, local copies, waits for them, and re-layouts: none -> 5.22 us  [the longest x1 4.05 us: scatter_halves(): kept = reduce_half(for_me.reshape(shape))]
    dot_general x6 -> x5, matrix products: 5.99 us -> 2.91 us  [contract_rows(): lax.dot_general(matrix_a, matrix_b, (((0,), (0,)), ((), ())), preferred_e...]
  transfers between devices with their start and end apart: 18 -> 18, of which waited for: 11 -> 11; matrix products, arithmetic and copies ran while one was open for 8% -> 12% of each run, Pallas kernels for 0% -> 0%
where the time goes in v10:
time: 279 us; the launch traced here: 275 us
  starting transfers between devices  121 us (43%)
  waiting for transfers between devices  87 us (31%)
  local copies, waits for them, and re-layouts  34.8 us (12%)
  other arithmetic  21.3 us (8%)
  matrix products  9.45 us (3%)
    ppermute x4, starting transfers between devices, swap_zh(): return lax.ppermute(value, 'zh', [(0, 1), (1, 0)])  41.9 us
    all_to_all x4, waiting for transfers between devices, spread_half(): return lax.all_to_all(copies, ('y', 'c'), 0, 0, tiled=False)  38.6 us
    all_to_all x4, starting transfers between devices, spread_half(): return lax.all_to_all(copies, ('y', 'c'), 0, 0, tiled=False)  26.7 us
    ppermute x2, starting transfers between devices, shifted(): return lax.ppermute(value, axis, pairs)  24.9 us
    all_to_all x4, starting transfers between devices, reduce_half(): spread = lax.all_to_all(summed, 'y', 0, 0, tiled=False)  16.3 us
    ppermute x2, waiting for transfers between devices, shifted(): return lax.ppermute(value, axis, pairs)  16.2 us
    all_to_all x4, waiting for transfers between devices, reduce_half(): spread = lax.all_to_all(summed, 'y', 0, 0, tiled=False)  16.1 us
    ppermute x4, waiting for transfers between devices, swap_zh(): return lax.ppermute(value, 'zh', [(0, 1), (1, 0)])  16 us
  transfers between devices with their start and end apart: 18, of which 11 were waited for; matrix products, arithmetic and copies ran while one was open for 12% of the time, Pallas kernels for 0%

profile of v10, /device:TPU:1, one launch (start us, length us, event | category | flops | bytes accessed | tf_op | source)
XLA Modules:
  0.0 275.4 jit_solution(2445601458639127508)
XLA Ops:
  0.7 2.3 broadcast_in_dim.60
  3.0 11.0 %all-to-all-start = ((bf16[8,384,256]{2,1,0:T(8,128)(2,1)}), bf16[8,384,256]{2,1,0:T(8,128)(2,1)}, u32[]{:S(2)}, u32[]{:S(2)}) async-start(bf16[8,384,256]{2,1,0:T(8,128)(2,1)} %broadcast_in_dim.60), calls=%async_computation | async-start | bytes 3145728 | tf_op jit(solution)/shard_map/all_to_all | solution.py:41
  14.0 10.4 %collective-permute-start.8 = (bf16[384,256]{1,0:T(8,128)(2,1)S(1)}, bf16[384,256]{1,0:T(8,128)(2,1)S(1)}, u32[]{:S(2)}, u32[]{:S(2)}) collective-permute-start(bf16[384,256]{1,0:T(8,128)(2,1)S(1)} %bitcast.142), channel_id=1, source_target_pairs={{0,8},{8,0},{1,9},{9,1},{2,10},{10,2},{3,11},{11,3},{4,12},{12,4},... | collective-permute-start | bytes 589832 | tf_op jit(solution)/shard_map/ppermute | solution.py:35
  24.4 6.5 %collective-permute-done.8 = bf16[384,256]{1,0:T(8,128)(2,1)S(1)} collective-permute-done((bf16[384,256]{1,0:T(8,128)(2,1)S(1)}, bf16[384,256]{1,0:T(8,128)(2,1)S(1)}, u32[]{:S(2)}, u32[]{:S(2)}) %collective-permute-start.8) | collective-permute-done | bytes 196640 | tf_op jit(solution)/shard_map/ppermute | solution.py:35
  30.9 3.8 %all-to-all-done = bf16[8,384,256]{2,1,0:T(8,128)(2,1)} async-done(((bf16[8,384,256]{2,1,0:T(8,128)(2,1)}), bf16[8,384,256]{2,1,0:T(8,128)(2,1)}, u32[]{:S(2)}, u32[]{:S(2)}) %all-to-all-start) | async-done | bytes 1572896 | tf_op jit(solution)/shard_map/all_to_all | solution.py:41
  34.7 1.3 broadcast_in_dim.61
  36.0 5.2 %all-to-all-start.1 = ((bf16[8,384,256]{2,1,0:T(8,128)(2,1)}), bf16[8,384,256]{2,1,0:T(8,128)(2,1)}, u32[]{:S(2)}, u32[]{:S(2)}) async-start(bf16[8,384,256]{2,1,0:T(8,128)(2,1)} %broadcast_in_dim.61), calls=%async_computation.1 | async-start | bytes 3145728 | tf_op jit(solution)/shard_map/all_to_all | solution.py:41
  41.2 20.7 %all-to-all-done.1 = bf16[8,384,256]{2,1,0:T(8,128)(2,1)} async-done(((bf16[8,384,256]{2,1,0:T(8,128)(2,1)}), bf16[8,384,256]{2,1,0:T(8,128)(2,1)}, u32[]{:S(2)}, u32[]{:S(2)}) %all-to-all-start.1) | async-done | bytes 1572896 | tf_op jit(solution)/shard_map/all_to_all | solution.py:41
  61.9 2.1 broadcast_select_fusion.1
  64.3 1.1 fusion.17
  65.5 1.0 broadcast_in_dim.63
  66.5 5.1 %all-to-all-start.3 = ((bf16[8,256,256]{2,1,0:T(8,128)(2,1)}), bf16[8,256,256]{2,1,0:T(8,128)(2,1)}, u32[]{:S(2)}, u32[]{:S(2)}) async-start(bf16[8,256,256]{2,1,0:T(8,128)(2,1)} %broadcast_in_dim.63), calls=%async_computation.3 | async-start | bytes 2097152 | tf_op jit(solution)/shard_map/all_to_all | solution.py:41
  71.6 10.5 %collective-permute-start.9 = (bf16[256,256]{0,1:T(8,128)(2,1)S(1)}, bf16[256,256]{0,1:T(8,128)(2,1)S(1)}, u32[]{:S(2)}, u32[]{:S(2)}) collective-permute-start(bf16[256,256]{0,1:T(8,128)(2,1)S(1)} %fusion.17), channel_id=1, source_target_pairs={{0,8},{8,0},{1,9},{9,1},{2,10},{10,2},{3,11},{11,3},{4,12},{12,4},... | collective-permute-start | bytes 393224 | tf_op jit(solution)/shard_map/ppermute | solution.py:35
  82.2 5.0 %collective-permute-done.9 = bf16[256,256]{0,1:T(8,128)(2,1)S(1)} collective-permute-done((bf16[256,256]{0,1:T(8,128)(2,1)S(1)}, bf16[256,256]{0,1:T(8,128)(2,1)S(1)}, u32[]{:S(2)}, u32[]{:S(2)}) %collective-permute-start.9) | collective-permute-done | bytes 131104 | tf_op jit(solution)/shard_map/ppermute | solution.py:35
  87.3 1.1 broadcast_in_dim.62
  88.4 5.5 %all-to-all-start.2 = ((bf16[8,256,256]{2,1,0:T(8,128)(2,1)}), bf16[8,256,256]{2,1,0:T(8,128)(2,1)}, u32[]{:S(2)}, u32[]{:S(2)}) async-start(bf16[8,256,256]{2,1,0:T(8,128)(2,1)} %broadcast_in_dim.62), calls=%async_computation.2 | async-start | bytes 2097152 | tf_op jit(solution)/shard_map/all_to_all | solution.py:41
  94.8 14.1 %all-to-all-done.2 = bf16[8,256,256]{2,1,0:T(8,128)(2,1)} async-done(((bf16[8,256,256]{2,1,0:T(8,128)(2,1)}), bf16[8,256,256]{2,1,0:T(8,128)(2,1)}, u32[]{:S(2)}, u32[]{:S(2)}) %all-to-all-start.2) | async-done | bytes 1048608 | tf_op jit(solution)/shard_map/all_to_all | solution.py:41
  108.9 1.7 pad_maximum_fusion.1
  110.9 1.2 fusion.50
  112.6 0.6 fusion.20
  113.2 0.8 fusion.7
  114.1 1.2 copy-done.6
  116.4 2.9 %collective-permute-start.11 = (bf16[4,256,256]{1,2,0:T(8,128)(2,1)S(1)}, bf16[4,256,256]{1,2,0:T(8,128)(2,1)S(1)}, u32[]{:S(2)}, u32[]{:S(2)}) collective-permute-start(bf16[4,256,256]{1,2,0:T(8,128)(2,1)S(1)} %select_bitcast_fusion.2), channel_id=1, source_target_pairs={{0,1},{1,0},{2,3},{3,2},{4,5},{5,4},{6,7},{7,6},{8,9},{9,8},{10,11... | collective-permute-start | bytes 1572872 | tf_op jit(solution)/shard_map/ppermute | solution.py:65
  120.6 1.0 fusion.30
  121.6 1.9 collective-permute-start.10
  123.5 1.0 fusion.22
  124.5 4.1 %all-to-all-start.5 = ((bf16[4,256,256]{1,2,0:T(8,128)(2,1)}), bf16[4,256,256]{1,2,0:T(8,128)(2,1)}, u32[]{:S(2)}, u32[]{:S(2)}) async-start(bf16[4,256,256]{1,2,0:T(8,128)(2,1)} %fusion.22), calls=%async_computation.5 | async-start | bytes 1048576 | tf_op jit(solution)/shard_map/all_to_all | solution.py:67
  128.7 2.4 fusion.23
  131.1 6.8 %all-to-all-done.5 = bf16[4,256,256]{1,2,0:T(8,128)(2,1)} async-done(((bf16[4,256,256]{1,2,0:T(8,128)(2,1)}), bf16[4,256,256]{1,2,0:T(8,128)(2,1)}, u32[]{:S(2)}, u32[]{:S(2)}) %all-to-all-start.5) | async-done | bytes 524320 | tf_op jit(solution)/shard_map/all_to_all | solution.py:67
  137.8 4.2 %all-to-all-start.4 = ((bf16[4,256,256]{1,2,0:T(8,128)(2,1)}), bf16[4,256,256]{1,2,0:T(8,128)(2,1)}, u32[]{:S(2)}, u32[]{:S(2)}) async-start(bf16[4,256,256]{1,2,0:T(8,128)(2,1)} %fusion.23), calls=%async_computation.4 | async-start | bytes 1048576 | tf_op jit(solution)/shard_map/all_to_all | solution.py:67
  142.0 1.1 reduce_sum.82
  143.1 10.6 %collective-permute-start.12 = (bf16[256,256]{0,1:T(8,128)(2,1)S(1)}, bf16[256,256]{0,1:T(8,128)(2,1)S(1)}, u32[]{:S(2)}, u32[]{:S(2)}) collective-permute-start(bf16[256,256]{0,1:T(8,128)(2,1)S(1)} %reduce_sum.82), channel_id=1, source_target_pairs={{0,8},{8,0},{1,9},{9,1},{2,10},{10,2},{3,11},{11,3},{4,12},{12,4},... | collective-permute-start | bytes 393224 | tf_op jit(solution)/shard_map/ppermute | solution.py:35
  153.8 1.1 convert_reduce_fusion
  154.9 2.6 collective-permute-done.12
  157.5 1.0 fusion
  158.5 1.4 broadcast_select_fusion.2
  159.9 1.2 reshape.123
  161.1 3.1 %fusion.48 = (bf16[4,1,384,256]{2,1,0,3:T(2,128)(2,1)}, bf16[4,1,384,256]{2,1,0,3:T(2,128)(2,1)S(1)}) fusion(bf16[4,2,384,256]{2,1,0,3:T(2,128)(2,1)S(1)} %reshape.123), kind=kLoop, calls=%fused_computation.90 | loop fusion | bytes 3145728 | tf_op jit(solution)/shard_map/slice | solution.py:63
  164.2 3.4 %copy.85 = bf16[4,1,384,256]{3,2,0,1:T(8,128)(2,1)S(1)} copy(bf16[4,1,384,256]{2,1,0,3:T(2,128)(2,1)} %get-tuple-element.60) | data formatting | bytes 1572864
  167.7 1.9 copy.86
  169.6 1.0 select_bitcast_fusion
  170.6 4.4 %collective-permute-start.14 = (bf16[4,384,256]{2,1,0:T(8,128)(2,1)}, bf16[4,384,256]{2,1,0:T(8,128)(2,1)}, u32[]{:S(2)}, u32[]{:S(2)}) collective-permute-start(bf16[4,384,256]{2,1,0:T(8,128)(2,1)} %select_bitcast_fusion), channel_id=1, source_target_pairs={{0,1},{1,0},{2,3},{3,2},{4,5},{5,4},{6,7},{7,6},{8,9},{9,8},{10,11... | collective-permute-start | bytes 2359304 | tf_op jit(solution)/shard_map/ppermute | solution.py:65
  175.1 4.1 %reshape.122 = bf16[4,2,384,256]{2,1,0,3:T(2,128)(2,1)S(1)} reshape(bf16[3072,256]{0,1:T(8,128)(2,1)} %get-tuple-element.53) | data formatting | bytes 3145728 | tf_op jit(solution)/shard_map/reshape | solution.py:76
  179.1 3.5 %fusion.49 = (bf16[4,1,384,256]{2,1,0,3:T(2,128)(2,1)}, bf16[4,1,384,256]{2,1,0,3:T(2,128)(2,1)}) fusion(bf16[4,2,384,256]{2,1,0,3:T(2,128)(2,1)S(1)} %reshape.122), kind=kLoop, calls=%fused_computation.91 | loop fusion | bytes 3145728 | tf_op jit(solution)/shard_map/slice | solution.py:63
  182.6 3.4 %copy.83 = bf16[4,1,384,256]{3,2,0,1:T(8,128)(2,1)S(1)} copy(bf16[4,1,384,256]{2,1,0,3:T(2,128)(2,1)} %get-tuple-element.62) | data formatting | bytes 1572864
  186.1 3.4 %copy.84 = bf16[4,1,384,256]{3,2,0,1:T(8,128)(2,1)S(1)} copy(bf16[4,1,384,256]{2,1,0,3:T(2,128)(2,1)} %get-tuple-element.63) | data formatting | bytes 1572864
  189.5 1.0 select_bitcast_fusion.1
  190.5 1.9 collective-permute-start.13
  192.5 2.3 fusion.12
  194.8 4.5 %all-to-all-start.7 = ((bf16[4,384,256]{2,1,0:T(8,128)(2,1)}), bf16[4,384,256]{2,1,0:T(8,128)(2,1)}, u32[]{:S(2)}, u32[]{:S(2)}) async-start(bf16[4,384,256]{2,1,0:T(8,128)(2,1)} %fusion.12), calls=%async_computation.7 | async-start | bytes 1572864 | tf_op jit(solution)/shard_map/all_to_all | solution.py:67
  199.3 2.4 fusion.13
  201.6 9.3 %all-to-all-done.7 = bf16[4,384,256]{2,1,0:T(8,128)(2,1)} async-done(((bf16[4,384,256]{2,1,0:T(8,128)(2,1)}), bf16[4,384,256]{2,1,0:T(8,128)(2,1)}, u32[]{:S(2)}, u32[]{:S(2)}) %all-to-all-start.7) | async-done | bytes 786464 | tf_op jit(solution)/shard_map/all_to_all | solution.py:67
  211.0 3.5 %all-to-all-start.6 = ((bf16[4,384,256]{2,1,0:T(8,128)(2,1)}), bf16[4,384,256]{2,1,0:T(8,128)(2,1)S(1)}, u32[]{:S(2)}, u32[]{:S(2)}) async-start(bf16[4,384,256]{2,1,0:T(8,128)(2,1)} %fusion.13), calls=%async_computation.6 | async-start | bytes 1572864 | tf_op jit(solution)/shard_map/all_to_all | solution.py:67
  215.2 1.3 reduce_sum.83
  216.5 10.5 %collective-permute-start.15 = (bf16[384,256]{1,0:T(8,128)(2,1)S(1)}, bf16[384,256]{1,0:T(8,128)(2,1)S(1)}, u32[]{:S(2)}, u32[]{:S(2)}) collective-permute-start(bf16[384,256]{1,0:T(8,128)(2,1)S(1)} %reduce_sum.83), channel_id=1, source_target_pairs={{0,8},{8,0},{1,9},{9,1},{2,10},{10,2},{3,11},{11,3},{4,12},{12,4},... | collective-permute-start | bytes 589832 | tf_op jit(solution)/shard_map/ppermute | solution.py:35
  226.9 3.0 %fusion.21 = bf16[1,256,128]{2,1,0:T(8,128)(2,1)} fusion(bf16[256,4096]{0,1:T(8,128)(2,1)} %copy-done.6, bf16[4096,256]{1,0:T(8,128)(2,1)S(1)} %bitcast.134), kind=kOutput, calls=%fused_computation.39 | convolution fusion | flops 268468224 | bytes 3211264 | tf_op jit(solution)/shard_map/dot_general | solution.py:153
  230.1 1.8 collective-permute-done.15
  231.9 41.4 %conditional.1 = (f32[1,384,256]{2,1,0:T(8,128)S(1)}) conditional(s32[]{:T(128)} %clamp.3, (f32[4,384,256]{2,1,0:T(8,128)S(1)}, f32[384,256]{1,0:T(8,128)S(1)}) %tuple.28, (f32[4,384,256]{2,1,0:T(8,128)S(1)}, f32[384,256]{1,0:T(8,128)S(1)}) %tuple.28, (f32[4,384,256]{2,1,0:T(8,128)S(1)}, ...), branch_computations={%region_6.8_spmd, %region_8.10_spmd, %region_10.12_spmd, %region_1... | conditional | flops 983040 | bytes 6094940 | solution.py:178
  232.1 3.1 %collective-permute-start.2 = (bf16[384,256]{1,0:T(8,128)(2,1)S(1)}, bf16[384,256]{1,0:T(8,128)(2,1)S(1)}, u32[]{:S(2)}, u32[]{:S(2)}) collective-permute-start(bf16[384,256]{1,0:T(8,128)(2,1)S(1)} %get-tuple-element.46), channel_id=1, source_target_pairs={{0,32},{16,48},{32,64},{48,80},{64,96},{80,112},{96,128},{112,144}... | collective-permute-start | bytes 589832 | tf_op jit(solution)/shard_map/cond/branch_1_fun/ppermute | solution.py:25
  235.2 21.8 %collective-permute-start.3 = (bf16[384,256]{1,0:T(8,128)(2,1)S(1)}, bf16[384,256]{1,0:T(8,128)(2,1)S(1)}, u32[]{:S(2)}, u32[]{:S(2)}) collective-permute-start(bf16[384,256]{1,0:T(8,128)(2,1)S(1)} %get-tuple-element.46), channel_id=1, source_target_pairs={{0,480},{16,496},{32,0},{48,16},{64,32},{80,48},{96,64},{112,80},{... | collective-permute-start | bytes 589832 | tf_op jit(solution)/shard_map/cond/branch_1_fun/ppermute | solution.py:25
  257.1 11.8 %collective-permute-done.2 = bf16[384,256]{1,0:T(8,128)(2,1)S(1)} collective-permute-done((bf16[384,256]{1,0:T(8,128)(2,1)S(1)}, bf16[384,256]{1,0:T(8,128)(2,1)S(1)}, u32[]{:S(2)}, u32[]{:S(2)}) %collective-permute-start.2) | collective-permute-done | bytes 196640 | tf_op jit(solution)/shard_map/cond/branch_1_fun/ppermute | solution.py:25
  268.9 4.4 %collective-permute-done.3 = bf16[384,256]{1,0:T(8,128)(2,1)S(1)} collective-permute-done((bf16[384,256]{1,0:T(8,128)(2,1)S(1)}, bf16[384,256]{1,0:T(8,128)(2,1)S(1)}, u32[]{:S(2)}, u32[]{:S(2)}) %collective-permute-start.3) | collective-permute-done | bytes 196640 | tf_op jit(solution)/shard_map/cond/branch_1_fun/ppermute | solution.py:25
  273.3 0.7 copy-done.9
  274.1 1.3 copy-done.1
  (58 shorter events, 5.2 us)
Async XLA Ops:
  0.6 63.7 %copy-start = (bf16[1,256,6144]{2,1,0:T(8,128)(2,1)S(1)}, bf16[1,256,6144]{2,1,0:T(8,128)(2,1)}, u32[]{:S(2)}) copy-start(bf16[1,256,6144]{2,1,0:T(8,128)(2,1)} %param.10) | copy-start | bytes 9437188
  0.6 13.4 %copy-start.10 = (bf16[1,384,256]{2,1,0:T(8,128)(2,1)S(1)}, bf16[1,384,256]{2,1,0:T(8,128)(2,1)}, u32[]{:S(2)}) copy-start(bf16[1,384,256]{2,1,0:T(8,128)(2,1)} %param.13) | copy-start | bytes 589828
  3.0 31.7 %all-to-all-start = ((bf16[8,384,256]{2,1,0:T(8,128)(2,1)}), bf16[8,384,256]{2,1,0:T(8,128)(2,1)}, u32[]{:S(2)}, u32[]{:S(2)}) async-start(bf16[8,384,256]{2,1,0:T(8,128)(2,1)} %broadcast_in_dim.60), calls=%async_computation | async-start | bytes 3145728 | tf_op jit(solution)/shard_map/all_to_all | solution.py:41
  14.0 16.9 %collective-permute-start.8 = (bf16[384,256]{1,0:T(8,128)(2,1)S(1)}, bf16[384,256]{1,0:T(8,128)(2,1)S(1)}, u32[]{:S(2)}, u32[]{:S(2)}) collective-permute-start(bf16[384,256]{1,0:T(8,128)(2,1)S(1)} %bitcast.142), channel_id=1, source_target_pairs={{0,8},{8,0},{1,9},{9,1},{2,10},{10,2},{3,11},{11,3},{4,12},{12,4},... | collective-permute-start | bytes 589832 | tf_op jit(solution)/shard_map/ppermute | solution.py:35
  36.0 25.9 %all-to-all-start.1 = ((bf16[8,384,256]{2,1,0:T(8,128)(2,1)}), bf16[8,384,256]{2,1,0:T(8,128)(2,1)}, u32[]{:S(2)}, u32[]{:S(2)}) async-start(bf16[8,384,256]{2,1,0:T(8,128)(2,1)} %broadcast_in_dim.61), calls=%async_computation.1 | async-start | bytes 3145728 | tf_op jit(solution)/shard_map/all_to_all | solution.py:41
  66.5 20.8 %all-to-all-start.3 = ((bf16[8,256,256]{2,1,0:T(8,128)(2,1)}), bf16[8,256,256]{2,1,0:T(8,128)(2,1)}, u32[]{:S(2)}, u32[]{:S(2)}) async-start(bf16[8,256,256]{2,1,0:T(8,128)(2,1)} %broadcast_in_dim.63), calls=%async_computation.3 | async-start | bytes 2097152 | tf_op jit(solution)/shard_map/all_to_all | solution.py:41
  71.6 22.4 %copy-start.11 = (s32[64,3]{0,1:T(4,128)S(1)}, s32[64,3]{0,1:T(4,128)}, u32[]{:S(2)}) copy-start(s32[64,3]{0,1:T(4,128)} %param.14) | copy-start | bytes 2308
  71.6 23.1 %copy-start.8 = (bf16[1,256,128]{2,1,0:T(8,128)(2,1)S(1)}, bf16[1,256,128]{2,1,0:T(8,128)(2,1)}, u32[]{:S(2)}) copy-start(bf16[1,256,128]{2,1,0:T(8,128)(2,1)} %param.12) | copy-start | bytes 196612
  71.6 15.6 %collective-permute-start.9 = (bf16[256,256]{0,1:T(8,128)(2,1)S(1)}, bf16[256,256]{0,1:T(8,128)(2,1)S(1)}, u32[]{:S(2)}, u32[]{:S(2)}) collective-permute-start(bf16[256,256]{0,1:T(8,128)(2,1)S(1)} %fusion.17), channel_id=1, source_target_pairs={{0,8},{8,0},{1,9},{9,1},{2,10},{10,2},{3,11},{11,3},{4,12},{12,4},... | collective-permute-start | bytes 393224 | tf_op jit(solution)/shard_map/ppermute | solution.py:35
  88.4 20.5 %all-to-all-start.2 = ((bf16[8,256,256]{2,1,0:T(8,128)(2,1)}), bf16[8,256,256]{2,1,0:T(8,128)(2,1)}, u32[]{:S(2)}, u32[]{:S(2)}) async-start(bf16[8,256,256]{2,1,0:T(8,128)(2,1)} %broadcast_in_dim.62), calls=%async_computation.2 | async-start | bytes 2097152 | tf_op jit(solution)/shard_map/all_to_all | solution.py:41
  94.8 16.2 %copy-start.7 = (bf16[1,256,128]{2,1,0:T(8,128)(2,1)S(1)}, bf16[1,256,128]{2,1,0:T(8,128)(2,1)}, u32[]{:S(2)}) copy-start(bf16[1,256,128]{2,1,0:T(8,128)(2,1)} %param.11) | copy-start | bytes 196612
  110.6 2.5 copy-start.4
  114.0 1.3 copy-start.6
  116.4 7.1 %collective-permute-start.11 = (bf16[4,256,256]{1,2,0:T(8,128)(2,1)S(1)}, bf16[4,256,256]{1,2,0:T(8,128)(2,1)S(1)}, u32[]{:S(2)}, u32[]{:S(2)}) collective-permute-start(bf16[4,256,256]{1,2,0:T(8,128)(2,1)S(1)} %select_bitcast_fusion.2), channel_id=1, source_target_pairs={{0,1},{1,0},{2,3},{3,2},{4,5},{5,4},{6,7},{7,6},{8,9},{9,8},{10,11... | collective-permute-start | bytes 1572872 | tf_op jit(solution)/shard_map/ppermute | solution.py:65
  119.8 0.8 copy-start.2
  120.6 1.0 copy-start.3
  121.6 7.1 %collective-permute-start.10 = (bf16[4,256,256]{1,2,0:T(8,128)(2,1)}, bf16[4,256,256]{1,2,0:T(8,128)(2,1)}, u32[]{:S(2)}, u32[]{:S(2)}) collective-permute-start(bf16[4,256,256]{1,2,0:T(8,128)(2,1)} %fusion.30), channel_id=1, source_target_pairs={{0,1},{1,0},{2,3},{3,2},{4,5},{5,4},{6,7},{7,6},{8,9},{9,8},{10,11... | collective-permute-start | bytes 1572872 | tf_op jit(solution)/shard_map/ppermute | solution.py:65
  124.5 13.3 %all-to-all-start.5 = ((bf16[4,256,256]{1,2,0:T(8,128)(2,1)}), bf16[4,256,256]{1,2,0:T(8,128)(2,1)}, u32[]{:S(2)}, u32[]{:S(2)}) async-start(bf16[4,256,256]{1,2,0:T(8,128)(2,1)} %fusion.22), calls=%async_computation.5 | async-start | bytes 1048576 | tf_op jit(solution)/shard_map/all_to_all | solution.py:67
  137.8 15.9 %all-to-all-start.4 = ((bf16[4,256,256]{1,2,0:T(8,128)(2,1)}), bf16[4,256,256]{1,2,0:T(8,128)(2,1)}, u32[]{:S(2)}, u32[]{:S(2)}) async-start(bf16[4,256,256]{1,2,0:T(8,128)(2,1)} %fusion.23), calls=%async_computation.4 | async-start | bytes 1048576 | tf_op jit(solution)/shard_map/all_to_all | solution.py:67
  143.1 14.4 %collective-permute-start.12 = (bf16[256,256]{0,1:T(8,128)(2,1)S(1)}, bf16[256,256]{0,1:T(8,128)(2,1)S(1)}, u32[]{:S(2)}, u32[]{:S(2)}) collective-permute-start(bf16[256,256]{0,1:T(8,128)(2,1)S(1)} %reduce_sum.82), channel_id=1, source_target_pairs={{0,8},{8,0},{1,9},{9,1},{2,10},{10,2},{3,11},{11,3},{4,12},{12,4},... | collective-permute-start | bytes 393224 | tf_op jit(solution)/shard_map/ppermute | solution.py:35
  170.6 21.8 %collective-permute-start.14 = (bf16[4,384,256]{2,1,0:T(8,128)(2,1)}, bf16[4,384,256]{2,1,0:T(8,128)(2,1)}, u32[]{:S(2)}, u32[]{:S(2)}) collective-permute-start(bf16[4,384,256]{2,1,0:T(8,128)(2,1)} %select_bitcast_fusion), channel_id=1, source_target_pairs={{0,1},{1,0},{2,3},{3,2},{4,5},{5,4},{6,7},{7,6},{8,9},{9,8},{10,11... | collective-permute-start | bytes 2359304 | tf_op jit(solution)/shard_map/ppermute | solution.py:65
  190.5 8.7 %collective-permute-start.13 = (bf16[4,384,256]{2,1,0:T(8,128)(2,1)}, bf16[4,384,256]{2,1,0:T(8,128)(2,1)}, u32[]{:S(2)}, u32[]{:S(2)}) collective-permute-start(bf16[4,384,256]{2,1,0:T(8,128)(2,1)} %select_bitcast_fusion.1), channel_id=1, source_target_pairs={{0,1},{1,0},{2,3},{3,2},{4,5},{5,4},{6,7},{7,6},{8,9},{9,8},{10,11... | collective-permute-start | bytes 2359304 | tf_op jit(solution)/shard_map/ppermute | solution.py:65
  194.8 16.2 %all-to-all-start.7 = ((bf16[4,384,256]{2,1,0:T(8,128)(2,1)}), bf16[4,384,256]{2,1,0:T(8,128)(2,1)}, u32[]{:S(2)}, u32[]{:S(2)}) async-start(bf16[4,384,256]{2,1,0:T(8,128)(2,1)} %fusion.12), calls=%async_computation.7 | async-start | bytes 1572864 | tf_op jit(solution)/shard_map/all_to_all | solution.py:67
  201.6 25.3 %copy-start.5 = (bf16[16,256,256]{2,1,0:T(8,128)(2,1)S(1)}, bf16[16,256,256]{2,1,0:T(8,128)(2,1)}, u32[]{:S(2)}) copy-start(bf16[16,256,256]{2,1,0:T(8,128)(2,1)} %copy-done.4) | copy-start | bytes 6291460
  211.0 18.9 %all-to-all-start.6 = ((bf16[4,384,256]{2,1,0:T(8,128)(2,1)}), bf16[4,384,256]{2,1,0:T(8,128)(2,1)S(1)}, u32[]{:S(2)}, u32[]{:S(2)}) async-start(bf16[4,384,256]{2,1,0:T(8,128)(2,1)} %fusion.13), calls=%async_computation.6 | async-start | bytes 1572864 | tf_op jit(solution)/shard_map/all_to_all | solution.py:67
  216.5 15.4 %collective-permute-start.15 = (bf16[384,256]{1,0:T(8,128)(2,1)S(1)}, bf16[384,256]{1,0:T(8,128)(2,1)S(1)}, u32[]{:S(2)}, u32[]{:S(2)}) collective-permute-start(bf16[384,256]{1,0:T(8,128)(2,1)S(1)} %reduce_sum.83), channel_id=1, source_target_pairs={{0,8},{8,0},{1,9},{9,1},{2,10},{10,2},{3,11},{11,3},{4,12},{12,4},... | collective-permute-start | bytes 589832 | tf_op jit(solution)/shard_map/ppermute | solution.py:35
  232.1 36.7 %collective-permute-start.2 = (bf16[384,256]{1,0:T(8,128)(2,1)S(1)}, bf16[384,256]{1,0:T(8,128)(2,1)S(1)}, u32[]{:S(2)}, u32[]{:S(2)}) collective-permute-start(bf16[384,256]{1,0:T(8,128)(2,1)S(1)} %get-tuple-element.46), channel_id=1, source_target_pairs={{0,32},{16,48},{32,64},{48,80},{64,96},{80,112},{96,128},{112,144}... | collective-permute-start | bytes 589832 | tf_op jit(solution)/shard_map/cond/branch_1_fun/ppermute | solution.py:25
  235.2 38.0 %collective-permute-start.3 = (bf16[384,256]{1,0:T(8,128)(2,1)S(1)}, bf16[384,256]{1,0:T(8,128)(2,1)S(1)}, u32[]{:S(2)}, u32[]{:S(2)}) collective-permute-start(bf16[384,256]{1,0:T(8,128)(2,1)S(1)} %get-tuple-element.46), channel_id=1, source_target_pairs={{0,480},{16,496},{32,0},{48,16},{64,32},{80,48},{96,64},{112,80},{... | collective-permute-start | bytes 589832 | tf_op jit(solution)/shard_map/cond/branch_1_fun/ppermute | solution.py:25
  273.3 0.7 copy-start.9
  273.3 2.0 copy-start.1

commit v11 on v8

--- a/solution.py
+++ b/solution.py
@@ -73,6 +73,7 @@
     shape = (y_n, c_n, for_other.shape[0] // (y_n * c_n)) + for_other.shape[1:]
     reduced = reduce_half(for_other.reshape(shape)).astype(jnp.bfloat16)
     got = swap_zh(reduced)
+    for_me = for_me() if callable(for_me) else for_me
     kept = reduce_half(for_me.reshape(shape))
     return kept + got.astype(jnp.float32)
 
@@ -162,14 +163,13 @@
         ).astype(jnp.bfloat16)
 
     kv_grad = scatter_halves(
-        terms_for(slice(0, half_keys)), terms_for(slice(half_keys, None))
+        terms_for(slice(0, half_keys)), lambda: terms_for(slice(half_keys, None))
     ).astype(jnp.bfloat16)
     tok_view = tokens_here.reshape(tok_count, 2, -1)
     tok_other = lax.dynamic_index_in_dim(tok_view, 1 - my_half, 1, keepdims=False)
     tok_mine = lax.dynamic_index_in_dim(tok_view, my_half, 1, keepdims=False)
     grad_slice = scatter_halves(
-        contract_rows(tok_other, kv_grad).astype(jnp.bfloat16),
-        contract_rows(tok_mine, kv_grad).astype(jnp.bfloat16),
+        contract_rows(tok_other, kv_grad).astype(jnp.bfloat16), contract_rows(tok_mine, kv_grad).astype(jnp.bfloat16)
     )
     branches = [
         partial(gossip, distance=(1 << level_idx) % rep_count, rep_count=rep_count)

time: 254 us -> 254 us (level)
  no operation moved by 1% of the time
where the time goes in v11:
time: 254 us; the launch traced here: 250 us
  starting transfers between devices  122 us (48%)
  waiting for transfers between devices  86.6 us (34%)
  local copies, waits for them, and re-layouts  15.3 us (6%)
  matrix products  12.5 us (5%)
  other arithmetic  12.1 us (5%)
    ppermute x4, starting transfers between devices, swap_zh(): return lax.ppermute(value, 'zh', [(0, 1), (1, 0)])  44.4 us
    all_to_all x4, waiting for transfers between devices, spread_half(): return lax.all_to_all(copies, ('y', 'c'), 0, 0, tiled=False)  38.3 us
    ppermute x2, starting transfers between devices, shifted(): return lax.ppermute(value, axis, pairs)  26.5 us
    all_to_all x4, starting transfers between devices, spread_half(): return lax.all_to_all(copies, ('y', 'c'), 0, 0, tiled=False)  24.6 us
    all_to_all x4, waiting for transfers between devices, reduce_half(): spread = lax.all_to_all(summed, 'y', 0, 0, tiled=False)  17.4 us
    ppermute x2, waiting for transfers between devices, shifted(): return lax.ppermute(value, axis, pairs)  16.2 us
    all_to_all x4, starting transfers between devices, reduce_half(): spread = lax.all_to_all(summed, 'y', 0, 0, tiled=False)  15.1 us
    ppermute x4, waiting for transfers between devices, swap_zh(): return lax.ppermute(value, 'zh', [(0, 1), (1, 0)])  14.7 us
  transfers between devices with their start and end apart: 18, of which 11 were waited for; matrix products, arithmetic and copies ran while one was open for 8% of the time, Pallas kernels for 0%

profile of v11, /device:TPU:1, one launch (start us, length us, event | category | flops | bytes accessed | tf_op | source)
XLA Modules:
  0.0 250.0 jit_solution(6972919854402417178)
XLA Ops:
  0.7 2.3 broadcast_in_dim.60
  2.9 10.3 %all-to-all-start = ((bf16[8,384,256]{2,1,0:T(8,128)(2,1)}), bf16[8,384,256]{2,1,0:T(8,128)(2,1)S(1)}, u32[]{:S(2)}, u32[]{:S(2)}) async-start(bf16[8,384,256]{2,1,0:T(8,128)(2,1)} %broadcast_in_dim.60), calls=%async_computation | async-start | bytes 3145728 | tf_op jit(solution)/shard_map/all_to_all | solution.py:41
  13.2 11.1 %collective-permute-start.8 = (bf16[384,256]{1,0:T(8,128)(2,1)S(1)}, bf16[384,256]{1,0:T(8,128)(2,1)S(1)}, u32[]{:S(2)}, u32[]{:S(2)}) collective-permute-start(bf16[384,256]{1,0:T(8,128)(2,1)S(1)} %bitcast.175), channel_id=1, source_target_pairs={{0,8},{8,0},{1,9},{9,1},{2,10},{10,2},{3,11},{11,3},{4,12},{12,4},... | collective-permute-start | bytes 589832 | tf_op jit(solution)/shard_map/ppermute | solution.py:35
  24.3 5.9 %collective-permute-done.8 = bf16[384,256]{1,0:T(8,128)(2,1)S(1)} collective-permute-done((bf16[384,256]{1,0:T(8,128)(2,1)S(1)}, bf16[384,256]{1,0:T(8,128)(2,1)S(1)}, u32[]{:S(2)}, u32[]{:S(2)}) %collective-permute-start.8) | collective-permute-done | bytes 196640 | tf_op jit(solution)/shard_map/ppermute | solution.py:35
  30.2 3.7 %all-to-all-done = bf16[8,384,256]{2,1,0:T(8,128)(2,1)S(1)} async-done(((bf16[8,384,256]{2,1,0:T(8,128)(2,1)}), bf16[8,384,256]{2,1,0:T(8,128)(2,1)S(1)}, u32[]{:S(2)}, u32[]{:S(2)}) %all-to-all-start) | async-done | bytes 1572896 | tf_op jit(solution)/shard_map/all_to_all | solution.py:41
  33.8 1.3 broadcast_in_dim.61
  35.1 4.4 %all-to-all-start.1 = ((bf16[8,384,256]{2,1,0:T(8,128)(2,1)}), bf16[8,384,256]{2,1,0:T(8,128)(2,1)S(1)}, u32[]{:S(2)}, u32[]{:S(2)}) async-start(bf16[8,384,256]{2,1,0:T(8,128)(2,1)} %broadcast_in_dim.61), calls=%async_computation.1 | async-start | bytes 3145728 | tf_op jit(solution)/shard_map/all_to_all | solution.py:41
  39.6 20.6 %all-to-all-done.1 = bf16[8,384,256]{2,1,0:T(8,128)(2,1)S(1)} async-done(((bf16[8,384,256]{2,1,0:T(8,128)(2,1)}), bf16[8,384,256]{2,1,0:T(8,128)(2,1)S(1)}, u32[]{:S(2)}, u32[]{:S(2)}) %all-to-all-start.1) | async-done | bytes 1572896 | tf_op jit(solution)/shard_map/all_to_all | solution.py:41
  60.2 0.2 broadcast_select_fusion.1
  60.4 0.3 pad_maximum_fusion
  60.7 1.6 copy-done.3
  62.3 1.0 fusion.19
  63.4 1.1 broadcast_in_dim.63
  64.5 4.4 %all-to-all-start.3 = ((bf16[8,256,256]{2,1,0:T(8,128)(2,1)}), bf16[8,256,256]{2,1,0:T(8,128)(2,1)S(1)}, u32[]{:S(2)}, u32[]{:S(2)}) async-start(bf16[8,256,256]{2,1,0:T(8,128)(2,1)} %broadcast_in_dim.63), calls=%async_computation.3 | async-start | bytes 2097152 | tf_op jit(solution)/shard_map/all_to_all | solution.py:41
  68.9 11.2 %collective-permute-start.9 = (bf16[256,256]{0,1:T(8,128)(2,1)S(1)}, bf16[256,256]{0,1:T(8,128)(2,1)S(1)}, u32[]{:S(2)}, u32[]{:S(2)}) collective-permute-start(bf16[256,256]{0,1:T(8,128)(2,1)S(1)} %fusion.19), channel_id=1, source_target_pairs={{0,8},{8,0},{1,9},{9,1},{2,10},{10,2},{3,11},{11,3},{4,12},{12,4},... | collective-permute-start | bytes 393224 | tf_op jit(solution)/shard_map/ppermute | solution.py:35
  80.2 4.4 %collective-permute-done.9 = bf16[256,256]{0,1:T(8,128)(2,1)S(1)} collective-permute-done((bf16[256,256]{0,1:T(8,128)(2,1)S(1)}, bf16[256,256]{0,1:T(8,128)(2,1)S(1)}, u32[]{:S(2)}, u32[]{:S(2)}) %collective-permute-start.9) | collective-permute-done | bytes 131104 | tf_op jit(solution)/shard_map/ppermute | solution.py:35
  84.7 1.1 broadcast_in_dim.62
  85.7 5.4 %all-to-all-start.2 = ((bf16[8,256,256]{2,1,0:T(8,128)(2,1)}), bf16[8,256,256]{2,1,0:T(8,128)(2,1)S(1)}, u32[]{:S(2)}, u32[]{:S(2)}) async-start(bf16[8,256,256]{2,1,0:T(8,128)(2,1)} %broadcast_in_dim.62), calls=%async_computation.2 | async-start | bytes 2097152 | tf_op jit(solution)/shard_map/all_to_all | solution.py:41
  91.7 0.1 broadcast_in_dim.57
  92.1 14.0 %all-to-all-done.2 = bf16[8,256,256]{2,1,0:T(8,128)(2,1)S(1)} async-done(((bf16[8,256,256]{2,1,0:T(8,128)(2,1)}), bf16[8,256,256]{2,1,0:T(8,128)(2,1)S(1)}, u32[]{:S(2)}, u32[]{:S(2)}) %all-to-all-start.2) | async-done | bytes 1048608 | tf_op jit(solution)/shard_map/all_to_all | solution.py:41
  106.1 0.2 pad_maximum_fusion.1
  106.3 0.3 broadcast_in_dim.58
  106.6 1.2 fusion.52
  107.8 0.3 fusion.9
  108.1 0.1 fusion.51
  108.3 0.6 fusion.22
  108.9 0.8 fusion.6
  109.6 0.1 fusion.50
  109.8 1.2 copy-done.4
  111.0 0.5 convolution_convert_fusion.3
  111.5 0.5 convolution_convert_fusion.2
  112.1 2.9 %collective-permute-start.11 = (bf16[4,256,256]{1,2,0:T(8,128)(2,1)S(1)}, bf16[4,256,256]{1,2,0:T(8,128)(2,1)S(1)}, u32[]{:S(2)}, u32[]{:S(2)}) collective-permute-start(bf16[4,256,256]{1,2,0:T(8,128)(2,1)S(1)} %select_bitcast_fusion.2), channel_id=1, source_target_pairs={{0,1},{1,0},{2,3},{3,2},{4,5},{5,4},{6,7},{7,6},{8,9},{9,8},{10,11... | collective-permute-start | bytes 1572872 | tf_op jit(solution)/shard_map/ppermute | solution.py:65
  115.0 0.5 convolution_convert_fusion.5
  115.5 0.5 convolution_convert_fusion.4
  116.1 1.9 collective-permute-start.10
  118.0 1.0 fusion.24
  119.0 3.5 %all-to-all-start.5 = ((bf16[4,256,256]{1,2,0:T(8,128)(2,1)}), bf16[4,256,256]{1,2,0:T(8,128)(2,1)S(1)}, u32[]{:S(2)}, u32[]{:S(2)}) async-start(bf16[4,256,256]{1,2,0:T(8,128)(2,1)} %fusion.24), calls=%async_computation.5 | async-start | bytes 1048576 | tf_op jit(solution)/shard_map/all_to_all | solution.py:67
  122.5 1.0 fusion.25
  123.5 8.1 %all-to-all-done.5 = bf16[4,256,256]{1,2,0:T(8,128)(2,1)S(1)} async-done(((bf16[4,256,256]{1,2,0:T(8,128)(2,1)}), bf16[4,256,256]{1,2,0:T(8,128)(2,1)S(1)}, u32[]{:S(2)}, u32[]{:S(2)}) %all-to-all-start.5) | async-done | bytes 524320 | tf_op jit(solution)/shard_map/all_to_all | solution.py:67
  131.6 3.5 %all-to-all-start.4 = ((bf16[4,256,256]{1,2,0:T(8,128)(2,1)}), bf16[4,256,256]{1,2,0:T(8,128)(2,1)S(1)}, u32[]{:S(2)}, u32[]{:S(2)}) async-start(bf16[4,256,256]{1,2,0:T(8,128)(2,1)} %fusion.25), calls=%async_computation.4 | async-start | bytes 1048576 | tf_op jit(solution)/shard_map/all_to_all | solution.py:67
  135.0 4.7 %copy.78 = bf16[1,256,6144]{1,2,0:T(8,128)(2,1)} copy(bf16[1,256,6144]{2,1,0:T(8,128)(2,1)} %param.10) | data formatting | bytes 6291456 | tf_op args[0]
  139.8 11.1 %collective-permute-start.12 = (bf16[256,256]{0,1:T(8,128)(2,1)S(1)}, bf16[256,256]{0,1:T(8,128)(2,1)S(1)}, u32[]{:S(2)}, u32[]{:S(2)}) collective-permute-start(bf16[256,256]{0,1:T(8,128)(2,1)S(1)} %reduce_sum.82), channel_id=1, source_target_pairs={{0,8},{8,0},{1,9},{9,1},{2,10},{10,2},{3,11},{11,3},{4,12},{12,4},... | collective-permute-start | bytes 393224 | tf_op jit(solution)/shard_map/ppermute | solution.py:35
  150.9 3.3 %collective-permute-done.12 = bf16[256,256]{0,1:T(8,128)(2,1)S(1)} collective-permute-done((bf16[256,256]{0,1:T(8,128)(2,1)S(1)}, bf16[256,256]{0,1:T(8,128)(2,1)S(1)}, u32[]{:S(2)}, u32[]{:S(2)}) %collective-permute-start.12) | collective-permute-done | bytes 131104 | tf_op jit(solution)/shard_map/ppermute | solution.py:35
  154.2 2.1 convolution_convert_fusion
  156.2 1.0 select_bitcast_fusion
  157.3 4.4 %collective-permute-start.14 = (bf16[4,384,256]{2,1,0:T(8,128)(2,1)}, bf16[4,384,256]{2,1,0:T(8,128)(2,1)}, u32[]{:S(2)}, u32[]{:S(2)}) collective-permute-start(bf16[4,384,256]{2,1,0:T(8,128)(2,1)} %select_bitcast_fusion), channel_id=1, source_target_pairs={{0,1},{1,0},{2,3},{3,2},{4,5},{5,4},{6,7},{7,6},{8,9},{9,8},{10,11... | collective-permute-start | bytes 2359304 | tf_op jit(solution)/shard_map/ppermute | solution.py:65
  161.7 2.0 convolution_convert_fusion.1
  163.7 1.0 select_bitcast_fusion.1
  164.7 1.9 collective-permute-start.13
  166.7 2.3 fusion.12
  169.0 4.5 %all-to-all-start.7 = ((bf16[4,384,256]{2,1,0:T(8,128)(2,1)}), bf16[4,384,256]{2,1,0:T(8,128)(2,1)}, u32[]{:S(2)}, u32[]{:S(2)}) async-start(bf16[4,384,256]{2,1,0:T(8,128)(2,1)} %fusion.12), calls=%async_computation.7 | async-start | bytes 1572864 | tf_op jit(solution)/shard_map/all_to_all | solution.py:67
  173.4 2.3 fusion.13
  175.8 9.4 %all-to-all-done.7 = bf16[4,384,256]{2,1,0:T(8,128)(2,1)} async-done(((bf16[4,384,256]{2,1,0:T(8,128)(2,1)}), bf16[4,384,256]{2,1,0:T(8,128)(2,1)}, u32[]{:S(2)}, u32[]{:S(2)}) %all-to-all-start.7) | async-done | bytes 786464 | tf_op jit(solution)/shard_map/all_to_all | solution.py:67
  185.1 3.7 %all-to-all-start.6 = ((bf16[4,384,256]{2,1,0:T(8,128)(2,1)}), bf16[4,384,256]{2,1,0:T(8,128)(2,1)S(1)}, u32[]{:S(2)}, u32[]{:S(2)}) async-start(bf16[4,384,256]{2,1,0:T(8,128)(2,1)} %fusion.13), calls=%async_computation.6 | async-start | bytes 1572864 | tf_op jit(solution)/shard_map/all_to_all | solution.py:67
  189.5 1.3 reduce_sum.83
  190.8 11.1 %collective-permute-start.15 = (bf16[384,256]{1,0:T(8,128)(2,1)S(1)}, bf16[384,256]{1,0:T(8,128)(2,1)S(1)}, u32[]{:S(2)}, u32[]{:S(2)}) collective-permute-start(bf16[384,256]{1,0:T(8,128)(2,1)S(1)} %reduce_sum.83), channel_id=1, source_target_pairs={{0,8},{8,0},{1,9},{9,1},{2,10},{10,2},{3,11},{11,3},{4,12},{12,4},... | collective-permute-start | bytes 589832 | tf_op jit(solution)/shard_map/ppermute | solution.py:35
  201.9 3.0 %fusion.23 = bf16[1,256,128]{2,1,0:T(8,128)(2,1)} fusion(bf16[256,4096]{0,1:T(8,128)(2,1)} %copy-done.4, bf16[4096,256]{1,0:T(8,128)(2,1)S(1)} %bitcast.167), kind=kOutput, calls=%fused_computation.40 | convolution fusion | flops 268468224 | bytes 3211264 | tf_op jit(solution)/shard_map/dot_general | solution.py:154
  205.0 1.2 collective-permute-done.15
  206.3 42.9 %conditional.1 = (f32[1,384,256]{2,1,0:T(8,128)S(1)}) conditional(s32[]{:T(128)} %clamp.3, (f32[4,384,256]{2,1,0:T(8,128)S(1)}, f32[384,256]{1,0:T(8,128)S(1)}) %tuple.28, (f32[4,384,256]{2,1,0:T(8,128)S(1)}, f32[384,256]{1,0:T(8,128)S(1)}) %tuple.28, (f32[4,384,256]{2,1,0:T(8,128)S(1)}, ...), branch_computations={%region_6.8_spmd, %region_8.10_spmd, %region_10.12_spmd, %region_1... | conditional | flops 983040 | bytes 6094940 | solution.py:178
  206.5 3.7 %collective-permute-start.2 = (bf16[384,256]{1,0:T(8,128)(2,1)S(1)}, bf16[384,256]{1,0:T(8,128)(2,1)S(1)}, u32[]{:S(2)}, u32[]{:S(2)}) collective-permute-start(bf16[384,256]{1,0:T(8,128)(2,1)S(1)} %get-tuple-element.46), channel_id=1, source_target_pairs={{0,32},{16,48},{32,64},{48,80},{64,96},{80,112},{96,128},{112,144}... | collective-permute-start | bytes 589832 | tf_op jit(solution)/shard_map/cond/branch_1_fun/ppermute | solution.py:25
  210.2 22.8 %collective-permute-start.3 = (bf16[384,256]{1,0:T(8,128)(2,1)S(1)}, bf16[384,256]{1,0:T(8,128)(2,1)S(1)}, u32[]{:S(2)}, u32[]{:S(2)}) collective-permute-start(bf16[384,256]{1,0:T(8,128)(2,1)S(1)} %get-tuple-element.46), channel_id=1, source_target_pairs={{0,480},{16,496},{32,0},{48,16},{64,32},{80,48},{96,64},{112,80},{... | collective-permute-start | bytes 589832 | tf_op jit(solution)/shard_map/cond/branch_1_fun/ppermute | solution.py:25
  233.0 11.8 %collective-permute-done.2 = bf16[384,256]{1,0:T(8,128)(2,1)S(1)} collective-permute-done((bf16[384,256]{1,0:T(8,128)(2,1)S(1)}, bf16[384,256]{1,0:T(8,128)(2,1)S(1)}, u32[]{:S(2)}, u32[]{:S(2)}) %collective-permute-start.2) | collective-permute-done | bytes 196640 | tf_op jit(solution)/shard_map/cond/branch_1_fun/ppermute | solution.py:25
  244.8 4.4 %collective-permute-done.3 = bf16[384,256]{1,0:T(8,128)(2,1)S(1)} collective-permute-done((bf16[384,256]{1,0:T(8,128)(2,1)S(1)}, bf16[384,256]{1,0:T(8,128)(2,1)S(1)}, u32[]{:S(2)}, u32[]{:S(2)}) %collective-permute-start.3) | collective-permute-done | bytes 196640 | tf_op jit(solution)/shard_map/cond/branch_1_fun/ppermute | solution.py:25
  249.2 0.7 copy-done.7
  (47 shorter events, 1.9 us)
Async XLA Ops:
  0.6 106.0 %copy-start = (bf16[1,256,128]{2,1,0:T(8,128)(2,1)S(1)}, bf16[1,256,128]{2,1,0:T(8,128)(2,1)}, u32[]{:S(2)}) copy-start(bf16[1,256,128]{2,1,0:T(8,128)(2,1)} %param.11) | copy-start | bytes 196612
  0.6 12.6 %copy-start.8 = (bf16[1,384,256]{2,1,0:T(8,128)(2,1)S(1)}, bf16[1,384,256]{2,1,0:T(8,128)(2,1)}, u32[]{:S(2)}) copy-start(bf16[1,384,256]{2,1,0:T(8,128)(2,1)} %param.13) | copy-start | bytes 589828
  2.9 30.9 %all-to-all-start = ((bf16[8,384,256]{2,1,0:T(8,128)(2,1)}), bf16[8,384,256]{2,1,0:T(8,128)(2,1)S(1)}, u32[]{:S(2)}, u32[]{:S(2)}) async-start(bf16[8,384,256]{2,1,0:T(8,128)(2,1)} %broadcast_in_dim.60), calls=%async_computation | async-start | bytes 3145728 | tf_op jit(solution)/shard_map/all_to_all | solution.py:41
  13.2 16.9 %collective-permute-start.8 = (bf16[384,256]{1,0:T(8,128)(2,1)S(1)}, bf16[384,256]{1,0:T(8,128)(2,1)S(1)}, u32[]{:S(2)}, u32[]{:S(2)}) collective-permute-start(bf16[384,256]{1,0:T(8,128)(2,1)S(1)} %bitcast.175), channel_id=1, source_target_pairs={{0,8},{8,0},{1,9},{9,1},{2,10},{10,2},{3,11},{11,3},{4,12},{12,4},... | collective-permute-start | bytes 589832 | tf_op jit(solution)/shard_map/ppermute | solution.py:35
  35.1 25.1 %all-to-all-start.1 = ((bf16[8,384,256]{2,1,0:T(8,128)(2,1)}), bf16[8,384,256]{2,1,0:T(8,128)(2,1)S(1)}, u32[]{:S(2)}, u32[]{:S(2)}) async-start(bf16[8,384,256]{2,1,0:T(8,128)(2,1)} %broadcast_in_dim.61), calls=%async_computation.1 | async-start | bytes 3145728 | tf_op jit(solution)/shard_map/all_to_all | solution.py:41
  60.4 1.9 copy-start.3
  64.5 20.2 %all-to-all-start.3 = ((bf16[8,256,256]{2,1,0:T(8,128)(2,1)}), bf16[8,256,256]{2,1,0:T(8,128)(2,1)S(1)}, u32[]{:S(2)}, u32[]{:S(2)}) async-start(bf16[8,256,256]{2,1,0:T(8,128)(2,1)} %broadcast_in_dim.63), calls=%async_computation.3 | async-start | bytes 2097152 | tf_op jit(solution)/shard_map/all_to_all | solution.py:41
  68.9 22.4 %copy-start.9 = (s32[64,3]{0,1:T(4,128)S(1)}, s32[64,3]{0,1:T(4,128)}, u32[]{:S(2)}) copy-start(s32[64,3]{0,1:T(4,128)} %param.14) | copy-start | bytes 2308
  68.9 23.1 %copy-start.5 = (bf16[1,256,128]{2,1,0:T(8,128)(2,1)S(1)}, bf16[1,256,128]{2,1,0:T(8,128)(2,1)}, u32[]{:S(2)}) copy-start(bf16[1,256,128]{2,1,0:T(8,128)(2,1)} %param.12) | copy-start | bytes 196612
  68.9 15.6 %collective-permute-start.9 = (bf16[256,256]{0,1:T(8,128)(2,1)S(1)}, bf16[256,256]{0,1:T(8,128)(2,1)S(1)}, u32[]{:S(2)}, u32[]{:S(2)}) collective-permute-start(bf16[256,256]{0,1:T(8,128)(2,1)S(1)} %fusion.19), channel_id=1, source_target_pairs={{0,8},{8,0},{1,9},{9,1},{2,10},{10,2},{3,11},{11,3},{4,12},{12,4},... | collective-permute-start | bytes 393224 | tf_op jit(solution)/shard_map/ppermute | solution.py:35
  85.7 20.4 %all-to-all-start.2 = ((bf16[8,256,256]{2,1,0:T(8,128)(2,1)}), bf16[8,256,256]{2,1,0:T(8,128)(2,1)S(1)}, u32[]{:S(2)}, u32[]{:S(2)}) async-start(bf16[8,256,256]{2,1,0:T(8,128)(2,1)} %broadcast_in_dim.62), calls=%async_computation.2 | async-start | bytes 2097152 | tf_op jit(solution)/shard_map/all_to_all | solution.py:41
  106.3 2.5 %copy-start.1 = (bf16[16,256,256]{2,1,0:T(8,128)(2,1)}, bf16[16,256,256]{2,1,0:T(8,128)(2,1)S(1)}, u32[]{:S(2)}) copy-start(bf16[16,256,256]{2,1,0:T(8,128)(2,1)S(1)} %pad_maximum_fusion.1) | copy-start | bytes 6291460
  109.6 1.4 copy-start.4
  112.1 5.9 %collective-permute-start.11 = (bf16[4,256,256]{1,2,0:T(8,128)(2,1)S(1)}, bf16[4,256,256]{1,2,0:T(8,128)(2,1)S(1)}, u32[]{:S(2)}, u32[]{:S(2)}) collective-permute-start(bf16[4,256,256]{1,2,0:T(8,128)(2,1)S(1)} %select_bitcast_fusion.2), channel_id=1, source_target_pairs={{0,1},{1,0},{2,3},{3,2},{4,5},{5,4},{6,7},{7,6},{8,9},{9,8},{10,11... | collective-permute-start | bytes 1572872 | tf_op jit(solution)/shard_map/ppermute | solution.py:65
  116.1 6.4 %collective-permute-start.10 = (bf16[4,256,256]{1,2,0:T(8,128)(2,1)S(1)}, bf16[4,256,256]{1,2,0:T(8,128)(2,1)S(1)}, u32[]{:S(2)}, u32[]{:S(2)}) collective-permute-start(bf16[4,256,256]{1,2,0:T(8,128)(2,1)S(1)} %fusion.32), channel_id=1, source_target_pairs={{0,1},{1,0},{2,3},{3,2},{4,5},{5,4},{6,7},{7,6},{8,9},{9,8},{10,11... | collective-permute-start | bytes 1572872 | tf_op jit(solution)/shard_map/ppermute | solution.py:65
  119.0 12.5 %all-to-all-start.5 = ((bf16[4,256,256]{1,2,0:T(8,128)(2,1)}), bf16[4,256,256]{1,2,0:T(8,128)(2,1)S(1)}, u32[]{:S(2)}, u32[]{:S(2)}) async-start(bf16[4,256,256]{1,2,0:T(8,128)(2,1)} %fusion.24), calls=%async_computation.5 | async-start | bytes 1048576 | tf_op jit(solution)/shard_map/all_to_all | solution.py:67
  131.6 19.3 %all-to-all-start.4 = ((bf16[4,256,256]{1,2,0:T(8,128)(2,1)}), bf16[4,256,256]{1,2,0:T(8,128)(2,1)S(1)}, u32[]{:S(2)}, u32[]{:S(2)}) async-start(bf16[4,256,256]{1,2,0:T(8,128)(2,1)} %fusion.25), calls=%async_computation.4 | async-start | bytes 1048576 | tf_op jit(solution)/shard_map/all_to_all | solution.py:67
  139.8 14.4 %collective-permute-start.12 = (bf16[256,256]{0,1:T(8,128)(2,1)S(1)}, bf16[256,256]{0,1:T(8,128)(2,1)S(1)}, u32[]{:S(2)}, u32[]{:S(2)}) collective-permute-start(bf16[256,256]{0,1:T(8,128)(2,1)S(1)} %reduce_sum.82), channel_id=1, source_target_pairs={{0,8},{8,0},{1,9},{9,1},{2,10},{10,2},{3,11},{11,3},{4,12},{12,4},... | collective-permute-start | bytes 393224 | tf_op jit(solution)/shard_map/ppermute | solution.py:35
  154.2 3.1 %copy-start.6 = (bf16[256,256]{0,1:T(8,128)(2,1)}, bf16[256,256]{0,1:T(8,128)(2,1)S(1)}, u32[]{:S(2)}) copy-start(bf16[256,256]{0,1:T(8,128)(2,1)S(1)} %collective-permute-done.12) | copy-start | bytes 393220
  157.3 9.4 %collective-permute-start.14 = (bf16[4,384,256]{2,1,0:T(8,128)(2,1)}, bf16[4,384,256]{2,1,0:T(8,128)(2,1)}, u32[]{:S(2)}, u32[]{:S(2)}) collective-permute-start(bf16[4,384,256]{2,1,0:T(8,128)(2,1)} %select_bitcast_fusion), channel_id=1, source_target_pairs={{0,1},{1,0},{2,3},{3,2},{4,5},{5,4},{6,7},{7,6},{8,9},{9,8},{10,11... | collective-permute-start | bytes 2359304 | tf_op jit(solution)/shard_map/ppermute | solution.py:65
  164.7 8.7 %collective-permute-start.13 = (bf16[4,384,256]{2,1,0:T(8,128)(2,1)}, bf16[4,384,256]{2,1,0:T(8,128)(2,1)}, u32[]{:S(2)}, u32[]{:S(2)}) collective-permute-start(bf16[4,384,256]{2,1,0:T(8,128)(2,1)} %select_bitcast_fusion.1), channel_id=1, source_target_pairs={{0,1},{1,0},{2,3},{3,2},{4,5},{5,4},{6,7},{7,6},{8,9},{9,8},{10,11... | collective-permute-start | bytes 2359304 | tf_op jit(solution)/shard_map/ppermute | solution.py:65
  169.0 16.2 %all-to-all-start.7 = ((bf16[4,384,256]{2,1,0:T(8,128)(2,1)}), bf16[4,384,256]{2,1,0:T(8,128)(2,1)}, u32[]{:S(2)}, u32[]{:S(2)}) async-start(bf16[4,384,256]{2,1,0:T(8,128)(2,1)} %fusion.12), calls=%async_computation.7 | async-start | bytes 1572864 | tf_op jit(solution)/shard_map/all_to_all | solution.py:67
  175.8 26.1 %copy-start.2 = (bf16[16,256,256]{2,1,0:T(8,128)(2,1)S(1)}, bf16[16,256,256]{2,1,0:T(8,128)(2,1)}, u32[]{:S(2)}) copy-start(bf16[16,256,256]{2,1,0:T(8,128)(2,1)} %copy-done.1) | copy-start | bytes 6291460
  185.1 19.7 %all-to-all-start.6 = ((bf16[4,384,256]{2,1,0:T(8,128)(2,1)}), bf16[4,384,256]{2,1,0:T(8,128)(2,1)S(1)}, u32[]{:S(2)}, u32[]{:S(2)}) async-start(bf16[4,384,256]{2,1,0:T(8,128)(2,1)} %fusion.13), calls=%async_computation.6 | async-start | bytes 1572864 | tf_op jit(solution)/shard_map/all_to_all | solution.py:67
  190.8 15.4 %collective-permute-start.15 = (bf16[384,256]{1,0:T(8,128)(2,1)S(1)}, bf16[384,256]{1,0:T(8,128)(2,1)S(1)}, u32[]{:S(2)}, u32[]{:S(2)}) collective-permute-start(bf16[384,256]{1,0:T(8,128)(2,1)S(1)} %reduce_sum.83), channel_id=1, source_target_pairs={{0,8},{8,0},{1,9},{9,1},{2,10},{10,2},{3,11},{11,3},{4,12},{12,4},... | collective-permute-start | bytes 589832 | tf_op jit(solution)/shard_map/ppermute | solution.py:35
  206.5 38.3 %collective-permute-start.2 = (bf16[384,256]{1,0:T(8,128)(2,1)S(1)}, bf16[384,256]{1,0:T(8,128)(2,1)S(1)}, u32[]{:S(2)}, u32[]{:S(2)}) collective-permute-start(bf16[384,256]{1,0:T(8,128)(2,1)S(1)} %get-tuple-element.46), channel_id=1, source_target_pairs={{0,32},{16,48},{32,64},{48,80},{64,96},{80,112},{96,128},{112,144}... | collective-permute-start | bytes 589832 | tf_op jit(solution)/shard_map/cond/branch_1_fun/ppermute | solution.py:25
  210.2 39.0 %collective-permute-start.3 = (bf16[384,256]{1,0:T(8,128)(2,1)S(1)}, bf16[384,256]{1,0:T(8,128)(2,1)S(1)}, u32[]{:S(2)}, u32[]{:S(2)}) collective-permute-start(bf16[384,256]{1,0:T(8,128)(2,1)S(1)} %get-tuple-element.46), channel_id=1, source_target_pairs={{0,480},{16,496},{32,0},{48,16},{64,32},{80,48},{96,64},{112,80},{... | collective-permute-start | bytes 589832 | tf_op jit(solution)/shard_map/cond/branch_1_fun/ppermute | solution.py:25
  249.2 0.7 copy-start.7
